TPU v7x, 32 devices: a whole 2x2x4 slice. The times are simulated.
32 devices in a mesh: replica: 8 (over z, x), tensor: 4 (over y, core).
Axes of the slice: x: 2, y: 2, z: 4, core: 2. Of those that a mesh axis runs over, the one named last changes fastest.
Arguments:
- hidden: bfloat16 [256, 8192], P('replica', 'tensor'), may hold values from -600 to 600
- input_norm_gain: float32 [8192], replicated, may hold values from 0.1 to 1.9
- key_value_weight: bfloat16 [8192, 2, 1024], P(None, None, 'tensor'), may hold values from -0.0625 to 0.0625
- adapter_down: bfloat16 [128, 8192, 128], P('replica', 'tensor'), may hold values from -0.0625 to 0.0625
- adapter_up: bfloat16 [128, 2, 64, 1024], P('replica', None, None, 'tensor'), may hold values from -0.75 to 0.75
- query: bfloat16 [256, 8192], P('replica', 'tensor'), may hold values from -6 to 6
- key_value_cache: bfloat16 [256, 512, 2, 1024], P('replica', None, None, 'tensor'), may hold values from -6 to 6
- segment_adapter: int32 [8, 16], P('replica'), may hold values from 0 to 127, as said below
- segment_sizes: int32 [8, 16], P('replica'), may hold values from 1 to 4, 32 in all within a row
- cached_length: int32 [256], P('replica'), may hold values from 2 to 512, as said below
Outputs:
- new_kv: bfloat16 [256, 2, 1024], P('replica', None, 'tensor')
- attended: bfloat16 [256, 8192], P('replica', 'tensor')
Inputs may be any that keep to these rules, and one draw needn't show every extreme that they name: `segment_adapter`: the segments of one replica name distinct adapters; adapter a is stored at index a // 16 of replica. At most 2 of one replica's segments name adapters stored at one index of replica, and in every replica's list some index of replica is named exactly 2 times. `segment_sizes`: the sizes of one replica's segments sum to 32. The new token takes position cached_length.
All inputs are finite; a program needn't handle non-finite values.
Results may differ from a plain program's by a relative error of at most 0.0058.
Values may be sent and summed in bfloat16 or wider, within the bound.
No kernel may reach another device: no remote copies, remote signals or barrier semaphores. Data moves between devices by JAX's collectives and lax.ppermute only.
A program may use at most 192 MiB of HBM per device.

v0:
```python
import jax
import jax.numpy as jnp
from jax import lax
from jax.sharding import PartitionSpec as P

HEAD = 128
ADP_DEV = 16
SLOT = 4
CAP = 2


ADAPTER_SCALE = 0.5
ROPE_BASE = 500000.0
EPSILON = 1e-05


def rotate(key_heads, token_position):
    half_size = key_heads.shape[-1] // 2
    inv_freq = ROPE_BASE ** (
        -(jnp.arange(half_size, dtype=jnp.float32) * 2.0) / key_heads.shape[-1]
    )
    angles = token_position.astype(jnp.float32)[:, None] * inv_freq[None, :]
    cosine_term = jnp.cos(angles)[:, None, :]
    sine_term = jnp.sin(angles)[:, None, :]
    first_half = key_heads[..., :half_size]
    second_half = key_heads[..., half_size:]
    return jnp.concatenate(
        [
            first_half * cosine_term - second_half * sine_term,
            second_half * cosine_term + first_half * sine_term,
        ],
        axis=-1,
    )


def body(
    hidden,
    input_norm_gain,
    key_value_weight,
    adapter_down,
    adapter_up,
    query,
    key_value_cache,
    segment_adapter,
    segment_sizes,
    cached_length,
):
    row_count = hidden.shape[0]
    part_width = hidden.shape[1]
    kv_width = key_value_weight.shape[2]
    kv_local = kv_width // HEAD
    cache_len = key_value_cache.shape[1]
    adapter_rank_size = adapter_up.shape[2]
    replicas = lax.axis_size("replica")
    segments = segment_sizes.shape[1]
    gathered = lax.all_gather(hidden, "tensor", axis=1, tiled=True)
    widened = gathered.astype(jnp.float32)
    normed = (
        widened
        * lax.rsqrt(jnp.mean(widened * widened, axis=1, keepdims=True) + EPSILON)
        * input_norm_gain
    ).astype(jnp.bfloat16)
    own_cols = lax.dynamic_slice_in_dim(
        normed, lax.axis_index("tensor") * part_width, part_width, 1
    )
    seg_counts = segment_sizes[0]
    adapters = segment_adapter[0]
    seg_ends = jnp.cumsum(seg_counts, dtype=jnp.int32)
    starts = seg_ends - seg_counts
    offsets = jnp.arange(SLOT, dtype=jnp.int32)
    row_ids = jnp.arange(row_count, dtype=jnp.int32)
    segment_index = jnp.sum((seg_ends[None, :] <= row_ids[:, None]).astype(jnp.int32), axis=1)
    token_position = row_ids - starts[segment_index]
    owners = adapters // ADP_DEV
    local_ids = adapters % ADP_DEV
    seg_ids = jnp.arange(segments, dtype=jnp.int32)
    slot_rank = jnp.sum(
        ((owners[None, :] == owners[:, None]) & (seg_ids[None, :] < seg_ids[:, None])).astype(
            jnp.int32
        ),
        axis=1,
    )
    owner_hit = (owners[None, None, :] == jnp.arange(replicas, dtype=jnp.int32)[:, None, None]) & (
        slot_rank[None, None, :] == jnp.arange(CAP, dtype=jnp.int32)[None, :, None]
    )
    wanted = jnp.sum(jnp.where(owner_hit, local_ids[None, None, :], 0), axis=2)
    fetch_slot = owners * CAP + slot_rank
    seg_at = jnp.sum(jnp.where(owner_hit, seg_ids[None, None, :], 0), axis=2)
    filled = jnp.any(owner_hit, axis=2)
    slot_counts = jnp.where(filled, seg_counts[seg_at], 0)
    slot_live = offsets[None, None, :] < slot_counts[:, :, None]
    source_row = jnp.where(slot_live, starts[seg_at][:, :, None] + offsets[None, None, :], 0)
    slot_rows = jnp.where(
        slot_live[:, :, :, None], own_cols[source_row], jnp.zeros((), jnp.bfloat16)
    )
    segment_member_mask = lax.all_to_all(wanted, "replica", split_axis=0, concat_axis=0, tiled=True)
    selected_down = adapter_down[segment_member_mask]
    selected_up = adapter_up[segment_member_mask]
    down_got = lax.all_to_all(selected_down, "replica", split_axis=0, concat_axis=0, tiled=True)
    up_got = lax.all_to_all(selected_up, "replica", split_axis=0, concat_axis=0, tiled=True)
    partial_value = jnp.einsum(
        "oksd,okdr->oksr", slot_rows, down_got, preferred_element_type=jnp.float32
    )
    summed = lax.psum(partial_value, "tensor").astype(jnp.bfloat16)
    summed = summed.reshape(summed.shape[:3] + (2, adapter_rank_size))
    slot_delta = (
        jnp.einsum("okscr,okcrw->okscw", summed, up_got, preferred_element_type=jnp.float32)
        * ADAPTER_SCALE
    )
    flat_delta = slot_delta.reshape((replicas * CAP * SLOT,) + slot_delta.shape[3:])
    adapter_delta = flat_delta[fetch_slot[segment_index] * SLOT + token_position]
    base_projection = jnp.dot(
        normed,
        key_value_weight.reshape(key_value_weight.shape[0], 2 * kv_width),
        preferred_element_type=jnp.float32,
    ).reshape(row_count, 2, kv_width)
    current_key_value = base_projection + adapter_delta
    rotated = rotate(
        current_key_value[:, 0].reshape(row_count, kv_local, HEAD), cached_length
    ).reshape(row_count, kv_width)
    new_kv = jnp.stack([rotated, current_key_value[:, 1]], axis=1).astype(jnp.bfloat16)
    group_size = query.shape[1] // HEAD // kv_local
    scale = float(HEAD) ** (-0.5)
    query_heads = query.reshape(row_count, kv_local, group_size, HEAD)
    cached_keys = key_value_cache[:, :, 0].reshape(row_count, cache_len, kv_local, HEAD)
    cached_values = key_value_cache[:, :, 1].reshape(row_count, cache_len, kv_local, HEAD)
    scores = (
        jnp.einsum("bhgd,bthd->bhgt", query_heads, cached_keys, preferred_element_type=jnp.float32)
        * scale
    )
    is_live = jnp.arange(cache_len, dtype=jnp.int32)[None, :] < cached_length[:, None]
    scores = jnp.where(is_live[:, None, None, :], scores, -jnp.inf)
    new_key = new_kv[:, 0].reshape(row_count, kv_local, HEAD)
    new_value = new_kv[:, 1].astype(jnp.float32).reshape(row_count, kv_local, HEAD)
    own_score = (
        jnp.einsum("bhgd,bhd->bhg", query_heads, new_key, preferred_element_type=jnp.float32)
        * scale
    )
    top_score = jnp.maximum(jnp.max(scores, axis=-1), own_score)
    weights = jnp.exp(scores - top_score[..., None])
    own_weight = jnp.exp(own_score - top_score)
    total_mass = jnp.sum(weights, axis=-1) + own_weight
    prob_rows = (weights / total_mass[..., None]).astype(jnp.bfloat16)
    own_prob = (own_weight / total_mass).astype(jnp.bfloat16)
    context = jnp.einsum(
        "bhgt,bthd->bhgd", prob_rows, cached_values, preferred_element_type=jnp.float32
    )
    context = context + own_prob.astype(jnp.float32)[..., None] * new_value[:, :, None, :]
    attended = context.reshape(row_count, kv_local * group_size * HEAD).astype(jnp.bfloat16)
    return (new_kv, attended)


def solution(mesh):
    in_specs = (
        P("replica", "tensor"),
        P(),
        P(None, None, "tensor"),
        P("replica", "tensor", None),
        P("replica", None, None, "tensor"),
        P("replica", "tensor"),
        P("replica", None, None, "tensor"),
        P("replica", None),
        P("replica", None),
        P("replica"),
    )
    out_specs = (P("replica", None, "tensor"), P("replica", "tensor"))
    return jax.shard_map(body, mesh=mesh, in_specs=in_specs, out_specs=out_specs, check_vma=False)
```

profile of v0, /device:TPU:0, one launch (start us, length us, event | category | flops | bytes accessed | tf_op | source)
XLA Modules:
  0.0 256.9 jit_solution(18434199444916356622)
XLA Ops:
  0.6 0.8 fusion.26
  2.5 13.5 %all_to_all.22 = s32[8,1,2]{2,1,0:T(1,128)S(1)} all-to-all(s32[8,1,2]{2,1,0:T(1,128)S(1)} %copy.82), channel_id=1, replica_groups=mesh['replica'=8,'tensor'=4] {'replica'}, dimensions={0} | all-to-all | bytes 128 | tf_op jit(solution)/shard_map/all_to_all | solution.py:96
  16.3 8.1 %gather_fusion.4 = bf16[16,2048,128]{2,1,0:T(8,128)(2,1)} fusion(bf16[16,2048,128]{2,1,0:T(8,128)(2,1)} %param.13, s32[1024]{0:T(1024)S(1)} %pad_clamp_fusion.4), kind=kCustom, calls=%fused_computation.4 | custom fusion | bytes 16777280 | tf_op jit(solution)/shard_map/gather | solution.py:97
  24.4 5.0 %all-to-all-start.2 = ((bf16[8,2,2048,128]{3,2,1,0:T(8,128)(2,1)}), bf16[8,2,2048,128]{3,2,1,0:T(8,128)(2,1)}, u32[]{:S(2)}, u32[]{:S(2)}) async-start(bf16[8,2,2048,128]{3,2,1,0:T(8,128)(2,1)} %bitcast.100), calls=%async_computation.2 | async-start | bytes 16777216 | tf_op jit(solution)/shard_map/all_to_all | solution.py:99
  29.4 8.0 %copy.109 = bf16[1024,8,2,256]{3,1,2,0:T(8,128)(2,1)} copy(bf16[1024,8,2,256]{3,2,1,0:T(2,128)(2,1)} %bitcast.104) | data formatting | bytes 16777216
  37.4 11.3 %copy.81 = bf16[512,8192]{1,0:T(8,128)(2,1)} copy(bf16[512,8192]{0,1:T(8,128)(2,1)} %bitcast.102) | data formatting | bytes 16777216 | tf_op jit(solution)/shard_map/dot_general | solution.py:112
  51.2 7.2 %all_gather.3 = bf16[32,8192]{1,0:T(8,128)(2,1)S(1)} all-gather(bf16[32,2048]{1,0:T(8,128)(2,1)S(1)} %copy-done.3), channel_id=1, replica_groups=mesh['replica'=8,'tensor'=4] {'tensor'}, dimensions={1}, use_global_device_ids=true | all-gather | bytes 655360 | tf_op jit(solution)/shard_map/all_gather | solution.py:56
  58.9 0.8 copy-done.2
  60.6 1.3 gather_fusion.6
  61.9 1.3 gather_fusion.5
  63.7 33.0 %fusion.28 = (bf16[32,512,1,256]{3,2,1,0:T(2,128)(2,1)}, bf16[32,512,1,256]{3,2,1,0:T(2,128)(2,1)}) fusion(bf16[32,512,2,256]{3,2,1,0:T(2,128)(2,1)} %param.16), kind=kLoop, calls=%fused_computation.94 | loop fusion | bytes 33554432 | tf_op jit(solution)/shard_map/slice | solution.py:125
  96.7 35.5 %copy.108 = bf16[32,512,1,256]{1,3,0,2:T(8,128)(2,1)} copy(bf16[32,512,1,256]{3,2,1,0:T(2,128)(2,1)} %get-tuple-element.17) | data formatting | bytes 16777216
  132.2 35.6 %copy.107 = bf16[32,512,1,256]{1,3,0,2:T(8,128)(2,1)} copy(bf16[32,512,1,256]{3,2,1,0:T(2,128)(2,1)} %get-tuple-element.16) | data formatting | bytes 16777216
  167.9 1.7 gather_fusion
  169.6 41.7 %all-to-all-done.2 = bf16[8,2,2048,128]{3,2,1,0:T(8,128)(2,1)} async-done(((bf16[8,2,2048,128]{3,2,1,0:T(8,128)(2,1)}), bf16[8,2,2048,128]{3,2,1,0:T(8,128)(2,1)}, u32[]{:S(2)}, u32[]{:S(2)}) %all-to-all-start.2) | async-done | bytes 8388640 | tf_op jit(solution)/shard_map/all_to_all | solution.py:99
  211.3 3.6 %all-to-all-start.1 = ((bf16[8,2,2,64,256]{4,3,2,1,0:T(8,128)(2,1)}), bf16[8,2,2,64,256]{4,3,2,1,0:T(8,128)(2,1)S(1)}, u32[]{:S(2)}, u32[]{:S(2)}) async-start(bf16[8,2,2,64,256]{4,3,2,1,0:T(8,128)(2,1)} %bitcast.7), calls=%async_computation.1 | async-start | bytes 2097152 | tf_op jit(solution)/shard_map/all_to_all | solution.py:100
  214.9 5.3 %fusion.29 = (f32[32,2,8]{2,1,0:T(2,128)}, f32[32,2,8,512]{3,2,1,0:T(8,128)S(1)}) fusion(bf16[32,2,8,128]{3,2,1,0:T(8,128)(2,1)S(1)} %bitcast.105, bf16[32,512,2,128]{1,3,2,0:T(8,128)(2,1)} %bitcast.99, pred[32,512]{1,0:T(8,128)(4,1)S(1)} %iota_compare_fusion), kind=kOutput, calls=%fused_computation.95 | convolution fusion | flops 67894784 | bytes 9586688 | tf_op jit(solution)/shard_map/bhgd,bthd->bhgt/dot_general | solution.py:128
  220.2 0.8 copy.95
  221.7 0.8 iota_compare_fusion.2
  222.5 1.4 multiply_cosine_fusion
  223.8 5.2 %fusion.10 = f32[8,2,4,128]{3,2,1,0:T(4,128)} fusion(bf16[8,2,2048,128]{3,2,1,0:T(8,128)(2,1)} %all-to-all-done.2, bf16[8,2,4,2048]{3,2,1,0:T(4,128)(2,1)S(1)} %reshape.408, pred[8,2,4]{2,1,0:T(4,128)(4,1)S(1)} %iota_compare_fusion.2), kind=kOutput, calls=%fused_computation.26 | convolution fusion | flops 33685504 | bytes 8683584 | tf_op jit(solution)/shard_map/oksd,okdr->oksr/dot_general | solution.py:101
  229.1 12.1 %psum.7 = bf16[8,2,4,128]{3,2,1,0:T(4,128)(2,1)S(1)} all-reduce(f32[8,2,4,128]{3,2,1,0:T(4,128)} %fusion.10), channel_id=1, replica_groups=mesh['replica'=8,'tensor'=4] {'tensor'}, use_global_device_ids=true, to_apply=%region_6.7 | all-reduce | flops 8192 | bytes 49152 | tf_op jit(solution)/shard_map/psum | solution.py:104
  242.2 6.2 %convolution_add_fusion.1 = f32[32,2,256]{2,0,1:T(8,128)S(1)} fusion(bf16[2,256,8192]{2,1,0:T(8,128)(2,1)} %bitcast.101, bf16[32,8192]{1,0:T(8,128)(2,1)} %copy-done.2, f32[32,2,256]{2,1,0:T(2,128)S(1)} %gather_fusion.7), kind=kOutput, calls=%fused_computation.16 | convolution fusion | flops 268451840 | bytes 9043968 | tf_op jit(solution)/shard_map/dot_general | solution.py:112
  250.5 5.7 %fusion.1 = bf16[32,2,8,128]{3,2,1,0:T(8,128)(2,1)S(1)} fusion(bf16[32,512,2,128]{1,3,2,0:T(8,128)(2,1)} %bitcast.103, f32[32,2,8,512]{3,2,1,0:T(8,128)S(1)} %get-tuple-element.27, f32[32,2,8]{2,1,0:T(2,128)S(1)} %copy.98, f32[32,2,8]{2,1,0:T(2,128)S(1)} %copy.96, f32[32,2,128]{2,1,0:T(2,128)S(1)} %reshape.382, f32[32,2,8]{2,1,0:T(2,128)S(1)} %copy.101), kind=kOutput, calls=%fused_computation.13 | convolution fusion | flops 68091904 | bytes 9607168 | tf_op jit(solution)/shard_map/bhgt,bthd->bhgd/dot_general | solution.py:145
  (90 shorter events, 10.3 us)
Async XLA Ops:
  0.6 167.3 %copy-start = (bf16[16,2,64,256]{3,2,1,0:T(8,128)(2,1)S(1)}, bf16[16,2,64,256]{3,2,1,0:T(8,128)(2,1)}, u32[]{:S(2)}) copy-start(bf16[16,2,64,256]{3,2,1,0:T(8,128)(2,1)} %param.14) | copy-start | bytes 3145732
  24.4 186.9 %all-to-all-start.2 = ((bf16[8,2,2048,128]{3,2,1,0:T(8,128)(2,1)}), bf16[8,2,2048,128]{3,2,1,0:T(8,128)(2,1)}, u32[]{:S(2)}, u32[]{:S(2)}) async-start(bf16[8,2,2048,128]{3,2,1,0:T(8,128)(2,1)} %bitcast.100), calls=%async_computation.2 | async-start | bytes 16777216 | tf_op jit(solution)/shard_map/all_to_all | solution.py:99
  37.4 11.4 %copy-start.1 = (s32[1,16]{1,0:T(1,128)S(1)}, s32[1,16]{1,0:T(1,128)}, u32[]{:S(2)}) copy-start(s32[1,16]{1,0:T(1,128)} %param.18) | copy-start | bytes 196
  48.7 2.5 copy-start.3
  48.7 9.9 %copy-start.8 = (f32[8192]{0:T(1024)S(1)}, f32[8192]{0:T(1024)}, u32[]{:S(2)}) copy-start(f32[8192]{0:T(1024)} %param.11) | copy-start | bytes 98308
  48.7 14.5 %copy-start.9 = (s32[32]{0:T(128)S(1)}, s32[32]{0:T(128)}, u32[]{:S(2)}) copy-start(s32[32]{0:T(128)} %param.19) | copy-start | bytes 388
  51.0 7.7 %copy-start.7 = (s32[8,2]{1,0:T(8,128)}, s32[8,2]{1,0:T(8,128)S(1)}, u32[]{:S(2)}) copy-start(s32[8,2]{1,0:T(8,128)S(1)} %copy.87) | copy-start | bytes 196
  58.9 0.8 copy-start.2
  96.7 35.5 %copy-start.4 = (bf16[32,2048]{1,0:T(8,128)(2,1)S(1)}, bf16[32,2048]{1,0:T(8,128)(2,1)}, u32[]{:S(2)}) copy-start(bf16[32,2048]{1,0:T(8,128)(2,1)} %param.15) | copy-start | bytes 393220
  211.3 30.0 %all-to-all-start.1 = ((bf16[8,2,2,64,256]{4,3,2,1,0:T(8,128)(2,1)}), bf16[8,2,2,64,256]{4,3,2,1,0:T(8,128)(2,1)S(1)}, u32[]{:S(2)}, u32[]{:S(2)}) async-start(bf16[8,2,2,64,256]{4,3,2,1,0:T(8,128)(2,1)} %bitcast.7), calls=%async_computation.1 | async-start | bytes 2097152 | tf_op jit(solution)/shard_map/all_to_all | solution.py:100
  229.1 19.4 %copy-start.5 = (f32[32,64]{1,0:T(8,128)S(1)}, f32[32,64]{1,0:T(8,128)}, u32[]{:S(2)}) copy-start(f32[32,64]{1,0:T(8,128)} %get-tuple-element.22) | copy-start | bytes 24580
  229.1 19.4 %copy-start.6 = (f32[32,64]{1,0:T(8,128)S(1)}, f32[32,64]{1,0:T(8,128)}, u32[]{:S(2)}) copy-start(f32[32,64]{1,0:T(8,128)} %get-tuple-element.23) | copy-start | bytes 24580
where the time goes:
time: 260 us; the launch traced here: 257 us
  local copies, waits for them, and re-layouts  143 us (55%)
  waiting for transfers between devices  41.7 us (16%)
  blocking collectives  32.8 us (13%)
  matrix products  22.9 us (9%)
  starting transfers between devices  8.57 us (3%)
  other arithmetic  6.85 us (3%)
    unnamed x26, local copies, waits for them, and re-layouts  81.3 us
    all_to_all x1, waiting for transfers between devices, body(): lax.all_to_all(selected_down, 'replica', split_axis=0, concat_axis=0, til...  41.7 us
    slice x1, local copies, waits for them, and re-layouts, body(): key_value_cache[:, :, 0].reshape(row_count, cache_len, kv_local, HEAD)  33 us
    all_to_all x1, blocking collectives, body(): lax.all_to_all(wanted, 'replica', split_axis=0, concat_axis=0, tiled=True)  13.5 us
    psum x1, blocking collectives, body(): summed = lax.psum(partial_value, 'tensor').astype(jnp.bfloat16)  12.1 us
    dot_general x1, local copies, waits for them, and re-layouts, body(): jnp.dot(normed, key_value_weight.reshape(key_value_weight.shape[0], 2 * k...  11.3 us
    gather x1, local copies, waits for them, and re-layouts, body(): selected_down = adapter_down[segment_member_mask]  8.13 us
    all_gather x1, blocking collectives, body(): gathered = lax.all_gather(hidden, 'tensor', axis=1, tiled=True)  7.2 us
  transfers between devices with their start and end apart: 2, of which 1 were waited for; matrix products, arithmetic and copies ran while one was open for 57% of the time, Pallas kernels for 0%

commit v1 on v0

--- a/solution.py
+++ b/solution.py
@@ -1,6 +1,10 @@
+import functools
+
 import jax
 import jax.numpy as jnp
 from jax import lax
+from jax.experimental import pallas as pl
+from jax.experimental.pallas import tpu as pltpu
 from jax.sharding import PartitionSpec as P
 
 HEAD = 128
@@ -31,6 +35,64 @@
         ],
         axis=-1,
     )
+
+
+def attention_kernel(len_ref, q_ref, kv_ref, nkv_ref, o_ref, *, rows, kv_local, group_size):
+    scale = float(HEAD) ** (-0.5)
+    step = pl.program_id(0)
+    cache_len = kv_ref.shape[1]
+    for i in range(rows):
+        length = len_ref[step * rows + i]
+        keys = kv_ref[i, :, 0, :]
+        values = kv_ref[i, :, 1, :]
+        live = lax.broadcasted_iota(jnp.int32, (group_size, cache_len), 1) < length
+        for h in range(kv_local):
+            cols = slice(h * HEAD, (h + 1) * HEAD)
+            qrows = slice(h * group_size, (h + 1) * group_size)
+            q = q_ref[i, qrows, :]
+            scores = lax.dot_general(
+                q, keys[:, cols], (((1,), (1,)), ((), ())), preferred_element_type=jnp.float32
+            ) * scale
+            scores = jnp.where(live, scores, -jnp.inf)
+            new_key = nkv_ref[i, 0:1, cols].astype(jnp.float32)
+            new_value = nkv_ref[i, 1:2, cols].astype(jnp.float32)
+            own = jnp.sum(q.astype(jnp.float32) * new_key, axis=1, keepdims=True) * scale
+            top = jnp.maximum(jnp.max(scores, axis=1, keepdims=True), own)
+            weights = jnp.exp(scores - top)
+            own_weight = jnp.exp(own - top)
+            total = jnp.sum(weights, axis=1, keepdims=True) + own_weight
+            probs = (weights / total).astype(jnp.bfloat16)
+            own_prob = (own_weight / total).astype(jnp.bfloat16).astype(jnp.float32)
+            context = jnp.dot(probs, values[:, cols], preferred_element_type=jnp.float32)
+            context = context + own_prob * new_value
+            o_ref[i, qrows, :] = context.astype(o_ref.dtype)
+
+
+def attend(query, key_value_cache, new_kv, cached_length, kv_local, group_size):
+    row_count = query.shape[0]
+    cache_len = key_value_cache.shape[1]
+    width = key_value_cache.shape[3]
+    heads = kv_local * group_size
+    rows = 4
+    query_heads = query.reshape(row_count, heads, HEAD)
+    kernel = functools.partial(
+        attention_kernel, rows=rows, kv_local=kv_local, group_size=group_size
+    )
+    out = pl.pallas_call(
+        kernel,
+        out_shape=jax.ShapeDtypeStruct((row_count, heads, HEAD), jnp.bfloat16),
+        grid_spec=pltpu.PrefetchScalarGridSpec(
+            num_scalar_prefetch=1,
+            grid=(row_count // rows,),
+            in_specs=[
+                pl.BlockSpec((rows, heads, HEAD), lambda b, lens: (b, 0, 0)),
+                pl.BlockSpec((rows, cache_len, 2, width), lambda b, lens: (b, 0, 0, 0)),
+                pl.BlockSpec((rows, 2, width), lambda b, lens: (b, 0, 0)),
+            ],
+            out_specs=pl.BlockSpec((rows, heads, HEAD), lambda b, lens: (b, 0, 0)),
+        ),
+    )(cached_length, query_heads, key_value_cache, new_kv)
+    return out.reshape(row_count, heads * HEAD)
 
 
 def body(
@@ -120,33 +182,7 @@
     ).reshape(row_count, kv_width)
     new_kv = jnp.stack([rotated, current_key_value[:, 1]], axis=1).astype(jnp.bfloat16)
     group_size = query.shape[1] // HEAD // kv_local
-    scale = float(HEAD) ** (-0.5)
-    query_heads = query.reshape(row_count, kv_local, group_size, HEAD)
-    cached_keys = key_value_cache[:, :, 0].reshape(row_count, cache_len, kv_local, HEAD)
-    cached_values = key_value_cache[:, :, 1].reshape(row_count, cache_len, kv_local, HEAD)
-    scores = (
-        jnp.einsum("bhgd,bthd->bhgt", query_heads, cached_keys, preferred_element_type=jnp.float32)
-        * scale
-    )
-    is_live = jnp.arange(cache_len, dtype=jnp.int32)[None, :] < cached_length[:, None]
-    scores = jnp.where(is_live[:, None, None, :], scores, -jnp.inf)
-    new_key = new_kv[:, 0].reshape(row_count, kv_local, HEAD)
-    new_value = new_kv[:, 1].astype(jnp.float32).reshape(row_count, kv_local, HEAD)
-    own_score = (
-        jnp.einsum("bhgd,bhd->bhg", query_heads, new_key, preferred_element_type=jnp.float32)
-        * scale
-    )
-    top_score = jnp.maximum(jnp.max(scores, axis=-1), own_score)
-    weights = jnp.exp(scores - top_score[..., None])
-    own_weight = jnp.exp(own_score - top_score)
-    total_mass = jnp.sum(weights, axis=-1) + own_weight
-    prob_rows = (weights / total_mass[..., None]).astype(jnp.bfloat16)
-    own_prob = (own_weight / total_mass).astype(jnp.bfloat16)
-    context = jnp.einsum(
-        "bhgt,bthd->bhgd", prob_rows, cached_values, preferred_element_type=jnp.float32
-    )
-    context = context + own_prob.astype(jnp.float32)[..., None] * new_value[:, :, None, :]
-    attended = context.reshape(row_count, kv_local * group_size * HEAD).astype(jnp.bfloat16)
+    attended = attend(query, key_value_cache, new_kv, cached_length, kv_local, group_size)
     return (new_kv, attended)
 
 

time: 260 us -> 315 us (1.21)
  waiting for transfers between devices: 41.7 us -> 169 us
  local copies, waits for them, and re-layouts: 143 us -> 36.9 us
  Pallas kernels: 0 us -> 52.7 us
  matrix products: 22.9 us -> 10.9 us
    all_to_all x1, waiting for transfers between devices: 41.7 us -> 169 us  [body(): lax.all_to_all(selected_down, 'replica', split_axis=0, concat_axis=0, til...]
    unnamed x26 -> x17, local copies, waits for them, and re-layouts: 81.3 us -> 10.3 us
    pallas_call x0 -> x1, Pallas kernels: none -> 52.7 us  [attend(): pl.pallas_call(kernel, out_shape=jax.ShapeDtypeStruct((row_count, heads,...]
    slice x1 -> x0, local copies, waits for them, and re-layouts: 33 us -> none  [body(): key_value_cache[:, :, 0].reshape(row_count, cache_len, kv_local, HEAD)]
    dot_general x3 -> x0, matrix products: 11.2 us -> none  [the longest x1 5.69 us: body(): jnp.einsum('bhgt,bthd->bhgd', prob_rows, cached_values, preferred_element...]
  transfers between devices with their start and end apart: 2 -> 2, of which waited for: 1 -> 1; matrix products, arithmetic and copies ran while one was open for 57% -> 12% of each run, Pallas kernels for 0% -> 0%
where the time goes in v1:
time: 315 us
  waiting for transfers between devices  169 us (54%)
  Pallas kernels  52.7 us (17%)
  local copies, waits for them, and re-layouts  36.9 us (12%)
  blocking collectives  32 us (10%)
  matrix products  10.9 us (3%)
  starting transfers between devices  8.71 us (3%)
  other arithmetic  3.97 us (1%)
    all_to_all x1, waiting for transfers between devices, body(): lax.all_to_all(selected_down, 'replica', split_axis=0, concat_axis=0, til...  169 us
    pallas_call x1, Pallas kernels, attend(): pl.pallas_call(kernel, out_shape=jax.ShapeDtypeStruct((row_count, heads,...  52.7 us
    all_to_all x1, blocking collectives, body(): lax.all_to_all(wanted, 'replica', split_axis=0, concat_axis=0, tiled=True)  13.5 us
    dot_general x1, local copies, waits for them, and re-layouts, body(): jnp.dot(normed, key_value_weight.reshape(key_value_weight.shape[0], 2 * k...  11.3 us
    psum x1, blocking collectives, body(): summed = lax.psum(partial_value, 'tensor').astype(jnp.bfloat16)  11.3 us
    unnamed x17, local copies, waits for them, and re-layouts  10.3 us
    gather x1, local copies, waits for them, and re-layouts, body(): selected_down = adapter_down[segment_member_mask]  8.14 us
    all_gather x1, blocking collectives, body(): gathered = lax.all_gather(hidden, 'tensor', axis=1, tiled=True)  7.2 us
  transfers between devices with their start and end apart: 2, of which 1 were waited for; matrix products, arithmetic and copies ran while one was open for 12% of the time, Pallas kernels for 0%

profile of v1, /device:TPU:0, one launch (start us, length us, event | category | flops | bytes accessed | tf_op | source)
XLA Modules:
  0.0 314.6 jit_solution(11189942218133958092)
XLA Ops:
  0.6 0.8 and_select_fusion.2
  1.4 0.7 fusion.17
  2.5 13.5 %all_to_all.22 = s32[8,1,2]{2,1,0:T(1,128)S(1)} all-to-all(s32[8,1,2]{2,1,0:T(1,128)S(1)} %copy.37), channel_id=1, replica_groups=mesh['replica'=8,'tensor'=4] {'replica'}, dimensions={0} | all-to-all | bytes 128 | tf_op jit(solution)/shard_map/all_to_all | solution.py:158
  16.3 8.1 %gather_fusion.4 = bf16[16,2048,128]{2,1,0:T(8,128)(2,1)} fusion(bf16[16,2048,128]{2,1,0:T(8,128)(2,1)} %param.13, s32[1024]{0:T(1024)S(1)} %pad_clamp_fusion.4), kind=kCustom, calls=%fused_computation.4 | custom fusion | bytes 16777280 | tf_op jit(solution)/shard_map/gather | solution.py:159
  24.4 5.1 %all-to-all-start.2 = ((bf16[8,2,2048,128]{3,2,1,0:T(8,128)(2,1)}), bf16[8,2,2048,128]{3,2,1,0:T(8,128)(2,1)}, u32[]{:S(2)}, u32[]{:S(2)}) async-start(bf16[8,2,2048,128]{3,2,1,0:T(8,128)(2,1)} %bitcast.70), calls=%async_computation.2 | async-start | bytes 16777216 | tf_op jit(solution)/shard_map/all_to_all | solution.py:161
  29.7 0.7 gather_fusion.1
  31.1 0.7 gather_fusion.2
  32.1 0.7 gather_fusion.6
  32.8 0.7 gather_fusion.5
  33.5 7.2 %all_gather.3 = bf16[32,8192]{1,0:T(8,128)(2,1)S(1)} all-gather(bf16[32,2048]{1,0:T(8,128)(2,1)S(1)} %copy-done.3), channel_id=1, replica_groups=mesh['replica'=8,'tensor'=4] {'tensor'}, dimensions={1}, use_global_device_ids=true | all-gather | bytes 655360 | tf_op jit(solution)/shard_map/all_gather | solution.py:118
  41.2 1.7 gather_fusion
  42.9 168.5 %all-to-all-done.2 = bf16[8,2,2048,128]{3,2,1,0:T(8,128)(2,1)} async-done(((bf16[8,2,2048,128]{3,2,1,0:T(8,128)(2,1)}), bf16[8,2,2048,128]{3,2,1,0:T(8,128)(2,1)}, u32[]{:S(2)}, u32[]{:S(2)}) %all-to-all-start.2) | async-done | bytes 8388640 | tf_op jit(solution)/shard_map/all_to_all | solution.py:161
  211.4 3.6 %all-to-all-start.1 = ((bf16[8,2,2,64,256]{4,3,2,1,0:T(8,128)(2,1)}), bf16[8,2,2,64,256]{4,3,2,1,0:T(8,128)(2,1)S(1)}, u32[]{:S(2)}, u32[]{:S(2)}) async-start(bf16[8,2,2,64,256]{4,3,2,1,0:T(8,128)(2,1)} %bitcast.7), calls=%async_computation.1 | async-start | bytes 2097152 | tf_op jit(solution)/shard_map/all_to_all | solution.py:162
  215.0 0.7 gather_fusion.3
  215.9 8.0 %copy.49 = bf16[1024,8,2,256]{3,1,2,0:T(8,128)(2,1)} copy(bf16[1024,8,2,256]{3,2,1,0:T(2,128)(2,1)} %bitcast.73) | data formatting | bytes 16777216
  223.9 11.3 %copy.36 = bf16[512,8192]{1,0:T(8,128)(2,1)} copy(bf16[512,8192]{0,1:T(8,128)(2,1)} %bitcast.72) | data formatting | bytes 16777216 | tf_op jit(solution)/shard_map/dot_general | solution.py:174
  235.3 0.7 copy.50
  236.2 6.0 %fusion.4 = f32[32,2,256]{2,0,1:T(8,128)S(1)} fusion(bf16[2,256,8192]{2,1,0:T(8,128)(2,1)} %bitcast.71, bf16[32,8192]{1,0:T(8,128)(2,1)S(1)} %fusion.3), kind=kOutput, calls=%fused_computation.15 | convolution fusion | flops 268435456 | bytes 8978432 | tf_op jit(solution)/shard_map/dot_general | solution.py:174
  242.2 4.6 %fusion.6 = f32[8,2,4,128]{3,2,1,0:T(4,128)S(1)} fusion(bf16[8,2,2048,128]{3,2,1,0:T(8,128)(2,1)} %all-to-all-done.2, bf16[8,2,4,2048]{3,2,1,0:T(4,128)(2,1)S(1)} %reshape.381, pred[8,2,4]{2,1,0:T(4,128)(4,1)S(1)} %iota_compare_fusion.1), kind=kOutput, calls=%fused_computation.17 | convolution fusion | flops 33685504 | bytes 8683584 | tf_op jit(solution)/shard_map/oksd,okdr->oksr/dot_general | solution.py:163
  246.8 11.3 %psum.7 = bf16[8,2,4,128]{3,2,1,0:T(4,128)(2,1)S(1)} all-reduce(f32[8,2,4,128]{3,2,1,0:T(4,128)S(1)} %fusion.6), channel_id=1, replica_groups=mesh['replica'=8,'tensor'=4] {'tensor'}, use_global_device_ids=true, to_apply=%region_6.7 | all-reduce | flops 8192 | bytes 49152 | tf_op jit(solution)/shard_map/psum | solution.py:166
  258.5 0.6 gather_fusion.7
  259.6 0.7 pad_maximum_fusion.nkv_ref
  260.3 52.7 %shard_map.113 = bf16[32,16,128]{2,1,0:T(8,128)(2,1)} custom-call(s32[32]{0:T(128)} %len_ref.1, bf16[32,16,128]{2,1,0:T(8,128)(2,1)} %bitcast.74, bf16[32,512,2,256]{3,2,1,0:T(2,128)(2,1)} %kv_ref.1, bf16[32,2,256]{2,1,0:T(2,128)(2,1)} %pad_maximum_fusion.nkv_ref), custom_call_target="tpu_custom_call" | custom-call | tf_op jit(solution)/shard_map/pallas_call | solution.py:81
  313.0 1.6 copy.56
  (66 shorter events, 3.5 us)
Async XLA Ops:
  0.6 40.6 %copy-start = (bf16[16,2,64,256]{3,2,1,0:T(8,128)(2,1)S(1)}, bf16[16,2,64,256]{3,2,1,0:T(8,128)(2,1)}, u32[]{:S(2)}) copy-start(bf16[16,2,64,256]{3,2,1,0:T(8,128)(2,1)} %param.14) | copy-start | bytes 3145732
  24.4 5.3 %copy-start.2 = (s32[1,16]{1,0:T(1,128)S(1)}, s32[1,16]{1,0:T(1,128)}, u32[]{:S(2)}) copy-start(s32[1,16]{1,0:T(1,128)} %param.18) | copy-start | bytes 196
  24.4 187.0 %all-to-all-start.2 = ((bf16[8,2,2048,128]{3,2,1,0:T(8,128)(2,1)}), bf16[8,2,2048,128]{3,2,1,0:T(8,128)(2,1)}, u32[]{:S(2)}, u32[]{:S(2)}) async-start(bf16[8,2,2048,128]{3,2,1,0:T(8,128)(2,1)} %bitcast.70), calls=%async_computation.2 | async-start | bytes 16777216 | tf_op jit(solution)/shard_map/all_to_all | solution.py:161
  29.5 4.0 %copy-start.3 = (bf16[32,2048]{1,0:T(8,128)(2,1)S(1)}, bf16[32,2048]{1,0:T(8,128)(2,1)}, u32[]{:S(2)}) copy-start(bf16[32,2048]{1,0:T(8,128)(2,1)} %param.10) | copy-start | bytes 393220
  29.5 11.5 %copy-start.5 = (f32[8192]{0:T(1024)S(1)}, f32[8192]{0:T(1024)}, u32[]{:S(2)}) copy-start(f32[8192]{0:T(1024)} %param.11) | copy-start | bytes 98308
  211.4 46.8 %all-to-all-start.1 = ((bf16[8,2,2,64,256]{4,3,2,1,0:T(8,128)(2,1)}), bf16[8,2,2,64,256]{4,3,2,1,0:T(8,128)(2,1)S(1)}, u32[]{:S(2)}, u32[]{:S(2)}) async-start(bf16[8,2,2,64,256]{4,3,2,1,0:T(8,128)(2,1)} %bitcast.7), calls=%async_computation.1 | async-start | bytes 2097152 | tf_op jit(solution)/shard_map/all_to_all | solution.py:162
  223.9 11.3 %copy-start.6 = (s32[32]{0:T(128)S(1)}, s32[32]{0:T(128)}, u32[]{:S(2)}) copy-start(s32[32]{0:T(128)} %len_ref.1) | copy-start | bytes 388
  223.9 11.3 %copy-start.4 = (bf16[32,2048]{1,0:T(8,128)(2,1)S(1)}, bf16[32,2048]{1,0:T(8,128)(2,1)}, u32[]{:S(2)}) copy-start(bf16[32,2048]{1,0:T(8,128)(2,1)} %param.15) | copy-start | bytes 393220
  260.3 54.3 %copy-start.1 = (bf16[16,2,64,256]{3,2,1,0:T(8,128)(2,1)S(1)}, bf16[16,2,64,256]{3,2,1,0:T(8,128)(2,1)}, u32[]{:S(2)}) copy-start(bf16[16,2,64,256]{3,2,1,0:T(8,128)(2,1)} %param.14) | copy-start | bytes 3145732

commit v2 on v1

--- a/solution.py
+++ b/solution.py
@@ -155,20 +155,25 @@
     slot_rows = jnp.where(
         slot_live[:, :, :, None], own_cols[source_row], jnp.zeros((), jnp.bfloat16)
     )
-    segment_member_mask = lax.all_to_all(wanted, "replica", split_axis=0, concat_axis=0, tiled=True)
-    selected_down = adapter_down[segment_member_mask]
-    selected_up = adapter_up[segment_member_mask]
-    down_got = lax.all_to_all(selected_down, "replica", split_axis=0, concat_axis=0, tiled=True)
-    up_got = lax.all_to_all(selected_up, "replica", split_axis=0, concat_axis=0, tiled=True)
+    tags = jnp.broadcast_to(
+        wanted.astype(jnp.bfloat16)[:, :, None, None], wanted.shape + (SLOT, HEAD)
+    )
+    payload = jnp.concatenate([slot_rows, tags], axis=3)
+    got = lax.all_to_all(payload, "replica", split_axis=0, concat_axis=0, tiled=True)
+    got_rows = got[..., :part_width]
+    got_ids = got[:, :, 0, part_width].astype(jnp.int32)
+    selected_down = adapter_down[got_ids]
+    selected_up = adapter_up[got_ids]
     partial_value = jnp.einsum(
-        "oksd,okdr->oksr", slot_rows, down_got, preferred_element_type=jnp.float32
+        "oksd,okdr->oksr", got_rows, selected_down, preferred_element_type=jnp.float32
     )
     summed = lax.psum(partial_value, "tensor").astype(jnp.bfloat16)
     summed = summed.reshape(summed.shape[:3] + (2, adapter_rank_size))
-    slot_delta = (
-        jnp.einsum("okscr,okcrw->okscw", summed, up_got, preferred_element_type=jnp.float32)
+    owner_delta = (
+        jnp.einsum("okscr,okcrw->okscw", summed, selected_up, preferred_element_type=jnp.float32)
         * ADAPTER_SCALE
     )
+    slot_delta = lax.all_to_all(owner_delta, "replica", split_axis=0, concat_axis=0, tiled=True)
     flat_delta = slot_delta.reshape((replicas * CAP * SLOT,) + slot_delta.shape[3:])
     adapter_delta = flat_delta[fetch_slot[segment_index] * SLOT + token_position]
     base_projection = jnp.dot(

time: 315 us -> 147 us (0.47)
  waiting for transfers between devices: 169 us -> 6.52 us
  blocking collectives: 32 us -> 19.6 us
  starting transfers between devices: 8.71 us -> 11.9 us
    all_to_all x2, waiting for transfers between devices: 169 us -> 6.52 us  [the longest x1 6.5 us: body(): lax.all_to_all(owner_delta, 'replica', split_axis=0, concat_axis=0, tiled...]
    all_to_all x1 -> x0, blocking collectives: 13.5 us -> none  [body(): lax.all_to_all(wanted, 'replica', split_axis=0, concat_axis=0, tiled=True)]
    all_to_all x2, starting transfers between devices: 8.71 us -> 11.9 us  [the longest x1 6.07 us: body(): lax.all_to_all(owner_delta, 'replica', split_axis=0, concat_axis=0, tiled...]
    unnamed x17 -> x14, local copies, waits for them, and re-layouts: 10.3 us -> 10.4 us
  transfers between devices with their start and end apart: 2 -> 2, of which waited for: 1 -> 1; matrix products, arithmetic and copies ran while one was open for 12% -> 19% of each run, Pallas kernels for 0% -> 0%
where the time goes in v2:
time: 147 us; the launch traced here: 146 us
  Pallas kernels  52.6 us (36%)
  local copies, waits for them, and re-layouts  37.3 us (25%)
  blocking collectives  19.6 us (13%)
  starting transfers between devices  11.9 us (8%)
  matrix products  11.5 us (8%)
  waiting for transfers between devices  6.52 us (4%)
  other arithmetic  5.65 us (4%)
    pallas_call x1, Pallas kernels, attend(): pl.pallas_call(kernel, out_shape=jax.ShapeDtypeStruct((row_count, heads,...  52.6 us
    dot_general x1, local copies, waits for them, and re-layouts, body(): jnp.dot(normed, key_value_weight.reshape(key_value_weight.shape[0], 2 * k...  11.4 us
    psum x1, blocking collectives, body(): summed = lax.psum(partial_value, 'tensor').astype(jnp.bfloat16)  11 us
    unnamed x14, local copies, waits for them, and re-layouts  10.4 us
    all_gather x1, blocking collectives, body(): gathered = lax.all_gather(hidden, 'tensor', axis=1, tiled=True)  8.65 us
    gather x1, local copies, waits for them, and re-layouts, body(): selected_down = adapter_down[got_ids]  8.11 us
    all_to_all x1, waiting for transfers between devices, body(): lax.all_to_all(owner_delta, 'replica', split_axis=0, concat_axis=0, tiled...  6.5 us
    all_to_all x1, starting transfers between devices, body(): lax.all_to_all(owner_delta, 'replica', split_axis=0, concat_axis=0, tiled...  6.07 us
  transfers between devices with their start and end apart: 2, of which 1 were waited for; matrix products, arithmetic and copies ran while one was open for 19% of the time, Pallas kernels for 0%

profile of v2, /device:TPU:0, one launch (start us, length us, event | category | flops | bytes accessed | tf_op | source)
XLA Modules:
  0.0 145.9 jit_solution(3279262149524823455)
XLA Ops:
  0.7 0.8 and_select_fusion.2
  1.4 0.7 fusion.15
  2.8 1.3 gather_fusion
  4.4 0.7 copy.83
  5.3 0.7 bitcast_subtract_fusion.1
  7.0 8.6 %all_gather.3 = bf16[32,8192]{1,0:T(8,128)(2,1)S(1)} all-gather(bf16[32,2048]{1,0:T(8,128)(2,1)S(1)} %copy-done.1), channel_id=1, replica_groups=mesh['replica'=8,'tensor'=4] {'tensor'}, dimensions={1}, use_global_device_ids=true | all-gather | bytes 655360 | tf_op jit(solution)/shard_map/all_gather | solution.py:118
  16.1 0.7 gather_fusion.2
  17.3 0.8 pad_maximum_fusion
  18.2 5.8 %all-to-all-start = ((bf16[8,2,4,2176]{3,2,1,0:T(4,128)(2,1)}), bf16[8,2,4,2176]{3,2,1,0:T(4,128)(2,1)S(1)}, u32[]{:S(2)}, u32[]{:S(2)}) async-start(bf16[8,2,4,2176]{3,2,1,0:T(4,128)(2,1)} %pad_maximum_fusion), calls=%async_computation | async-start | bytes 557056 | tf_op jit(solution)/shard_map/all_to_all | solution.py:162
  24.1 0.7 gather_fusion.6
  24.8 0.7 gather_fusion.5
  25.5 8.0 %copy.92 = bf16[1024,8,2,256]{3,1,2,0:T(8,128)(2,1)} copy(bf16[1024,8,2,256]{3,2,1,0:T(2,128)(2,1)} %bitcast.73) | data formatting | bytes 16777216
  33.5 11.4 %copy.78 = bf16[512,8192]{1,0:T(8,128)(2,1)} copy(bf16[512,8192]{0,1:T(8,128)(2,1)} %bitcast.72) | data formatting | bytes 16777216 | tf_op jit(solution)/shard_map/dot_general | solution.py:179
  44.9 6.0 %fusion.4 = f32[32,2,256]{2,0,1:T(8,128)S(1)} fusion(bf16[2,256,8192]{2,1,0:T(8,128)(2,1)} %bitcast.71, bf16[32,8192]{1,0:T(8,128)(2,1)S(1)} %fusion.3), kind=kOutput, calls=%fused_computation.15 | convolution fusion | flops 268435456 | bytes 8978432 | tf_op jit(solution)/shard_map/dot_general | solution.py:179
  51.2 8.1 %gather_fusion.4 = bf16[16,2048,128]{2,1,0:T(8,128)(2,1)} fusion(bf16[16,2048,128]{2,1,0:T(8,128)(2,1)} %param.13, s32[1024]{0:T(1024)S(1)} %pad_clamp_fusion.2), kind=kCustom, calls=%fused_computation.4 | custom fusion | bytes 16777280 | tf_op jit(solution)/shard_map/gather | solution.py:165
  59.3 4.6 %fusion.6 = f32[8,2,4,128]{3,2,1,0:T(4,128)S(1)} fusion(bf16[8,2,2048,128]{3,2,1,0:T(8,128)(2,1)} %bitcast.70, bf16[8,2,4,2176]{3,2,1,0:T(4,128)(2,1)S(1)} %all-to-all-done), kind=kOutput, calls=%fused_computation.18 | convolution fusion | flops 33554432 | bytes 8683520 | tf_op jit(solution)/shard_map/oksd,okdr->oksr/dot_general | solution.py:167
  63.9 11.0 %psum.7 = bf16[8,2,4,128]{3,2,1,0:T(4,128)(2,1)S(1)} all-reduce(f32[8,2,4,128]{3,2,1,0:T(4,128)S(1)} %fusion.6), channel_id=1, replica_groups=mesh['replica'=8,'tensor'=4] {'tensor'}, use_global_device_ids=true, to_apply=%region_6.7 | all-reduce | flops 8192 | bytes 49152 | tf_op jit(solution)/shard_map/psum | solution.py:170
  75.6 0.9 fusion
  76.5 6.1 %all-to-all-start.1 = ((f32[8,2,4,2,256]{4,2,3,1,0:T(4,128)}), f32[8,2,4,2,256]{4,2,3,1,0:T(4,128)S(1)}, u32[]{:S(2)}, u32[]{:S(2)}) async-start(f32[8,2,4,2,256]{4,2,3,1,0:T(4,128)} %fusion), calls=%async_computation.1 | async-start | bytes 262144 | tf_op jit(solution)/shard_map/all_to_all | solution.py:176
  82.6 0.7 copy.93
  83.4 6.5 %all-to-all-done.1 = f32[8,2,4,2,256]{4,2,3,1,0:T(4,128)S(1)} async-done(((f32[8,2,4,2,256]{4,2,3,1,0:T(4,128)}), f32[8,2,4,2,256]{4,2,3,1,0:T(4,128)S(1)}, u32[]{:S(2)}, u32[]{:S(2)}) %all-to-all-start.1) | async-done | bytes 131104 | tf_op jit(solution)/shard_map/all_to_all | solution.py:176
  91.0 0.7 pad_maximum_fusion.1.nkv_ref
  91.7 52.6 %shard_map.113 = bf16[32,16,128]{2,1,0:T(8,128)(2,1)} custom-call(s32[32]{0:T(128)} %len_ref.1, bf16[32,16,128]{2,1,0:T(8,128)(2,1)} %bitcast.75, bf16[32,512,2,256]{3,2,1,0:T(2,128)(2,1)} %kv_ref.1, bf16[32,2,256]{2,1,0:T(2,128)(2,1)} %pad_maximum_fusion.1.nkv_ref), custom_call_target="tpu_custom_call" | custom-call | tf_op jit(solution)/shard_map/pallas_call | solution.py:81
  144.3 1.6 %copy.99 = bf16[4,8,16,128]{3,1,2,0:T(8,128)(2,1)} copy(bf16[4,8,16,128]{3,2,1,0:T(8,128)(2,1)} %bitcast.76) | data formatting | bytes 262144
  (66 shorter events, 5.4 us)
Async XLA Ops:
  0.6 74.4 %copy-start = (bf16[16,2,64,256]{3,2,1,0:T(8,128)(2,1)S(1)}, bf16[16,2,64,256]{3,2,1,0:T(8,128)(2,1)}, u32[]{:S(2)}) copy-start(bf16[16,2,64,256]{3,2,1,0:T(8,128)(2,1)} %param.14) | copy-start | bytes 3145732
  0.6 6.3 %copy-start.1 = (bf16[32,2048]{1,0:T(8,128)(2,1)S(1)}, bf16[32,2048]{1,0:T(8,128)(2,1)}, u32[]{:S(2)}) copy-start(bf16[32,2048]{1,0:T(8,128)(2,1)} %param.10) | copy-start | bytes 393220
  0.7 15.2 %copy-start.3 = (f32[8192]{0:T(1024)S(1)}, f32[8192]{0:T(1024)}, u32[]{:S(2)}) copy-start(f32[8192]{0:T(1024)} %param.11) | copy-start | bytes 98308
  18.2 32.7 %all-to-all-start = ((bf16[8,2,4,2176]{3,2,1,0:T(4,128)(2,1)}), bf16[8,2,4,2176]{3,2,1,0:T(4,128)(2,1)S(1)}, u32[]{:S(2)}, u32[]{:S(2)}) async-start(bf16[8,2,4,2176]{3,2,1,0:T(4,128)(2,1)} %pad_maximum_fusion), calls=%async_computation | async-start | bytes 557056 | tf_op jit(solution)/shard_map/all_to_all | solution.py:162
  59.3 23.3 %copy-start.4 = (s32[32]{0:T(128)S(1)}, s32[32]{0:T(128)}, u32[]{:S(2)}) copy-start(s32[32]{0:T(128)} %len_ref.1) | copy-start | bytes 388
  59.3 23.3 %copy-start.2 = (bf16[32,2048]{1,0:T(8,128)(2,1)S(1)}, bf16[32,2048]{1,0:T(8,128)(2,1)}, u32[]{:S(2)}) copy-start(bf16[32,2048]{1,0:T(8,128)(2,1)} %param.15) | copy-start | bytes 393220
  76.5 13.4 %all-to-all-start.1 = ((f32[8,2,4,2,256]{4,2,3,1,0:T(4,128)}), f32[8,2,4,2,256]{4,2,3,1,0:T(4,128)S(1)}, u32[]{:S(2)}, u32[]{:S(2)}) async-start(f32[8,2,4,2,256]{4,2,3,1,0:T(4,128)} %fusion), calls=%async_computation.1 | async-start | bytes 262144 | tf_op jit(solution)/shard_map/all_to_all | solution.py:176

commit v3 on v2

--- a/solution.py
+++ b/solution.py
@@ -41,17 +41,19 @@
     scale = float(HEAD) ** (-0.5)
     step = pl.program_id(0)
     cache_len = kv_ref.shape[1]
+    width = kv_ref.shape[3]
+    pos = lax.broadcasted_iota(jnp.int32, (group_size, 2 * cache_len), 1)
     for i in range(rows):
         length = len_ref[step * rows + i]
-        keys = kv_ref[i, :, 0, :]
-        values = kv_ref[i, :, 1, :]
-        live = lax.broadcasted_iota(jnp.int32, (group_size, cache_len), 1) < length
+        stacked = kv_ref[i].reshape(2 * cache_len, width)
+        live = (pos % 2 == 0) & (pos < 2 * length)
         for h in range(kv_local):
             cols = slice(h * HEAD, (h + 1) * HEAD)
             qrows = slice(h * group_size, (h + 1) * group_size)
             q = q_ref[i, qrows, :]
+            block = stacked[:, cols]
             scores = lax.dot_general(
-                q, keys[:, cols], (((1,), (1,)), ((), ())), preferred_element_type=jnp.float32
+                q, block, (((1,), (1,)), ((), ())), preferred_element_type=jnp.float32
             ) * scale
             scores = jnp.where(live, scores, -jnp.inf)
             new_key = nkv_ref[i, 0:1, cols].astype(jnp.float32)
@@ -61,9 +63,9 @@
             weights = jnp.exp(scores - top)
             own_weight = jnp.exp(own - top)
             total = jnp.sum(weights, axis=1, keepdims=True) + own_weight
-            probs = (weights / total).astype(jnp.bfloat16)
+            probs = pltpu.roll(weights / total, 1, 1).astype(jnp.bfloat16)
             own_prob = (own_weight / total).astype(jnp.bfloat16).astype(jnp.float32)
-            context = jnp.dot(probs, values[:, cols], preferred_element_type=jnp.float32)
+            context = jnp.dot(probs, block, preferred_element_type=jnp.float32)
             context = context + own_prob * new_value
             o_ref[i, qrows, :] = context.astype(o_ref.dtype)
 

time: 147 us -> 128 us (0.87)
  Pallas kernels: 52.6 us -> 33.4 us
    pallas_call x1, Pallas kernels: 52.6 us -> 33.4 us  [attend(): pl.pallas_call(kernel, out_shape=jax.ShapeDtypeStruct((row_count, heads,...]
  transfers between devices with their start and end apart: 2 -> 2, of which waited for: 1 -> 1; matrix products, arithmetic and copies ran while one was open for 19% -> 22% of each run, Pallas kernels for 0% -> 0%
where the time goes in v3:
time: 128 us; the launch traced here: 127 us
  local copies, waits for them, and re-layouts  37.3 us (29%)
  Pallas kernels  33.4 us (26%)
  blocking collectives  19.6 us (15%)
  starting transfers between devices  11.8 us (9%)
  matrix products  11.5 us (9%)
  waiting for transfers between devices  6.52 us (5%)
  other arithmetic  5.65 us (4%)
    pallas_call x1, Pallas kernels, attend(): pl.pallas_call(kernel, out_shape=jax.ShapeDtypeStruct((row_count, heads,...  33.4 us
    dot_general x1, local copies, waits for them, and re-layouts, body(): jnp.dot(normed, key_value_weight.reshape(key_value_weight.shape[0], 2 * k...  11.4 us
    psum x1, blocking collectives, body(): summed = lax.psum(partial_value, 'tensor').astype(jnp.bfloat16)  11 us
    unnamed x14, local copies, waits for them, and re-layouts  10.4 us
    all_gather x1, blocking collectives, body(): gathered = lax.all_gather(hidden, 'tensor', axis=1, tiled=True)  8.65 us
    gather x1, local copies, waits for them, and re-layouts, body(): selected_down = adapter_down[got_ids]  8.15 us
    all_to_all x1, waiting for transfers between devices, body(): lax.all_to_all(owner_delta, 'replica', split_axis=0, concat_axis=0, tiled...  6.5 us
    all_to_all x1, starting transfers between devices, body(): lax.all_to_all(owner_delta, 'replica', split_axis=0, concat_axis=0, tiled...  6.03 us
  transfers between devices with their start and end apart: 2, of which 1 were waited for; matrix products, arithmetic and copies ran while one was open for 22% of the time, Pallas kernels for 0%

profile of v3, /device:TPU:0, one launch (start us, length us, event | category | flops | bytes accessed | tf_op | source)
XLA Modules:
  0.0 126.8 jit_solution(14575111698575176047)
XLA Ops:
  0.7 0.8 and_select_fusion.2
  1.4 0.7 fusion.15
  2.8 1.3 %gather_fusion = s32[16]{0:T(128)S(1)} fusion(s32[16]{0:T(128)} %bitcast.68, s32[1024]{0:T(1024)S(1)} %pad_clamp_fusion.4), kind=kCustom, calls=%fused_computation | custom fusion | bytes 192 | tf_op jit(solution)/shard_map/gather | solution.py:154
  4.4 0.7 copy.83
  5.3 0.7 bitcast_subtract_fusion.1
  7.0 8.6 %all_gather.3 = bf16[32,8192]{1,0:T(8,128)(2,1)S(1)} all-gather(bf16[32,2048]{1,0:T(8,128)(2,1)S(1)} %copy-done.1), channel_id=1, replica_groups=mesh['replica'=8,'tensor'=4] {'tensor'}, dimensions={1}, use_global_device_ids=true | all-gather | bytes 655360 | tf_op jit(solution)/shard_map/all_gather | solution.py:120
  16.1 0.7 gather_fusion.2
  17.3 0.8 pad_maximum_fusion
  18.2 5.8 %all-to-all-start = ((bf16[8,2,4,2176]{3,2,1,0:T(4,128)(2,1)}), bf16[8,2,4,2176]{3,2,1,0:T(4,128)(2,1)S(1)}, u32[]{:S(2)}, u32[]{:S(2)}) async-start(bf16[8,2,4,2176]{3,2,1,0:T(4,128)(2,1)} %pad_maximum_fusion), calls=%async_computation | async-start | bytes 557056 | tf_op jit(solution)/shard_map/all_to_all | solution.py:164
  24.1 0.7 gather_fusion.6
  24.8 0.7 gather_fusion.5
  25.5 8.0 %copy.92 = bf16[1024,8,2,256]{3,1,2,0:T(8,128)(2,1)} copy(bf16[1024,8,2,256]{3,2,1,0:T(2,128)(2,1)} %bitcast.73) | data formatting | bytes 16777216
  33.5 11.4 %copy.78 = bf16[512,8192]{1,0:T(8,128)(2,1)} copy(bf16[512,8192]{0,1:T(8,128)(2,1)} %bitcast.72) | data formatting | bytes 16777216 | tf_op jit(solution)/shard_map/dot_general | solution.py:181
  44.9 6.0 %fusion.4 = f32[32,2,256]{2,0,1:T(8,128)S(1)} fusion(bf16[2,256,8192]{2,1,0:T(8,128)(2,1)} %bitcast.71, bf16[32,8192]{1,0:T(8,128)(2,1)S(1)} %fusion.3), kind=kOutput, calls=%fused_computation.15 | convolution fusion | flops 268435456 | bytes 8978432 | tf_op jit(solution)/shard_map/dot_general | solution.py:181
  51.2 8.1 %gather_fusion.4 = bf16[16,2048,128]{2,1,0:T(8,128)(2,1)} fusion(bf16[16,2048,128]{2,1,0:T(8,128)(2,1)} %param.13, s32[1024]{0:T(1024)S(1)} %pad_clamp_fusion.2), kind=kCustom, calls=%fused_computation.4 | custom fusion | bytes 16777280 | tf_op jit(solution)/shard_map/gather | solution.py:167
  59.4 4.6 %fusion.6 = f32[8,2,4,128]{3,2,1,0:T(4,128)S(1)} fusion(bf16[8,2,2048,128]{3,2,1,0:T(8,128)(2,1)} %bitcast.70, bf16[8,2,4,2176]{3,2,1,0:T(4,128)(2,1)S(1)} %all-to-all-done), kind=kOutput, calls=%fused_computation.18 | convolution fusion | flops 33554432 | bytes 8683520 | tf_op jit(solution)/shard_map/oksd,okdr->oksr/dot_general | solution.py:169
  64.0 11.0 %psum.7 = bf16[8,2,4,128]{3,2,1,0:T(4,128)(2,1)S(1)} all-reduce(f32[8,2,4,128]{3,2,1,0:T(4,128)S(1)} %fusion.6), channel_id=1, replica_groups=mesh['replica'=8,'tensor'=4] {'tensor'}, use_global_device_ids=true, to_apply=%region_6.7 | all-reduce | flops 8192 | bytes 49152 | tf_op jit(solution)/shard_map/psum | solution.py:172
  75.7 0.9 fusion
  76.6 6.0 %all-to-all-start.1 = ((f32[8,2,4,2,256]{4,2,3,1,0:T(4,128)}), f32[8,2,4,2,256]{4,2,3,1,0:T(4,128)S(1)}, u32[]{:S(2)}, u32[]{:S(2)}) async-start(f32[8,2,4,2,256]{4,2,3,1,0:T(4,128)} %fusion), calls=%async_computation.1 | async-start | bytes 262144 | tf_op jit(solution)/shard_map/all_to_all | solution.py:178
  82.6 0.7 copy.93
  83.4 6.5 %all-to-all-done.1 = f32[8,2,4,2,256]{4,2,3,1,0:T(4,128)S(1)} async-done(((f32[8,2,4,2,256]{4,2,3,1,0:T(4,128)}), f32[8,2,4,2,256]{4,2,3,1,0:T(4,128)S(1)}, u32[]{:S(2)}, u32[]{:S(2)}) %all-to-all-start.1) | async-done | bytes 131104 | tf_op jit(solution)/shard_map/all_to_all | solution.py:178
  91.0 0.7 pad_maximum_fusion.1.nkv_ref
  91.7 33.4 %shard_map.113 = bf16[32,16,128]{2,1,0:T(8,128)(2,1)} custom-call(s32[32]{0:T(128)} %len_ref.1, bf16[32,16,128]{2,1,0:T(8,128)(2,1)} %bitcast.75, bf16[32,512,2,256]{3,2,1,0:T(2,128)(2,1)} %kv_ref.1, bf16[32,2,256]{2,1,0:T(2,128)(2,1)} %pad_maximum_fusion.1.nkv_ref), custom_call_target="tpu_custom_call" | custom-call | tf_op jit(solution)/shard_map/pallas_call | solution.py:83
  125.2 1.6 %copy.99 = bf16[4,8,16,128]{3,1,2,0:T(8,128)(2,1)} copy(bf16[4,8,16,128]{3,2,1,0:T(8,128)(2,1)} %bitcast.76) | data formatting | bytes 262144
  (66 shorter events, 5.4 us)
Async XLA Ops:
  0.6 74.4 %copy-start = (bf16[16,2,64,256]{3,2,1,0:T(8,128)(2,1)S(1)}, bf16[16,2,64,256]{3,2,1,0:T(8,128)(2,1)}, u32[]{:S(2)}) copy-start(bf16[16,2,64,256]{3,2,1,0:T(8,128)(2,1)} %param.14) | copy-start | bytes 3145732
  0.6 6.3 %copy-start.1 = (bf16[32,2048]{1,0:T(8,128)(2,1)S(1)}, bf16[32,2048]{1,0:T(8,128)(2,1)}, u32[]{:S(2)}) copy-start(bf16[32,2048]{1,0:T(8,128)(2,1)} %param.10) | copy-start | bytes 393220
  0.7 15.2 %copy-start.3 = (f32[8192]{0:T(1024)S(1)}, f32[8192]{0:T(1024)}, u32[]{:S(2)}) copy-start(f32[8192]{0:T(1024)} %param.11) | copy-start | bytes 98308
  18.2 32.7 %all-to-all-start = ((bf16[8,2,4,2176]{3,2,1,0:T(4,128)(2,1)}), bf16[8,2,4,2176]{3,2,1,0:T(4,128)(2,1)S(1)}, u32[]{:S(2)}, u32[]{:S(2)}) async-start(bf16[8,2,4,2176]{3,2,1,0:T(4,128)(2,1)} %pad_maximum_fusion), calls=%async_computation | async-start | bytes 557056 | tf_op jit(solution)/shard_map/all_to_all | solution.py:164
  59.3 23.3 %copy-start.4 = (s32[32]{0:T(128)S(1)}, s32[32]{0:T(128)}, u32[]{:S(2)}) copy-start(s32[32]{0:T(128)} %len_ref.1) | copy-start | bytes 388
  59.3 23.3 %copy-start.2 = (bf16[32,2048]{1,0:T(8,128)(2,1)S(1)}, bf16[32,2048]{1,0:T(8,128)(2,1)}, u32[]{:S(2)}) copy-start(bf16[32,2048]{1,0:T(8,128)(2,1)} %param.15) | copy-start | bytes 393220
  76.6 13.4 %all-to-all-start.1 = ((f32[8,2,4,2,256]{4,2,3,1,0:T(4,128)}), f32[8,2,4,2,256]{4,2,3,1,0:T(4,128)S(1)}, u32[]{:S(2)}, u32[]{:S(2)}) async-start(f32[8,2,4,2,256]{4,2,3,1,0:T(4,128)} %fusion), calls=%async_computation.1 | async-start | bytes 262144 | tf_op jit(solution)/shard_map/all_to_all | solution.py:178

commit v4 on v3

--- a/solution.py
+++ b/solution.py
@@ -178,11 +178,9 @@
     slot_delta = lax.all_to_all(owner_delta, "replica", split_axis=0, concat_axis=0, tiled=True)
     flat_delta = slot_delta.reshape((replicas * CAP * SLOT,) + slot_delta.shape[3:])
     adapter_delta = flat_delta[fetch_slot[segment_index] * SLOT + token_position]
-    base_projection = jnp.dot(
-        normed,
-        key_value_weight.reshape(key_value_weight.shape[0], 2 * kv_width),
-        preferred_element_type=jnp.float32,
-    ).reshape(row_count, 2, kv_width)
+    base_projection = jnp.einsum(
+        "jd,dcw->jcw", normed, key_value_weight, preferred_element_type=jnp.float32
+    )
     current_key_value = base_projection + adapter_delta
     rotated = rotate(
         current_key_value[:, 0].reshape(row_count, kv_local, HEAD), cached_length

time: 128 us -> 108 us (0.84)
  local copies, waits for them, and re-layouts: 37.3 us -> 17.9 us
  waiting for transfers between devices: 6.52 us -> 9.75 us
  starting transfers between devices: 11.8 us -> 10.1 us
    dot_general x1 -> x0, local copies, waits for them, and re-layouts: 11.4 us -> none  [body(): jnp.dot(normed, key_value_weight.reshape(key_value_weight.shape[0], 2 * k...]
    unnamed x14 -> x13, local copies, waits for them, and re-layouts: 10.4 us -> 2.37 us
    all_to_all x1, waiting for transfers between devices: 0.01 us -> 3.25 us  [body(): lax.all_to_all(payload, 'replica', split_axis=0, concat_axis=0, tiled=True)]
    all_to_all x1, starting transfers between devices: 6.03 us -> 4.33 us  [body(): lax.all_to_all(owner_delta, 'replica', split_axis=0, concat_axis=0, tiled...]
  transfers between devices with their start and end apart: 2 -> 2, of which waited for: 1 -> 2; matrix products, arithmetic and copies ran while one was open for 22% -> 7% of each run, Pallas kernels for 0% -> 0%
where the time goes in v4:
time: 108 us; the launch traced here: 107 us
  Pallas kernels  33.4 us (31%)
  blocking collectives  18.9 us (17%)
  local copies, waits for them, and re-layouts  17.9 us (17%)
  matrix products  10.5 us (10%)
  starting transfers between devices  10.1 us (9%)
  waiting for transfers between devices  9.75 us (9%)
  other arithmetic  5.64 us (5%)
    pallas_call x1, Pallas kernels, attend(): pl.pallas_call(kernel, out_shape=jax.ShapeDtypeStruct((row_count, heads,...  33.4 us
    psum x1, blocking collectives, body(): summed = lax.psum(partial_value, 'tensor').astype(jnp.bfloat16)  10.3 us
    all_gather x1, blocking collectives, body(): gathered = lax.all_gather(hidden, 'tensor', axis=1, tiled=True)  8.65 us
    gather x1, local copies, waits for them, and re-layouts, body(): selected_down = adapter_down[got_ids]  8.15 us
    all_to_all x1, waiting for transfers between devices, body(): lax.all_to_all(owner_delta, 'replica', split_axis=0, concat_axis=0, tiled...  6.5 us
    all_to_all x1, starting transfers between devices, body(): lax.all_to_all(payload, 'replica', split_axis=0, concat_axis=0, tiled=True)  5.81 us
    dot_general x1, matrix products, body(): jnp.einsum('jd,dcw->jcw', normed, key_value_weight, preferred_element_typ...  4.95 us
    dot_general x1, matrix products, body(): jnp.einsum('oksd,okdr->oksr', got_rows, selected_down, preferred_element_...  4.62 us
  transfers between devices with their start and end apart: 2, of which 2 were waited for; matrix products, arithmetic and copies ran while one was open for 7% of the time, Pallas kernels for 0%

profile of v4, /device:TPU:0, one launch (start us, length us, event | category | flops | bytes accessed | tf_op | source)
XLA Modules:
  0.0 107.2 jit_solution(11416209269258374876)
XLA Ops:
  0.7 0.8 and_select_fusion.2
  1.4 0.7 fusion.16
  2.8 1.3 %gather_fusion = s32[16]{0:T(128)S(1)} fusion(s32[16]{0:T(128)} %bitcast.62, s32[1024]{0:T(1024)S(1)} %pad_clamp_fusion.4), kind=kCustom, calls=%fused_computation | custom fusion | bytes 192 | tf_op jit(solution)/shard_map/gather | solution.py:154
  4.4 0.7 copy.83
  5.3 0.7 bitcast_subtract_fusion.1
  5.9 0.7 gather_fusion.1
  7.0 8.6 %all_gather.3 = bf16[32,8192]{1,0:T(8,128)(2,1)S(1)} all-gather(bf16[32,2048]{1,0:T(8,128)(2,1)S(1)} %copy-done.1), channel_id=1, replica_groups=mesh['replica'=8,'tensor'=4] {'tensor'}, dimensions={1}, use_global_device_ids=true | all-gather | bytes 655360 | tf_op jit(solution)/shard_map/all_gather | solution.py:120
  16.1 0.7 gather_fusion.2
  17.3 0.8 pad_maximum_fusion
  18.2 5.8 %all-to-all-start = ((bf16[8,2,4,2176]{3,2,1,0:T(4,128)(2,1)}), bf16[8,2,4,2176]{3,2,1,0:T(4,128)(2,1)S(1)}, u32[]{:S(2)}, u32[]{:S(2)}) async-start(bf16[8,2,4,2176]{3,2,1,0:T(4,128)(2,1)} %pad_maximum_fusion), calls=%async_computation | async-start | bytes 557056 | tf_op jit(solution)/shard_map/all_to_all | solution.py:164
  24.1 0.7 gather_fusion.6
  24.8 0.7 gather_fusion.5
  25.5 4.9 %fusion = f32[32,2,256]{2,0,1:T(8,128)S(1)} fusion(bf16[8192,2,256]{2,1,0:T(2,128)(2,1)} %param.12, bf16[32,8192]{1,0:T(8,128)(2,1)S(1)} %fusion.5), kind=kOutput, calls=%fused_computation.8 | convolution fusion | flops 268435456 | bytes 8978432 | tf_op jit(solution)/shard_map/jd,dcw->jcw/dot_general | solution.py:181
  30.4 3.2 %all-to-all-done = bf16[8,2,4,2176]{3,2,1,0:T(4,128)(2,1)S(1)} async-done(((bf16[8,2,4,2176]{3,2,1,0:T(4,128)(2,1)}), bf16[8,2,4,2176]{3,2,1,0:T(4,128)(2,1)S(1)}, u32[]{:S(2)}, u32[]{:S(2)}) %all-to-all-start) | async-done | bytes 278560 | tf_op jit(solution)/shard_map/all_to_all | solution.py:164
  34.0 8.1 %gather_fusion.4 = bf16[16,2048,128]{2,1,0:T(8,128)(2,1)} fusion(bf16[16,2048,128]{2,1,0:T(8,128)(2,1)} %param.13, s32[1024]{0:T(1024)S(1)} %pad_clamp_fusion.2), kind=kCustom, calls=%fused_computation.4 | custom fusion | bytes 16777280 | tf_op jit(solution)/shard_map/gather | solution.py:167
  42.1 4.6 %fusion.7 = f32[8,2,4,128]{3,2,1,0:T(4,128)S(1)} fusion(bf16[8,2,2048,128]{3,2,1,0:T(8,128)(2,1)} %bitcast.64, bf16[8,2,4,2176]{3,2,1,0:T(4,128)(2,1)S(1)} %all-to-all-done), kind=kOutput, calls=%fused_computation.19 | convolution fusion | flops 33554432 | bytes 8683520 | tf_op jit(solution)/shard_map/oksd,okdr->oksr/dot_general | solution.py:169
  46.8 10.3 %psum.7 = bf16[8,2,4,128]{3,2,1,0:T(4,128)(2,1)S(1)} all-reduce(f32[8,2,4,128]{3,2,1,0:T(4,128)S(1)} %fusion.7), channel_id=1, replica_groups=mesh['replica'=8,'tensor'=4] {'tensor'}, use_global_device_ids=true, to_apply=%region_6.7 | all-reduce | flops 8192 | bytes 49152 | tf_op jit(solution)/shard_map/psum | solution.py:172
  57.8 0.9 fusion.2
  58.7 4.3 %all-to-all-start.1 = ((f32[8,2,4,2,256]{4,2,3,1,0:T(4,128)}), f32[8,2,4,2,256]{4,2,3,1,0:T(4,128)S(1)}, u32[]{:S(2)}, u32[]{:S(2)}) async-start(f32[8,2,4,2,256]{4,2,3,1,0:T(4,128)} %fusion.2), calls=%async_computation.1 | async-start | bytes 262144 | tf_op jit(solution)/shard_map/all_to_all | solution.py:178
  63.0 0.7 copy.92
  63.8 6.5 %all-to-all-done.1 = f32[8,2,4,2,256]{4,2,3,1,0:T(4,128)S(1)} async-done(((f32[8,2,4,2,256]{4,2,3,1,0:T(4,128)}), f32[8,2,4,2,256]{4,2,3,1,0:T(4,128)S(1)}, u32[]{:S(2)}, u32[]{:S(2)}) %all-to-all-start.1) | async-done | bytes 131104 | tf_op jit(solution)/shard_map/all_to_all | solution.py:178
  71.4 0.7 pad_maximum_fusion.1.nkv_ref
  72.1 33.4 %shard_map.113 = bf16[32,16,128]{2,1,0:T(8,128)(2,1)} custom-call(s32[32]{0:T(128)} %len_ref.1, bf16[32,16,128]{2,1,0:T(8,128)(2,1)} %bitcast.66, bf16[32,512,2,256]{3,2,1,0:T(2,128)(2,1)} %kv_ref.1, bf16[32,2,256]{2,1,0:T(2,128)(2,1)} %pad_maximum_fusion.1.nkv_ref), custom_call_target="tpu_custom_call" | custom-call | tf_op jit(solution)/shard_map/pallas_call | solution.py:83
  105.6 1.6 %copy.100 = bf16[4,8,16,128]{3,1,2,0:T(8,128)(2,1)} copy(bf16[4,8,16,128]{3,2,1,0:T(8,128)(2,1)} %bitcast.67) | data formatting | bytes 262144
  (64 shorter events, 4.7 us)
Async XLA Ops:
  0.6 56.5 %copy-start = (bf16[16,2,64,256]{3,2,1,0:T(8,128)(2,1)S(1)}, bf16[16,2,64,256]{3,2,1,0:T(8,128)(2,1)}, u32[]{:S(2)}) copy-start(bf16[16,2,64,256]{3,2,1,0:T(8,128)(2,1)} %param.14) | copy-start | bytes 3145732
  0.6 6.3 %copy-start.1 = (bf16[32,2048]{1,0:T(8,128)(2,1)S(1)}, bf16[32,2048]{1,0:T(8,128)(2,1)}, u32[]{:S(2)}) copy-start(bf16[32,2048]{1,0:T(8,128)(2,1)} %param.10) | copy-start | bytes 393220
  0.7 15.2 %copy-start.3 = (f32[8192]{0:T(1024)S(1)}, f32[8192]{0:T(1024)}, u32[]{:S(2)}) copy-start(f32[8192]{0:T(1024)} %param.11) | copy-start | bytes 98308
  18.2 15.5 %all-to-all-start = ((bf16[8,2,4,2176]{3,2,1,0:T(4,128)(2,1)}), bf16[8,2,4,2176]{3,2,1,0:T(4,128)(2,1)S(1)}, u32[]{:S(2)}, u32[]{:S(2)}) async-start(bf16[8,2,4,2176]{3,2,1,0:T(4,128)(2,1)} %pad_maximum_fusion), calls=%async_computation | async-start | bytes 557056 | tf_op jit(solution)/shard_map/all_to_all | solution.py:164
  42.1 20.9 %copy-start.4 = (s32[32]{0:T(128)S(1)}, s32[32]{0:T(128)}, u32[]{:S(2)}) copy-start(s32[32]{0:T(128)} %len_ref.1) | copy-start | bytes 388
  42.1 20.9 %copy-start.2 = (bf16[32,2048]{1,0:T(8,128)(2,1)S(1)}, bf16[32,2048]{1,0:T(8,128)(2,1)}, u32[]{:S(2)}) copy-start(bf16[32,2048]{1,0:T(8,128)(2,1)} %param.15) | copy-start | bytes 393220
  58.7 11.7 %all-to-all-start.1 = ((f32[8,2,4,2,256]{4,2,3,1,0:T(4,128)}), f32[8,2,4,2,256]{4,2,3,1,0:T(4,128)S(1)}, u32[]{:S(2)}, u32[]{:S(2)}) async-start(f32[8,2,4,2,256]{4,2,3,1,0:T(4,128)} %fusion.2), calls=%async_computation.1 | async-start | bytes 262144 | tf_op jit(solution)/shard_map/all_to_all | solution.py:178

commit v5 on v4

--- a/solution.py
+++ b/solution.py
@@ -37,12 +37,13 @@
     )
 
 
-def attention_kernel(len_ref, q_ref, kv_ref, nkv_ref, o_ref, *, rows, kv_local, group_size):
+def cached_attention_kernel(len_ref, q_ref, kv_ref, acc_ref, stat_ref, *, rows, kv_local, group_size):
     scale = float(HEAD) ** (-0.5)
     step = pl.program_id(0)
     cache_len = kv_ref.shape[1]
     width = kv_ref.shape[3]
     pos = lax.broadcasted_iota(jnp.int32, (group_size, 2 * cache_len), 1)
+    lane = lax.broadcasted_iota(jnp.int32, (group_size, HEAD), 1)
     for i in range(rows):
         length = len_ref[step * rows + i]
         stacked = kv_ref[i].reshape(2 * cache_len, width)
@@ -56,21 +57,15 @@
                 q, block, (((1,), (1,)), ((), ())), preferred_element_type=jnp.float32
             ) * scale
             scores = jnp.where(live, scores, -jnp.inf)
-            new_key = nkv_ref[i, 0:1, cols].astype(jnp.float32)
-            new_value = nkv_ref[i, 1:2, cols].astype(jnp.float32)
-            own = jnp.sum(q.astype(jnp.float32) * new_key, axis=1, keepdims=True) * scale
-            top = jnp.maximum(jnp.max(scores, axis=1, keepdims=True), own)
+            top = jnp.max(scores, axis=1, keepdims=True)
             weights = jnp.exp(scores - top)
-            own_weight = jnp.exp(own - top)
-            total = jnp.sum(weights, axis=1, keepdims=True) + own_weight
-            probs = pltpu.roll(weights / total, 1, 1).astype(jnp.bfloat16)
-            own_prob = (own_weight / total).astype(jnp.bfloat16).astype(jnp.float32)
-            context = jnp.dot(probs, block, preferred_element_type=jnp.float32)
-            context = context + own_prob * new_value
-            o_ref[i, qrows, :] = context.astype(o_ref.dtype)
-
-
-def attend(query, key_value_cache, new_kv, cached_length, kv_local, group_size):
+            mass = jnp.sum(weights, axis=1, keepdims=True)
+            shifted = pltpu.roll(weights, 1, 1).astype(jnp.bfloat16)
+            acc_ref[i, qrows, :] = jnp.dot(shifted, block, preferred_element_type=jnp.float32)
+            stat_ref[i, qrows, :] = jnp.where(lane == 0, top, jnp.where(lane == 1, mass, 0.0))
+
+
+def cached_attention(query, key_value_cache, cached_length, kv_local, group_size):
     row_count = query.shape[0]
     cache_len = key_value_cache.shape[1]
     width = key_value_cache.shape[3]
@@ -78,23 +73,50 @@
     rows = 4
     query_heads = query.reshape(row_count, heads, HEAD)
     kernel = functools.partial(
-        attention_kernel, rows=rows, kv_local=kv_local, group_size=group_size
-    )
-    out = pl.pallas_call(
+        cached_attention_kernel, rows=rows, kv_local=kv_local, group_size=group_size
+    )
+    spec = pl.BlockSpec((rows, heads, HEAD), lambda b, lens: (b, 0, 0))
+    return pl.pallas_call(
         kernel,
-        out_shape=jax.ShapeDtypeStruct((row_count, heads, HEAD), jnp.bfloat16),
+        out_shape=(
+            jax.ShapeDtypeStruct((row_count, heads, HEAD), jnp.float32),
+            jax.ShapeDtypeStruct((row_count, heads, HEAD), jnp.float32),
+        ),
         grid_spec=pltpu.PrefetchScalarGridSpec(
             num_scalar_prefetch=1,
             grid=(row_count // rows,),
             in_specs=[
-                pl.BlockSpec((rows, heads, HEAD), lambda b, lens: (b, 0, 0)),
+                spec,
                 pl.BlockSpec((rows, cache_len, 2, width), lambda b, lens: (b, 0, 0, 0)),
-                pl.BlockSpec((rows, 2, width), lambda b, lens: (b, 0, 0)),
             ],
-            out_specs=pl.BlockSpec((rows, heads, HEAD), lambda b, lens: (b, 0, 0)),
+            out_specs=(spec, spec),
         ),
-    )(cached_length, query_heads, key_value_cache, new_kv)
-    return out.reshape(row_count, heads * HEAD)
+    )(cached_length, query_heads, key_value_cache)
+
+
+def attend(query, key_value_cache, new_kv, cached_length, kv_local, group_size):
+    row_count = query.shape[0]
+    heads = kv_local * group_size
+    scale = float(HEAD) ** (-0.5)
+    acc, stats = cached_attention(query, key_value_cache, cached_length, kv_local, group_size)
+    cached_top = stats[:, :, 0].reshape(row_count, kv_local, group_size)
+    cached_mass = stats[:, :, 1].reshape(row_count, kv_local, group_size)
+    acc = acc.reshape(row_count, kv_local, group_size, HEAD)
+    query_heads = query.reshape(row_count, kv_local, group_size, HEAD)
+    new_key = new_kv[:, 0].reshape(row_count, kv_local, HEAD)
+    new_value = new_kv[:, 1].astype(jnp.float32).reshape(row_count, kv_local, HEAD)
+    own_score = (
+        jnp.einsum("bhgd,bhd->bhg", query_heads, new_key, preferred_element_type=jnp.float32)
+        * scale
+    )
+    top = jnp.maximum(cached_top, own_score)
+    cached_factor = jnp.exp(cached_top - top)
+    own_weight = jnp.exp(own_score - top)
+    total = cached_mass * cached_factor + own_weight
+    own_prob = (own_weight / total).astype(jnp.bfloat16).astype(jnp.float32)
+    context = acc * (cached_factor / total)[..., None]
+    context = context + own_prob[..., None] * new_value[:, :, None, :]
+    return context.reshape(row_count, heads * HEAD).astype(jnp.bfloat16)
 
 
 def body(

time: 108 us -> 105 us (0.972)
  Pallas kernels: 33.4 us -> 27.8 us
  waiting for transfers between devices: 9.75 us -> 6.8 us
  starting transfers between devices: 10.1 us -> 11.9 us
  local copies, waits for them, and re-layouts: 17.9 us -> 19.5 us
    pallas_call x1, Pallas kernels: 33.4 us -> 27.8 us  [cached_attention(): pl.pallas_call(kernel, out_shape=(jax.ShapeDtypeStruct((row_count, heads,...]
    all_to_all x1, waiting for transfers between devices: 3.25 us -> 0.01 us  [body(): lax.all_to_all(payload, 'replica', split_axis=0, concat_axis=0, tiled=True)]
    all_to_all x1, starting transfers between devices: 4.33 us -> 6.07 us  [body(): lax.all_to_all(owner_delta, 'replica', split_axis=0, concat_axis=0, tiled...]
    slice x0 -> x3, local copies, waits for them, and re-layouts: none -> 1.53 us  [the longest x2 1.34 us: attend(): cached_top = stats[:, :, 0].reshape(row_count, kv_local, group_size)]
    unnamed x13 -> x17, local copies, waits for them, and re-layouts: 2.37 us -> 1.46 us
  transfers between devices with their start and end apart: 2 -> 2, of which waited for: 2 -> 1; matrix products, arithmetic and copies ran while one was open for 7% -> 4% of each run, Pallas kernels for 0% -> 27%
where the time goes in v5:
time: 105 us; the launch traced here: 104 us
  Pallas kernels  27.8 us (26%)
  blocking collectives  19.8 us (19%)
  local copies, waits for them, and re-layouts  19.5 us (19%)
  starting transfers between devices  11.9 us (11%)
  matrix products  11.4 us (11%)
  waiting for transfers between devices  6.8 us (6%)
  other arithmetic  6.01 us (6%)
    pallas_call x1, Pallas kernels, cached_attention(): pl.pallas_call(kernel, out_shape=(jax.ShapeDtypeStruct((row_count, heads,...  27.8 us
    psum x1, blocking collectives, body(): summed = lax.psum(partial_value, 'tensor').astype(jnp.bfloat16)  11.1 us
    all_gather x1, blocking collectives, body(): gathered = lax.all_gather(hidden, 'tensor', axis=1, tiled=True)  8.65 us
    gather x1, local copies, waits for them, and re-layouts, body(): selected_down = adapter_down[got_ids]  8.11 us
    all_to_all x1, waiting for transfers between devices, body(): lax.all_to_all(owner_delta, 'replica', split_axis=0, concat_axis=0, tiled...  6.8 us
    all_to_all x1, starting transfers between devices, body(): lax.all_to_all(owner_delta, 'replica', split_axis=0, concat_axis=0, tiled...  6.07 us
    all_to_all x1, starting transfers between devices, body(): lax.all_to_all(payload, 'replica', split_axis=0, concat_axis=0, tiled=True)  5.8 us
    dot_general x1, matrix products, body(): jnp.einsum('jd,dcw->jcw', normed, key_value_weight, preferred_element_typ...  4.93 us
  transfers between devices with their start and end apart: 2, of which 1 were waited for; matrix products, arithmetic and copies ran while one was open for 4% of the time, Pallas kernels for 27%

profile of v5, /device:TPU:0, one launch (start us, length us, event | category | flops | bytes accessed | tf_op | source)
XLA Modules:
  0.0 104.0 jit_solution(6849670898608674745)
XLA Ops:
  0.7 0.8 and_select_fusion.2
  1.4 0.7 fusion.27
  2.8 1.3 %gather_fusion = s32[16]{0:T(128)S(1)} fusion(s32[16]{0:T(128)} %bitcast.117, s32[1024]{0:T(1024)S(1)} %pad_clamp_fusion.4), kind=kCustom, calls=%fused_computation | custom fusion | bytes 192 | tf_op jit(solution)/shard_map/gather | solution.py:176
  4.4 0.7 copy.103
  5.3 0.7 bitcast_subtract_fusion.1
  5.9 0.7 gather_fusion.1
  7.0 8.6 %all_gather.3 = bf16[32,8192]{1,0:T(8,128)(2,1)S(1)} all-gather(bf16[32,2048]{1,0:T(8,128)(2,1)S(1)} %copy-done.3), channel_id=1, replica_groups=mesh['replica'=8,'tensor'=4] {'tensor'}, dimensions={1}, use_global_device_ids=true | all-gather | bytes 655360 | tf_op jit(solution)/shard_map/all_gather | solution.py:142
  16.1 0.7 gather_fusion.2
  17.3 0.8 pad_maximum_fusion
  18.2 5.8 %all-to-all-start = ((bf16[8,2,4,2176]{3,2,1,0:T(4,128)(2,1)}), bf16[8,2,4,2176]{3,2,1,0:T(4,128)(2,1)S(1)}, u32[]{:S(2)}, u32[]{:S(2)}) async-start(bf16[8,2,4,2176]{3,2,1,0:T(4,128)(2,1)} %pad_maximum_fusion), calls=%async_computation | async-start | bytes 557056 | tf_op jit(solution)/shard_map/all_to_all | solution.py:186
  24.1 0.7 gather_fusion.6
  24.8 0.7 gather_fusion.5
  25.5 0.7 copy.118
  26.2 27.8 %shard_map.113 = (f32[32,16,128]{2,1,0:T(8,128)}, f32[32,16,128]{2,1,0:T(8,128)}) custom-call(s32[32]{0:T(128)} %len_ref.1, bf16[32,16,128]{2,1,0:T(8,128)(2,1)} %bitcast.123, bf16[32,512,2,256]{3,2,1,0:T(2,128)(2,1)} %kv_ref.1), custom_call_target="tpu_custom_call" | custom-call | tf_op jit(solution)/shard_map/pallas_call | solution.py:79
  53.9 1.2 %fusion.28 = (f32[32,16,1]{2,1,0:T(8,128)S(1)}, f32[32,16,1]{2,1,0:T(8,128)S(1)}) fusion(f32[32,16,128]{2,1,0:T(8,128)} %get-tuple-element.5), kind=kLoop, calls=%fused_computation.92 | loop fusion | bytes 8192 | tf_op jit(solution)/shard_map/slice | solution.py:102
  55.4 8.1 %gather_fusion.4 = bf16[16,2048,128]{2,1,0:T(8,128)(2,1)} fusion(bf16[16,2048,128]{2,1,0:T(8,128)(2,1)} %param.13, s32[1024]{0:T(1024)S(1)} %pad_clamp_fusion.2), kind=kCustom, calls=%fused_computation.4 | custom fusion | bytes 16777280 | tf_op jit(solution)/shard_map/gather | solution.py:189
  63.5 4.6 %fusion.11 = f32[8,2,4,128]{3,2,1,0:T(4,128)S(1)} fusion(bf16[8,2,2048,128]{3,2,1,0:T(8,128)(2,1)} %bitcast.119, bf16[8,2,4,2176]{3,2,1,0:T(4,128)(2,1)S(1)} %all-to-all-done), kind=kOutput, calls=%fused_computation.23 | convolution fusion | flops 33554432 | bytes 8683520 | tf_op jit(solution)/shard_map/oksd,okdr->oksr/dot_general | solution.py:191
  68.1 11.1 %psum.7 = bf16[8,2,4,128]{3,2,1,0:T(4,128)(2,1)S(1)} all-reduce(f32[8,2,4,128]{3,2,1,0:T(4,128)S(1)} %fusion.11), channel_id=1, replica_groups=mesh['replica'=8,'tensor'=4] {'tensor'}, use_global_device_ids=true, to_apply=%region_6.7 | all-reduce | flops 8192 | bytes 49152 | tf_op jit(solution)/shard_map/psum | solution.py:194
  79.3 0.7 reshape.359
  80.6 1.7 %fusion.2 = f32[8,2,4,2,256]{4,2,3,1,0:T(4,128)} fusion(bf16[8,2,2,64,256]{4,3,2,1,0:T(8,128)(2,1)S(1)} %bitcast.120, bf16[8,2,4,2,64]{4,3,2,1,0:T(2,128)(2,1)} %reshape.359), kind=kOutput, calls=%fused_computation.13 | convolution fusion | flops 4227072 | bytes 1196032 | tf_op jit(solution)/shard_map/okscr,okcrw->okscw/dot_general | solution.py:197
  82.2 6.1 %all-to-all-start.1 = ((f32[8,2,4,2,256]{4,2,3,1,0:T(4,128)}), f32[8,2,4,2,256]{4,2,3,1,0:T(4,128)S(1)}, u32[]{:S(2)}, u32[]{:S(2)}) async-start(f32[8,2,4,2,256]{4,2,3,1,0:T(4,128)} %fusion.2), calls=%async_computation.1 | async-start | bytes 262144 | tf_op jit(solution)/shard_map/all_to_all | solution.py:200
  88.9 6.8 %all-to-all-done.1 = f32[8,2,4,2,256]{4,2,3,1,0:T(4,128)S(1)} async-done(((f32[8,2,4,2,256]{4,2,3,1,0:T(4,128)}), f32[8,2,4,2,256]{4,2,3,1,0:T(4,128)S(1)}, u32[]{:S(2)}, u32[]{:S(2)}) %all-to-all-start.1) | async-done | bytes 131104 | tf_op jit(solution)/shard_map/all_to_all | solution.py:200
  96.4 4.9 %fusion.3 = f32[32,2,256]{2,0,1:T(8,128)S(1)} fusion(bf16[8192,2,256]{2,1,0:T(2,128)(2,1)} %param.12, bf16[32,8192]{1,0:T(8,128)(2,1)S(1)} %fusion.8, f32[32,2,256]{2,1,0:T(2,128)S(1)} %gather_fusion.7), kind=kOutput, calls=%fused_computation.14 | convolution fusion | flops 268451840 | bytes 9043968 | tf_op jit(solution)/shard_map/jd,dcw->jcw/dot_general | solution.py:203
  103.2 0.9 fusion.10
  (81 shorter events, 6.4 us)
Async XLA Ops:
  0.6 79.3 %copy-start = (bf16[16,2,64,256]{3,2,1,0:T(8,128)(2,1)S(1)}, bf16[16,2,64,256]{3,2,1,0:T(8,128)(2,1)}, u32[]{:S(2)}) copy-start(bf16[16,2,64,256]{3,2,1,0:T(8,128)(2,1)} %param.14) | copy-start | bytes 3145732
  0.6 6.3 %copy-start.3 = (bf16[32,2048]{1,0:T(8,128)(2,1)S(1)}, bf16[32,2048]{1,0:T(8,128)(2,1)}, u32[]{:S(2)}) copy-start(bf16[32,2048]{1,0:T(8,128)(2,1)} %param.10) | copy-start | bytes 393220
  0.7 15.2 %copy-start.5 = (f32[8192]{0:T(1024)S(1)}, f32[8192]{0:T(1024)}, u32[]{:S(2)}) copy-start(f32[8192]{0:T(1024)} %param.11) | copy-start | bytes 98308
  0.7 24.8 %copy-start.4 = (bf16[32,2048]{1,0:T(8,128)(2,1)S(1)}, bf16[32,2048]{1,0:T(8,128)(2,1)}, u32[]{:S(2)}) copy-start(bf16[32,2048]{1,0:T(8,128)(2,1)} %param.15) | copy-start | bytes 393220
  18.2 36.9 %all-to-all-start = ((bf16[8,2,4,2176]{3,2,1,0:T(4,128)(2,1)}), bf16[8,2,4,2176]{3,2,1,0:T(4,128)(2,1)S(1)}, u32[]{:S(2)}, u32[]{:S(2)}) async-start(bf16[8,2,4,2176]{3,2,1,0:T(4,128)(2,1)} %pad_maximum_fusion), calls=%async_computation | async-start | bytes 557056 | tf_op jit(solution)/shard_map/all_to_all | solution.py:186
  63.5 24.8 %copy-start.6 = (s32[32]{0:T(128)S(1)}, s32[32]{0:T(128)}, u32[]{:S(2)}) copy-start(s32[32]{0:T(128)} %len_ref.1) | copy-start | bytes 388
  68.1 33.5 %copy-start.1 = (bf16[4,8,16,128]{3,2,1,0:T(8,128)(2,1)S(1)}, bf16[4,8,16,128]{3,2,1,0:T(8,128)(2,1)}, u32[]{:S(2)}) copy-start(bf16[4,8,16,128]{3,2,1,0:T(8,128)(2,1)} %copy.118) | copy-start | bytes 393220
  68.1 35.0 %copy-start.2 = (f32[32,16,128]{2,1,0:T(8,128)S(1)}, f32[32,16,128]{2,1,0:T(8,128)}, u32[]{:S(2)}) copy-start(f32[32,16,128]{2,1,0:T(8,128)} %get-tuple-element.4) | copy-start | bytes 786436
  82.2 13.4 %all-to-all-start.1 = ((f32[8,2,4,2,256]{4,2,3,1,0:T(4,128)}), f32[8,2,4,2,256]{4,2,3,1,0:T(4,128)S(1)}, u32[]{:S(2)}, u32[]{:S(2)}) async-start(f32[8,2,4,2,256]{4,2,3,1,0:T(4,128)} %fusion.2), calls=%async_computation.1 | async-start | bytes 262144 | tf_op jit(solution)/shard_map/all_to_all | solution.py:200

commit v6 on v4

--- a/solution.py
+++ b/solution.py
@@ -97,6 +97,18 @@
     return out.reshape(row_count, heads * HEAD)
 
 
+def butterfly_sum(value, axis):
+    size = lax.axis_size(axis)
+    if size & (size - 1):
+        return lax.psum(value, axis)
+    stride = 1
+    while stride < size:
+        pairs = [(i, i ^ stride) for i in range(size)]
+        value = value + lax.ppermute(value, axis, pairs)
+        stride *= 2
+    return value
+
+
 def body(
     hidden,
     input_norm_gain,
@@ -169,7 +181,7 @@
     partial_value = jnp.einsum(
         "oksd,okdr->oksr", got_rows, selected_down, preferred_element_type=jnp.float32
     )
-    summed = lax.psum(partial_value, "tensor").astype(jnp.bfloat16)
+    summed = butterfly_sum(partial_value, "tensor").astype(jnp.bfloat16)
     summed = summed.reshape(summed.shape[:3] + (2, adapter_rank_size))
     owner_delta = (
         jnp.einsum("okscr,okcrw->okscw", summed, selected_up, preferred_element_type=jnp.float32)

time: 108 us -> 101 us (0.935)
  blocking collectives: 18.9 us -> 8.65 us
  waiting for transfers between devices: 9.75 us -> 13.1 us
    psum x1 -> x0, blocking collectives: 10.3 us -> none  [body(): summed = lax.psum(partial_value, 'tensor').astype(jnp.bfloat16)]
    ppermute x0 -> x2, waiting for transfers between devices: none -> 3.36 us  [butterfly_sum(): value = value + lax.ppermute(value, axis, pairs)]
    ppermute x0 -> x2, starting transfers between devices: none -> 1.22 us  [butterfly_sum(): value = value + lax.ppermute(value, axis, pairs)]
  transfers between devices with their start and end apart: 2 -> 4, of which waited for: 2 -> 4; matrix products, arithmetic and copies ran while one was open for 7% -> 8% of each run, Pallas kernels for 0% -> 0%
where the time goes in v6:
time: 101 us
  Pallas kernels  33.4 us (33%)
  local copies, waits for them, and re-layouts  17.9 us (18%)
  waiting for transfers between devices  13.1 us (13%)
  starting transfers between devices  10.6 us (10%)
  matrix products  10.5 us (10%)
  blocking collectives  8.65 us (9%)
  other arithmetic  5.66 us (6%)
    pallas_call x1, Pallas kernels, attend(): pl.pallas_call(kernel, out_shape=jax.ShapeDtypeStruct((row_count, heads,...  33.4 us
    all_gather x1, blocking collectives, body(): gathered = lax.all_gather(hidden, 'tensor', axis=1, tiled=True)  8.65 us
    gather x1, local copies, waits for them, and re-layouts, body(): selected_down = adapter_down[got_ids]  8.15 us
    all_to_all x1, waiting for transfers between devices, body(): lax.all_to_all(owner_delta, 'replica', split_axis=0, concat_axis=0, tiled...  6.5 us
    all_to_all x1, starting transfers between devices, body(): lax.all_to_all(payload, 'replica', split_axis=0, concat_axis=0, tiled=True)  5.81 us
    dot_general x1, matrix products, body(): jnp.einsum('jd,dcw->jcw', normed, key_value_weight, preferred_element_typ...  4.94 us
    dot_general x1, matrix products, body(): jnp.einsum('oksd,okdr->oksr', got_rows, selected_down, preferred_element_...  4.6 us
    all_to_all x1, starting transfers between devices, body(): lax.all_to_all(owner_delta, 'replica', split_axis=0, concat_axis=0, tiled...  3.6 us
  transfers between devices with their start and end apart: 4, of which 4 were waited for; matrix products, arithmetic and copies ran while one was open for 8% of the time, Pallas kernels for 0%

profile of v6, /device:TPU:0, one launch (start us, length us, event | category | flops | bytes accessed | tf_op | source)
XLA Modules:
  0.0 100.8 jit_solution(5362204909715581204)
XLA Ops:
  0.7 0.8 and_select_fusion.2
  1.4 0.7 fusion.16
  2.8 1.3 %gather_fusion = s32[16]{0:T(128)S(1)} fusion(s32[16]{0:T(128)} %bitcast.62, s32[1024]{0:T(1024)S(1)} %pad_clamp_fusion.4), kind=kCustom, calls=%fused_computation | custom fusion | bytes 192 | tf_op jit(solution)/shard_map/gather | solution.py:166
  4.4 0.7 copy.83
  5.3 0.7 bitcast_subtract_fusion.1
  7.0 8.6 %all_gather.3 = bf16[32,8192]{1,0:T(8,128)(2,1)S(1)} all-gather(bf16[32,2048]{1,0:T(8,128)(2,1)S(1)} %copy-done.1), channel_id=1, replica_groups=mesh['replica'=8,'tensor'=4] {'tensor'}, dimensions={1}, use_global_device_ids=true | all-gather | bytes 655360 | tf_op jit(solution)/shard_map/all_gather | solution.py:132
  16.1 0.7 gather_fusion.2
  17.3 0.8 pad_maximum_fusion
  18.2 5.8 %all-to-all-start = ((bf16[8,2,4,2176]{3,2,1,0:T(4,128)(2,1)}), bf16[8,2,4,2176]{3,2,1,0:T(4,128)(2,1)S(1)}, u32[]{:S(2)}, u32[]{:S(2)}) async-start(bf16[8,2,4,2176]{3,2,1,0:T(4,128)(2,1)} %pad_maximum_fusion), calls=%async_computation | async-start | bytes 557056 | tf_op jit(solution)/shard_map/all_to_all | solution.py:176
  24.1 0.7 gather_fusion.6
  24.8 0.7 gather_fusion.5
  25.5 4.9 %fusion = f32[32,2,256]{2,0,1:T(8,128)S(1)} fusion(bf16[8192,2,256]{2,1,0:T(2,128)(2,1)} %param.12, bf16[32,8192]{1,0:T(8,128)(2,1)S(1)} %fusion.5), kind=kOutput, calls=%fused_computation.8 | convolution fusion | flops 268435456 | bytes 8978432 | tf_op jit(solution)/shard_map/jd,dcw->jcw/dot_general | solution.py:193
  30.4 3.3 %all-to-all-done = bf16[8,2,4,2176]{3,2,1,0:T(4,128)(2,1)S(1)} async-done(((bf16[8,2,4,2176]{3,2,1,0:T(4,128)(2,1)}), bf16[8,2,4,2176]{3,2,1,0:T(4,128)(2,1)S(1)}, u32[]{:S(2)}, u32[]{:S(2)}) %all-to-all-start) | async-done | bytes 278560 | tf_op jit(solution)/shard_map/all_to_all | solution.py:176
  34.0 8.1 %gather_fusion.4 = bf16[16,2048,128]{2,1,0:T(8,128)(2,1)} fusion(bf16[16,2048,128]{2,1,0:T(8,128)(2,1)} %param.13, s32[1024]{0:T(1024)S(1)} %pad_clamp_fusion.2), kind=kCustom, calls=%fused_computation.4 | custom fusion | bytes 16777280 | tf_op jit(solution)/shard_map/gather | solution.py:179
  42.1 4.6 %fusion.7 = f32[8,2,4,128]{3,2,1,0:T(4,128)S(1)} fusion(bf16[8,2,2048,128]{3,2,1,0:T(8,128)(2,1)} %bitcast.64, bf16[8,2,4,2176]{3,2,1,0:T(4,128)(2,1)S(1)} %all-to-all-done), kind=kOutput, calls=%fused_computation.19 | convolution fusion | flops 33554432 | bytes 8683520 | tf_op jit(solution)/shard_map/oksd,okdr->oksr/dot_general | solution.py:181
  46.8 1.2 %collective-permute-done = f32[8,2,4,128]{3,2,1,0:T(4,128)S(1)} collective-permute-done((f32[8,2,4,128]{3,2,1,0:T(4,128)S(1)}, f32[8,2,4,128]{3,2,1,0:T(4,128)S(1)}, u32[]{:S(2)}, u32[]{:S(2)}) %collective-permute-start) | collective-permute-done | bytes 32800 | tf_op jit(solution)/shard_map/ppermute | solution.py:107
  48.0 1.2 %collective-permute-start.1 = (f32[8,2,4,128]{3,2,1,0:T(4,128)S(1)}, f32[8,2,4,128]{3,2,1,0:T(4,128)S(1)}, u32[]{:S(2)}, u32[]{:S(2)}) collective-permute-start(f32[8,2,4,128]{3,2,1,0:T(4,128)S(1)} %add.146), channel_id=1, source_target_pairs={{0,2},{1,3},{2,0},{3,1},{4,6},{5,7},{6,4},{7,5},{8,10},{9,11},{10,... | collective-permute-start | bytes 98312 | tf_op jit(solution)/shard_map/ppermute | solution.py:107
  49.8 2.2 %collective-permute-done.1 = f32[8,2,4,128]{3,2,1,0:T(4,128)S(1)} collective-permute-done((f32[8,2,4,128]{3,2,1,0:T(4,128)S(1)}, f32[8,2,4,128]{3,2,1,0:T(4,128)S(1)}, u32[]{:S(2)}, u32[]{:S(2)}) %collective-permute-start.1) | collective-permute-done | bytes 32800 | tf_op jit(solution)/shard_map/ppermute | solution.py:107
  52.1 0.9 fusion.2
  53.0 3.6 %all-to-all-start.1 = ((f32[8,2,4,2,256]{4,2,3,1,0:T(4,128)}), f32[8,2,4,2,256]{4,2,3,1,0:T(4,128)S(1)}, u32[]{:S(2)}, u32[]{:S(2)}) async-start(f32[8,2,4,2,256]{4,2,3,1,0:T(4,128)} %fusion.2), calls=%async_computation.1 | async-start | bytes 262144 | tf_op jit(solution)/shard_map/all_to_all | solution.py:190
  57.5 6.5 %all-to-all-done.1 = f32[8,2,4,2,256]{4,2,3,1,0:T(4,128)S(1)} async-done(((f32[8,2,4,2,256]{4,2,3,1,0:T(4,128)}), f32[8,2,4,2,256]{4,2,3,1,0:T(4,128)S(1)}, u32[]{:S(2)}, u32[]{:S(2)}) %all-to-all-start.1) | async-done | bytes 131104 | tf_op jit(solution)/shard_map/all_to_all | solution.py:190
  65.0 0.7 pad_maximum_fusion.1.nkv_ref
  65.7 33.4 %shard_map.113 = bf16[32,16,128]{2,1,0:T(8,128)(2,1)} custom-call(s32[32]{0:T(128)} %len_ref.1, bf16[32,16,128]{2,1,0:T(8,128)(2,1)} %bitcast.66, bf16[32,512,2,256]{3,2,1,0:T(2,128)(2,1)} %kv_ref.1, bf16[32,2,256]{2,1,0:T(2,128)(2,1)} %pad_maximum_fusion.1.nkv_ref), custom_call_target="tpu_custom_call" | custom-call | tf_op jit(solution)/shard_map/pallas_call | solution.py:83
  99.2 1.6 %copy.100 = bf16[4,8,16,128]{3,1,2,0:T(8,128)(2,1)} copy(bf16[4,8,16,128]{3,2,1,0:T(8,128)(2,1)} %bitcast.67) | data formatting | bytes 262144
  (69 shorter events, 6.1 us)
Async XLA Ops:
  0.6 48.6 %copy-start = (bf16[16,2,64,256]{3,2,1,0:T(8,128)(2,1)S(1)}, bf16[16,2,64,256]{3,2,1,0:T(8,128)(2,1)}, u32[]{:S(2)}) copy-start(bf16[16,2,64,256]{3,2,1,0:T(8,128)(2,1)} %param.14) | copy-start | bytes 3145732
  0.6 6.3 %copy-start.1 = (bf16[32,2048]{1,0:T(8,128)(2,1)S(1)}, bf16[32,2048]{1,0:T(8,128)(2,1)}, u32[]{:S(2)}) copy-start(bf16[32,2048]{1,0:T(8,128)(2,1)} %param.10) | copy-start | bytes 393220
  0.7 15.2 %copy-start.3 = (f32[8192]{0:T(1024)S(1)}, f32[8192]{0:T(1024)}, u32[]{:S(2)}) copy-start(f32[8192]{0:T(1024)} %param.11) | copy-start | bytes 98308
  18.2 15.5 %all-to-all-start = ((bf16[8,2,4,2176]{3,2,1,0:T(4,128)(2,1)}), bf16[8,2,4,2176]{3,2,1,0:T(4,128)(2,1)S(1)}, u32[]{:S(2)}, u32[]{:S(2)}) async-start(bf16[8,2,4,2176]{3,2,1,0:T(4,128)(2,1)} %pad_maximum_fusion), calls=%async_computation | async-start | bytes 557056 | tf_op jit(solution)/shard_map/all_to_all | solution.py:176
  42.1 14.5 %copy-start.4 = (s32[32]{0:T(128)S(1)}, s32[32]{0:T(128)}, u32[]{:S(2)}) copy-start(s32[32]{0:T(128)} %len_ref.1) | copy-start | bytes 388
  42.1 14.5 %copy-start.2 = (bf16[32,2048]{1,0:T(8,128)(2,1)S(1)}, bf16[32,2048]{1,0:T(8,128)(2,1)}, u32[]{:S(2)}) copy-start(bf16[32,2048]{1,0:T(8,128)(2,1)} %param.15) | copy-start | bytes 393220
  46.7 1.3 %collective-permute-start = (f32[8,2,4,128]{3,2,1,0:T(4,128)S(1)}, f32[8,2,4,128]{3,2,1,0:T(4,128)S(1)}, u32[]{:S(2)}, u32[]{:S(2)}) collective-permute-start(f32[8,2,4,128]{3,2,1,0:T(4,128)S(1)} %fusion.7), channel_id=1, source_target_pairs={{0,1},{1,0},{2,3},{3,2},{4,5},{5,4},{6,7},{7,6},{8,9},{9,8},{10,11... | collective-permute-start | bytes 98312 | tf_op jit(solution)/shard_map/ppermute | solution.py:107
  48.0 4.0 %collective-permute-start.1 = (f32[8,2,4,128]{3,2,1,0:T(4,128)S(1)}, f32[8,2,4,128]{3,2,1,0:T(4,128)S(1)}, u32[]{:S(2)}, u32[]{:S(2)}) collective-permute-start(f32[8,2,4,128]{3,2,1,0:T(4,128)S(1)} %add.146), channel_id=1, source_target_pairs={{0,2},{1,3},{2,0},{3,1},{4,6},{5,7},{6,4},{7,5},{8,10},{9,11},{10,... | collective-permute-start | bytes 98312 | tf_op jit(solution)/shard_map/ppermute | solution.py:107
  53.0 10.9 %all-to-all-start.1 = ((f32[8,2,4,2,256]{4,2,3,1,0:T(4,128)}), f32[8,2,4,2,256]{4,2,3,1,0:T(4,128)S(1)}, u32[]{:S(2)}, u32[]{:S(2)}) async-start(f32[8,2,4,2,256]{4,2,3,1,0:T(4,128)} %fusion.2), calls=%async_computation.1 | async-start | bytes 262144 | tf_op jit(solution)/shard_map/all_to_all | solution.py:190

commit v7 on v6

--- a/solution.py
+++ b/solution.py
@@ -109,6 +109,24 @@
     return value
 
 
+def butterfly_gather(value, axis):
+    size = lax.axis_size(axis)
+    if size & (size - 1):
+        return lax.all_gather(value, axis, axis=1, tiled=True)
+    index = lax.axis_index(axis)
+    stride = 1
+    while stride < size:
+        pairs = [(i, i ^ stride) for i in range(size)]
+        other = lax.ppermute(value, axis, pairs)
+        value = jnp.where(
+            (index & stride) == 0,
+            jnp.concatenate([value, other], axis=1),
+            jnp.concatenate([other, value], axis=1),
+        )
+        stride *= 2
+    return value
+
+
 def body(
     hidden,
     input_norm_gain,
@@ -129,7 +147,7 @@
     adapter_rank_size = adapter_up.shape[2]
     replicas = lax.axis_size("replica")
     segments = segment_sizes.shape[1]
-    gathered = lax.all_gather(hidden, "tensor", axis=1, tiled=True)
+    gathered = butterfly_gather(hidden, "tensor")
     widened = gathered.astype(jnp.float32)
     normed = (
         widened

time: 101 us -> 102 us (level)
  blocking collectives: 8.65 us -> 0 us
  waiting for transfers between devices: 13.1 us -> 18.9 us
  starting transfers between devices: 10.6 us -> 14.5 us
    all_gather x1 -> x0, blocking collectives: 8.65 us -> none  [body(): gathered = lax.all_gather(hidden, 'tensor', axis=1, tiled=True)]
    ppermute x0 -> x2, waiting for transfers between devices: none -> 6 us  [butterfly_gather(): other = lax.ppermute(value, axis, pairs)]
    all_to_all x1, waiting for transfers between devices: 3.28 us -> 8.2 us  [body(): lax.all_to_all(payload, 'replica', split_axis=0, concat_axis=0, tiled=True)]
    all_to_all x1, waiting for transfers between devices: 6.5 us -> 2.4 us  [body(): lax.all_to_all(owner_delta, 'replica', split_axis=0, concat_axis=0, tiled...]
    ppermute x0 -> x2, starting transfers between devices: none -> 3.19 us  [butterfly_gather(): other = lax.ppermute(value, axis, pairs)]
    ppermute x2, waiting for transfers between devices: 3.36 us -> 2.28 us  [butterfly_sum(): value = value + lax.ppermute(value, axis, pairs)]
  transfers between devices with their start and end apart: 4 -> 6, of which waited for: 4 -> 5; matrix products, arithmetic and copies ran while one was open for 8% -> 14% of each run, Pallas kernels for 0% -> 0%
where the time goes in v7:
time: 102 us
  Pallas kernels  33.4 us (33%)
  waiting for transfers between devices  18.9 us (19%)
  local copies, waits for them, and re-layouts  17.9 us (18%)
  starting transfers between devices  14.5 us (14%)
  matrix products  10.5 us (10%)
  other arithmetic  5.71 us (6%)
    pallas_call x1, Pallas kernels, attend(): pl.pallas_call(kernel, out_shape=jax.ShapeDtypeStruct((row_count, heads,...  33.4 us
    all_to_all x1, waiting for transfers between devices, body(): lax.all_to_all(payload, 'replica', split_axis=0, concat_axis=0, tiled=True)  8.2 us
    gather x1, local copies, waits for them, and re-layouts, body(): selected_down = adapter_down[got_ids]  8.15 us
    all_to_all x1, starting transfers between devices, body(): lax.all_to_all(payload, 'replica', split_axis=0, concat_axis=0, tiled=True)  6.04 us
    ppermute x2, waiting for transfers between devices, butterfly_gather(): other = lax.ppermute(value, axis, pairs)  6 us
    dot_general x1, matrix products, body(): jnp.einsum('jd,dcw->jcw', normed, key_value_weight, preferred_element_typ...  4.94 us
    dot_general x1, matrix products, body(): jnp.einsum('oksd,okdr->oksr', got_rows, selected_down, preferred_element_...  4.62 us
    all_to_all x1, starting transfers between devices, body(): lax.all_to_all(owner_delta, 'replica', split_axis=0, concat_axis=0, tiled...  3.59 us
  transfers between devices with their start and end apart: 6, of which 5 were waited for; matrix products, arithmetic and copies ran while one was open for 14% of the time, Pallas kernels for 0%

profile of v7, /device:TPU:0, one launch (start us, length us, event | category | flops | bytes accessed | tf_op | source)
XLA Modules:
  0.0 101.8 jit_solution(1866206097229301999)
XLA Ops:
  1.2 0.7 and_select_fusion.2
  2.5 0.7 copy.83
  4.8 1.3 %gather_fusion = s32[16]{0:T(128)S(1)} fusion(s32[16]{0:T(128)} %bitcast.63, s32[1024]{0:T(1024)S(1)} %pad_clamp_fusion.4), kind=kCustom, calls=%fused_computation | custom fusion | bytes 192 | tf_op jit(solution)/shard_map/gather | solution.py:184
  6.4 0.7 gather_fusion.1
  7.5 2.7 %collective-permute-start.1 = (bf16[32,4096]{1,0:T(8,128)(2,1)S(1)}, bf16[32,4096]{1,0:T(8,128)(2,1)S(1)}, u32[]{:S(2)}, u32[]{:S(2)}) collective-permute-start(bf16[32,4096]{1,0:T(8,128)(2,1)S(1)} %maximum_select_fusion.1), channel_id=1, source_target_pairs={{0,2},{1,3},{2,0},{3,1},{4,6},{5,7},{6,4},{7,5},{8,10},{9,11},{10,... | collective-permute-start | bytes 786440 | tf_op jit(solution)/shard_map/ppermute | solution.py:120
  10.3 0.7 gather_fusion.6
  11.1 6.0 %collective-permute-done.1 = bf16[32,4096]{1,0:T(8,128)(2,1)S(1)} collective-permute-done((bf16[32,4096]{1,0:T(8,128)(2,1)S(1)}, bf16[32,4096]{1,0:T(8,128)(2,1)S(1)}, u32[]{:S(2)}, u32[]{:S(2)}) %collective-permute-start.1) | collective-permute-done | bytes 262176 | tf_op jit(solution)/shard_map/ppermute | solution.py:120
  17.6 0.7 gather_fusion.2
  18.7 0.8 pad_maximum_fusion
  19.6 6.0 %all-to-all-start = ((bf16[8,2,4,2176]{3,2,1,0:T(4,128)(2,1)}), bf16[8,2,4,2176]{3,2,1,0:T(4,128)(2,1)S(1)}, u32[]{:S(2)}, u32[]{:S(2)}) async-start(bf16[8,2,4,2176]{3,2,1,0:T(4,128)(2,1)} %pad_maximum_fusion), calls=%async_computation | async-start | bytes 557056 | tf_op jit(solution)/shard_map/all_to_all | solution.py:194
  25.6 0.7 gather_fusion.5
  26.5 8.2 %all-to-all-done = bf16[8,2,4,2176]{3,2,1,0:T(4,128)(2,1)S(1)} async-done(((bf16[8,2,4,2176]{3,2,1,0:T(4,128)(2,1)}), bf16[8,2,4,2176]{3,2,1,0:T(4,128)(2,1)S(1)}, u32[]{:S(2)}, u32[]{:S(2)}) %all-to-all-start) | async-done | bytes 278560 | tf_op jit(solution)/shard_map/all_to_all | solution.py:194
  35.0 8.1 %gather_fusion.4 = bf16[16,2048,128]{2,1,0:T(8,128)(2,1)} fusion(bf16[16,2048,128]{2,1,0:T(8,128)(2,1)} %param.13, s32[1024]{0:T(1024)S(1)} %pad_clamp_fusion.2), kind=kCustom, calls=%fused_computation.4 | custom fusion | bytes 16777280 | tf_op jit(solution)/shard_map/gather | solution.py:197
  43.1 4.6 %fusion.7 = f32[8,2,4,128]{3,2,1,0:T(4,128)S(1)} fusion(bf16[8,2,2048,128]{3,2,1,0:T(8,128)(2,1)} %bitcast.64, bf16[8,2,4,2176]{3,2,1,0:T(4,128)(2,1)S(1)} %all-to-all-done), kind=kOutput, calls=%fused_computation.20 | convolution fusion | flops 33554432 | bytes 8683520 | tf_op jit(solution)/shard_map/oksd,okdr->oksr/dot_general | solution.py:199
  47.8 1.2 %collective-permute-done.2 = f32[8,2,4,128]{3,2,1,0:T(4,128)S(1)} collective-permute-done((f32[8,2,4,128]{3,2,1,0:T(4,128)S(1)}, f32[8,2,4,128]{3,2,1,0:T(4,128)S(1)}, u32[]{:S(2)}, u32[]{:S(2)}) %collective-permute-start.2) | collective-permute-done | bytes 32800 | tf_op jit(solution)/shard_map/ppermute | solution.py:107
  49.0 1.6 %collective-permute-start.3 = (f32[8,2,4,128]{3,2,1,0:T(4,128)S(1)}, f32[8,2,4,128]{3,2,1,0:T(4,128)S(1)}, u32[]{:S(2)}, u32[]{:S(2)}) collective-permute-start(f32[8,2,4,128]{3,2,1,0:T(4,128)S(1)} %add.146), channel_id=1, source_target_pairs={{0,2},{1,3},{2,0},{3,1},{4,6},{5,7},{6,4},{7,5},{8,10},{9,11},{10,... | collective-permute-start | bytes 98312 | tf_op jit(solution)/shard_map/ppermute | solution.py:107
  51.9 1.1 %collective-permute-done.3 = f32[8,2,4,128]{3,2,1,0:T(4,128)S(1)} collective-permute-done((f32[8,2,4,128]{3,2,1,0:T(4,128)S(1)}, f32[8,2,4,128]{3,2,1,0:T(4,128)S(1)}, u32[]{:S(2)}, u32[]{:S(2)}) %collective-permute-start.3) | collective-permute-done | bytes 32800 | tf_op jit(solution)/shard_map/ppermute | solution.py:107
  53.1 0.9 fusion.2
  54.0 3.6 %all-to-all-start.1 = ((f32[8,2,4,2,256]{4,2,3,1,0:T(4,128)}), f32[8,2,4,2,256]{4,2,3,1,0:T(4,128)S(1)}, u32[]{:S(2)}, u32[]{:S(2)}) async-start(f32[8,2,4,2,256]{4,2,3,1,0:T(4,128)} %fusion.2), calls=%async_computation.1 | async-start | bytes 262144 | tf_op jit(solution)/shard_map/all_to_all | solution.py:208
  57.6 4.9 %fusion = f32[32,2,256]{2,0,1:T(8,128)S(1)} fusion(bf16[8192,2,256]{2,1,0:T(2,128)(2,1)} %param.12, bf16[32,8192]{1,0:T(8,128)(2,1)S(1)} %fusion.5), kind=kOutput, calls=%fused_computation.8 | convolution fusion | flops 268435456 | bytes 8978432 | tf_op jit(solution)/shard_map/jd,dcw->jcw/dot_general | solution.py:211
  62.6 2.4 %all-to-all-done.1 = f32[8,2,4,2,256]{4,2,3,1,0:T(4,128)S(1)} async-done(((f32[8,2,4,2,256]{4,2,3,1,0:T(4,128)}), f32[8,2,4,2,256]{4,2,3,1,0:T(4,128)S(1)}, u32[]{:S(2)}, u32[]{:S(2)}) %all-to-all-start.1) | async-done | bytes 131104 | tf_op jit(solution)/shard_map/all_to_all | solution.py:208
  66.1 0.7 pad_maximum_fusion.1.nkv_ref
  66.7 33.4 %shard_map.113 = bf16[32,16,128]{2,1,0:T(8,128)(2,1)} custom-call(s32[32]{0:T(128)} %len_ref.1, bf16[32,16,128]{2,1,0:T(8,128)(2,1)} %bitcast.66, bf16[32,512,2,256]{3,2,1,0:T(2,128)(2,1)} %kv_ref.1, bf16[32,2,256]{2,1,0:T(2,128)(2,1)} %pad_maximum_fusion.1.nkv_ref), custom_call_target="tpu_custom_call" | custom-call | tf_op jit(solution)/shard_map/pallas_call | solution.py:83
  100.2 1.6 %copy.100 = bf16[4,8,16,128]{3,1,2,0:T(8,128)(2,1)} copy(bf16[4,8,16,128]{3,2,1,0:T(8,128)(2,1)} %bitcast.67) | data formatting | bytes 262144
  (73 shorter events, 7.4 us)
Async XLA Ops:
  0.6 50.7 %copy-start = (bf16[16,2,64,256]{3,2,1,0:T(8,128)(2,1)S(1)}, bf16[16,2,64,256]{3,2,1,0:T(8,128)(2,1)}, u32[]{:S(2)}) copy-start(bf16[16,2,64,256]{3,2,1,0:T(8,128)(2,1)} %param.14) | copy-start | bytes 3145732
  0.6 6.8 %copy-start.1 = (bf16[32,2048]{1,0:T(8,128)(2,1)S(1)}, bf16[32,2048]{1,0:T(8,128)(2,1)}, u32[]{:S(2)}) copy-start(bf16[32,2048]{1,0:T(8,128)(2,1)} %param.10) | copy-start | bytes 393220
  0.7 16.7 %copy-start.3 = (f32[8192]{0:T(1024)S(1)}, f32[8192]{0:T(1024)}, u32[]{:S(2)}) copy-start(f32[8192]{0:T(1024)} %param.11) | copy-start | bytes 98308
  0.7 25.7 %copy-start.4 = (s32[32]{0:T(128)S(1)}, s32[32]{0:T(128)}, u32[]{:S(2)}) copy-start(s32[32]{0:T(128)} %len_ref.1) | copy-start | bytes 388
  0.7 6.7 %collective-permute-start = (bf16[32,2048]{1,0:T(8,128)(2,1)}, bf16[32,2048]{1,0:T(8,128)(2,1)S(1)}, u32[]{:S(2)}, u32[]{:S(2)}) collective-permute-start(bf16[32,2048]{1,0:T(8,128)(2,1)} %param.10), channel_id=1, source_target_pairs={{0,1},{1,0},{2,3},{3,2},{4,5},{5,4},{6,7},{7,6},{8,9},{9,8},{10,11... | collective-permute-start | bytes 393224 | tf_op jit(solution)/shard_map/ppermute | solution.py:120
  7.5 9.6 %collective-permute-start.1 = (bf16[32,4096]{1,0:T(8,128)(2,1)S(1)}, bf16[32,4096]{1,0:T(8,128)(2,1)S(1)}, u32[]{:S(2)}, u32[]{:S(2)}) collective-permute-start(bf16[32,4096]{1,0:T(8,128)(2,1)S(1)} %maximum_select_fusion.1), channel_id=1, source_target_pairs={{0,2},{1,3},{2,0},{3,1},{4,6},{5,7},{6,4},{7,5},{8,10},{9,11},{10,... | collective-permute-start | bytes 786440 | tf_op jit(solution)/shard_map/ppermute | solution.py:120
  19.6 15.1 %all-to-all-start = ((bf16[8,2,4,2176]{3,2,1,0:T(4,128)(2,1)}), bf16[8,2,4,2176]{3,2,1,0:T(4,128)(2,1)S(1)}, u32[]{:S(2)}, u32[]{:S(2)}) async-start(bf16[8,2,4,2176]{3,2,1,0:T(4,128)(2,1)} %pad_maximum_fusion), calls=%async_computation | async-start | bytes 557056 | tf_op jit(solution)/shard_map/all_to_all | solution.py:194
  43.1 7.5 %copy-start.2 = (bf16[32,2048]{1,0:T(8,128)(2,1)S(1)}, bf16[32,2048]{1,0:T(8,128)(2,1)}, u32[]{:S(2)}) copy-start(bf16[32,2048]{1,0:T(8,128)(2,1)} %param.15) | copy-start | bytes 393220
  47.8 1.3 %collective-permute-start.2 = (f32[8,2,4,128]{3,2,1,0:T(4,128)S(1)}, f32[8,2,4,128]{3,2,1,0:T(4,128)S(1)}, u32[]{:S(2)}, u32[]{:S(2)}) collective-permute-start(f32[8,2,4,128]{3,2,1,0:T(4,128)S(1)} %fusion.7), channel_id=1, source_target_pairs={{0,1},{1,0},{2,3},{3,2},{4,5},{5,4},{6,7},{7,6},{8,9},{9,8},{10,11... | collective-permute-start | bytes 98312 | tf_op jit(solution)/shard_map/ppermute | solution.py:107
  49.0 4.0 %collective-permute-start.3 = (f32[8,2,4,128]{3,2,1,0:T(4,128)S(1)}, f32[8,2,4,128]{3,2,1,0:T(4,128)S(1)}, u32[]{:S(2)}, u32[]{:S(2)}) collective-permute-start(f32[8,2,4,128]{3,2,1,0:T(4,128)S(1)} %add.146), channel_id=1, source_target_pairs={{0,2},{1,3},{2,0},{3,1},{4,6},{5,7},{6,4},{7,5},{8,10},{9,11},{10,... | collective-permute-start | bytes 98312 | tf_op jit(solution)/shard_map/ppermute | solution.py:107
  54.0 10.9 %all-to-all-start.1 = ((f32[8,2,4,2,256]{4,2,3,1,0:T(4,128)}), f32[8,2,4,2,256]{4,2,3,1,0:T(4,128)S(1)}, u32[]{:S(2)}, u32[]{:S(2)}) async-start(f32[8,2,4,2,256]{4,2,3,1,0:T(4,128)} %fusion.2), calls=%async_computation.1 | async-start | bytes 262144 | tf_op jit(solution)/shard_map/all_to_all | solution.py:208

commit v8 on v6

--- a/solution.py
+++ b/solution.py
@@ -109,6 +109,31 @@
     return value
 
 
+def down_kernel(ids_ref, rows_ref, down_ref, out_ref):
+    out_ref[0] = jnp.dot(rows_ref[0], down_ref[0], preferred_element_type=jnp.float32)
+
+
+def down_project(rows, ids, adapter_down):
+    lead = ids.shape
+    slots = ids.size
+    slot_len, width = rows.shape[-2:]
+    rank2 = adapter_down.shape[2]
+    out = pl.pallas_call(
+        down_kernel,
+        out_shape=jax.ShapeDtypeStruct((slots, slot_len, rank2), jnp.float32),
+        grid_spec=pltpu.PrefetchScalarGridSpec(
+            num_scalar_prefetch=1,
+            grid=(slots,),
+            in_specs=[
+                pl.BlockSpec((1, slot_len, width), lambda s, ids: (s, 0, 0)),
+                pl.BlockSpec((1, width, rank2), lambda s, ids: (ids[s], 0, 0)),
+            ],
+            out_specs=pl.BlockSpec((1, slot_len, rank2), lambda s, ids: (s, 0, 0)),
+        ),
+    )(ids.reshape(slots), rows.reshape(slots, slot_len, width), adapter_down)
+    return out.reshape(lead + (slot_len, rank2))
+
+
 def body(
     hidden,
     input_norm_gain,
@@ -176,11 +201,9 @@
     got = lax.all_to_all(payload, "replica", split_axis=0, concat_axis=0, tiled=True)
     got_rows = got[..., :part_width]
     got_ids = got[:, :, 0, part_width].astype(jnp.int32)
-    selected_down = adapter_down[got_ids]
+    got_ids = jnp.clip(got_ids, 0, adapter_down.shape[0] - 1)
     selected_up = adapter_up[got_ids]
-    partial_value = jnp.einsum(
-        "oksd,okdr->oksr", got_rows, selected_down, preferred_element_type=jnp.float32
-    )
+    partial_value = down_project(got_rows, got_ids, adapter_down)
     summed = butterfly_sum(partial_value, "tensor").astype(jnp.bfloat16)
     summed = summed.reshape(summed.shape[:3] + (2, adapter_rank_size))
     owner_delta = (

time: 101 us -> 104 us (1.030)
  Pallas kernels: 33.4 us -> 45.5 us
  local copies, waits for them, and re-layouts: 17.9 us -> 12.6 us
  matrix products: 10.5 us -> 5.86 us
    pallas_call x0 -> x1, Pallas kernels: none -> 12.1 us  [down_project(): pl.pallas_call(down_kernel, out_shape=jax.ShapeDtypeStruct((slots, slot_l...]
    gather x1 -> x0, local copies, waits for them, and re-layouts: 8.15 us -> none  [body(): selected_down = adapter_down[got_ids]]
    dot_general x1 -> x0, matrix products: 4.6 us -> none  [body(): jnp.einsum('oksd,okdr->oksr', got_rows, selected_down, preferred_element_...]
    unnamed x13 -> x12, local copies, waits for them, and re-layouts: 2.37 us -> 2.28 us
where the time goes in v8:
time: 104 us; the launch traced here: 103 us
  Pallas kernels  45.5 us (44%)
  waiting for transfers between devices  12.9 us (12%)
  local copies, waits for them, and re-layouts  12.6 us (12%)
  starting transfers between devices  10.6 us (10%)
  blocking collectives  8.65 us (8%)
  other arithmetic  5.89 us (6%)
  matrix products  5.86 us (6%)
    pallas_call x1, Pallas kernels, attend(): pl.pallas_call(kernel, out_shape=jax.ShapeDtypeStruct((row_count, heads,...  33.4 us
    pallas_call x1, Pallas kernels, down_project(): pl.pallas_call(down_kernel, out_shape=jax.ShapeDtypeStruct((slots, slot_l...  12.1 us
    all_gather x1, blocking collectives, body(): gathered = lax.all_gather(hidden, 'tensor', axis=1, tiled=True)  8.65 us
    all_to_all x1, waiting for transfers between devices, body(): lax.all_to_all(owner_delta, 'replica', split_axis=0, concat_axis=0, tiled...  6.5 us
    all_to_all x1, starting transfers between devices, body(): lax.all_to_all(payload, 'replica', split_axis=0, concat_axis=0, tiled=True)  5.81 us
    dot_general x1, matrix products, body(): jnp.einsum('jd,dcw->jcw', normed, key_value_weight, preferred_element_typ...  4.95 us
    all_to_all x1, starting transfers between devices, body(): lax.all_to_all(owner_delta, 'replica', split_axis=0, concat_axis=0, tiled...  3.64 us
    all_to_all x1, waiting for transfers between devices, body(): lax.all_to_all(payload, 'replica', split_axis=0, concat_axis=0, tiled=True)  3.23 us
  transfers between devices with their start and end apart: 4, of which 4 were waited for; matrix products, arithmetic and copies ran while one was open for 8% of the time, Pallas kernels for 0%

profile of v8, /device:TPU:0, one launch (start us, length us, event | category | flops | bytes accessed | tf_op | source)
XLA Modules:
  0.0 103.0 jit_solution(5552935023088655894)
XLA Ops:
  0.7 0.8 fusion.15
  2.8 1.3 %gather_fusion = s32[16]{0:T(128)S(1)} fusion(s32[16]{0:T(128)} %bitcast.65, s32[1024]{0:T(1024)S(1)} %pad_clamp_fusion.4), kind=kCustom, calls=%fused_computation | custom fusion | bytes 192 | tf_op jit(solution)/shard_map/gather | solution.py:191
  4.4 0.7 copy.51
  6.9 8.6 %all_gather.3 = bf16[32,8192]{1,0:T(8,128)(2,1)S(1)} all-gather(bf16[32,2048]{1,0:T(8,128)(2,1)S(1)} %copy-done.1), channel_id=1, replica_groups=mesh['replica'=8,'tensor'=4] {'tensor'}, dimensions={1}, use_global_device_ids=true | all-gather | bytes 655360 | tf_op jit(solution)/shard_map/all_gather | solution.py:157
  16.0 0.7 gather_fusion.2
  17.1 0.8 copy.53
  18.0 5.8 %all-to-all-start = ((bf16[8,2,4,2176]{3,2,1,0:T(4,128)(2,1)}), bf16[8,2,4,2176]{3,2,1,0:T(4,128)(2,1)S(1)}, u32[]{:S(2)}, u32[]{:S(2)}) async-start(bf16[8,2,4,2176]{3,2,1,0:T(4,128)(2,1)} %copy.53), calls=%async_computation | async-start | bytes 557056 | tf_op jit(solution)/shard_map/all_to_all | solution.py:201
  23.9 0.7 gather_fusion.5
  24.6 0.7 gather_fusion.4
  25.3 4.9 %fusion = f32[32,2,256]{2,0,1:T(8,128)S(1)} fusion(bf16[8192,2,256]{2,1,0:T(2,128)(2,1)} %param.12, bf16[32,8192]{1,0:T(8,128)(2,1)S(1)} %fusion.5), kind=kOutput, calls=%fused_computation.7 | convolution fusion | flops 268435456 | bytes 8978432 | tf_op jit(solution)/shard_map/jd,dcw->jcw/dot_general | solution.py:216
  30.3 3.2 %all-to-all-done = bf16[8,2,4,2176]{3,2,1,0:T(4,128)(2,1)S(1)} async-done(((bf16[8,2,4,2176]{3,2,1,0:T(4,128)(2,1)}), bf16[8,2,4,2176]{3,2,1,0:T(4,128)(2,1)S(1)}, u32[]{:S(2)}, u32[]{:S(2)}) %all-to-all-start) | async-done | bytes 278560 | tf_op jit(solution)/shard_map/all_to_all | solution.py:201
  34.6 0.8 slice.40
  35.4 12.1 %shard_map.113 = f32[16,4,128]{2,1,0:T(4,128)} custom-call(s32[16]{0:T(128)} %min.15.ids_ref, bf16[16,4,2048]{2,1,0:T(4,128)(2,1)} %bitcast.68, bf16[16,2048,128]{2,1,0:T(8,128)(2,1)} %down_ref.1), custom_call_target="tpu_custom_call" | custom-call | tf_op jit(solution)/shard_map/pallas_call | solution.py:121
  47.5 0.8 copy.57
  48.4 1.0 collective-permute-done
  49.4 0.8 copy_add_fusion.1
  50.2 1.2 %collective-permute-start.1 = (f32[8,2,4,128]{3,0,2,1:T(8,128)S(1)}, f32[8,2,4,128]{3,0,2,1:T(8,128)S(1)}, u32[]{:S(2)}, u32[]{:S(2)}) collective-permute-start(f32[8,2,4,128]{3,0,2,1:T(8,128)S(1)} %copy_add_fusion.1), channel_id=1, source_target_pairs={{0,2},{1,3},{2,0},{3,1},{4,6},{5,7},{6,4},{7,5},{8,10},{9,11},{10,... | collective-permute-start | bytes 98312 | tf_op jit(solution)/shard_map/ppermute | solution.py:107
  52.0 2.2 %collective-permute-done.1 = f32[8,2,4,128]{3,0,2,1:T(8,128)S(1)} collective-permute-done((f32[8,2,4,128]{3,0,2,1:T(8,128)S(1)}, f32[8,2,4,128]{3,0,2,1:T(8,128)S(1)}, u32[]{:S(2)}, u32[]{:S(2)}) %collective-permute-start.1) | collective-permute-done | bytes 32800 | tf_op jit(solution)/shard_map/ppermute | solution.py:107
  54.3 0.9 fusion.2
  55.2 3.6 %all-to-all-start.1 = ((f32[8,2,4,2,256]{4,2,3,1,0:T(4,128)}), f32[8,2,4,2,256]{4,2,3,1,0:T(4,128)S(1)}, u32[]{:S(2)}, u32[]{:S(2)}) async-start(f32[8,2,4,2,256]{4,2,3,1,0:T(4,128)} %fusion.2), calls=%async_computation.1 | async-start | bytes 262144 | tf_op jit(solution)/shard_map/all_to_all | solution.py:213
  59.7 6.5 %all-to-all-done.1 = f32[8,2,4,2,256]{4,2,3,1,0:T(4,128)S(1)} async-done(((f32[8,2,4,2,256]{4,2,3,1,0:T(4,128)}), f32[8,2,4,2,256]{4,2,3,1,0:T(4,128)S(1)}, u32[]{:S(2)}, u32[]{:S(2)}) %all-to-all-start.1) | async-done | bytes 131104 | tf_op jit(solution)/shard_map/all_to_all | solution.py:213
  67.3 0.7 pad_maximum_fusion.1.nkv_ref
  68.0 33.4 %shard_map.114 = bf16[32,16,128]{2,1,0:T(8,128)(2,1)} custom-call(s32[32]{0:T(128)} %len_ref.1, bf16[32,16,128]{2,1,0:T(8,128)(2,1)} %bitcast.69, bf16[32,512,2,256]{3,2,1,0:T(2,128)(2,1)} %kv_ref.1, bf16[32,2,256]{2,1,0:T(2,128)(2,1)} %pad_maximum_fusion.1.nkv_ref), custom_call_target="tpu_custom_call" | custom-call | tf_op jit(solution)/shard_map/pallas_call | solution.py:83
  101.4 1.6 %copy.72 = bf16[4,8,16,128]{3,1,2,0:T(8,128)(2,1)} copy(bf16[4,8,16,128]{3,2,1,0:T(8,128)(2,1)} %bitcast.70) | data formatting | bytes 262144
  (71 shorter events, 8.1 us)
Async XLA Ops:
  0.6 50.7 %copy-start = (bf16[16,2,64,256]{3,2,1,0:T(8,128)(2,1)S(1)}, bf16[16,2,64,256]{3,2,1,0:T(8,128)(2,1)}, u32[]{:S(2)}) copy-start(bf16[16,2,64,256]{3,2,1,0:T(8,128)(2,1)} %param.14) | copy-start | bytes 3145732
  0.6 6.2 %copy-start.1 = (bf16[32,2048]{1,0:T(8,128)(2,1)S(1)}, bf16[32,2048]{1,0:T(8,128)(2,1)}, u32[]{:S(2)}) copy-start(bf16[32,2048]{1,0:T(8,128)(2,1)} %param.10) | copy-start | bytes 393220
  0.7 15.1 %copy-start.3 = (f32[8192]{0:T(1024)S(1)}, f32[8192]{0:T(1024)}, u32[]{:S(2)}) copy-start(f32[8192]{0:T(1024)} %param.11) | copy-start | bytes 98308
  18.0 15.5 %all-to-all-start = ((bf16[8,2,4,2176]{3,2,1,0:T(4,128)(2,1)}), bf16[8,2,4,2176]{3,2,1,0:T(4,128)(2,1)S(1)}, u32[]{:S(2)}, u32[]{:S(2)}) async-start(bf16[8,2,4,2176]{3,2,1,0:T(4,128)(2,1)} %copy.53), calls=%async_computation | async-start | bytes 557056 | tf_op jit(solution)/shard_map/all_to_all | solution.py:201
  30.2 28.6 %copy-start.4 = (s32[32]{0:T(128)S(1)}, s32[32]{0:T(128)}, u32[]{:S(2)}) copy-start(s32[32]{0:T(128)} %len_ref.1) | copy-start | bytes 388
  30.2 28.6 %copy-start.2 = (bf16[32,2048]{1,0:T(8,128)(2,1)S(1)}, bf16[32,2048]{1,0:T(8,128)(2,1)}, u32[]{:S(2)}) copy-start(bf16[32,2048]{1,0:T(8,128)(2,1)} %param.15) | copy-start | bytes 393220
  48.2 1.2 %collective-permute-start = (f32[8,2,4,128]{3,0,2,1:T(8,128)S(1)}, f32[8,2,4,128]{3,0,2,1:T(8,128)S(1)}, u32[]{:S(2)}, u32[]{:S(2)}) collective-permute-start(f32[8,2,4,128]{3,0,2,1:T(8,128)S(1)} %copy.57), channel_id=1, source_target_pairs={{0,1},{1,0},{2,3},{3,2},{4,5},{5,4},{6,7},{7,6},{8,9},{9,8},{10,11... | collective-permute-start | bytes 98312 | tf_op jit(solution)/shard_map/ppermute | solution.py:107
  50.2 4.0 %collective-permute-start.1 = (f32[8,2,4,128]{3,0,2,1:T(8,128)S(1)}, f32[8,2,4,128]{3,0,2,1:T(8,128)S(1)}, u32[]{:S(2)}, u32[]{:S(2)}) collective-permute-start(f32[8,2,4,128]{3,0,2,1:T(8,128)S(1)} %copy_add_fusion.1), channel_id=1, source_target_pairs={{0,2},{1,3},{2,0},{3,1},{4,6},{5,7},{6,4},{7,5},{8,10},{9,11},{10,... | collective-permute-start | bytes 98312 | tf_op jit(solution)/shard_map/ppermute | solution.py:107
  55.2 11.0 %all-to-all-start.1 = ((f32[8,2,4,2,256]{4,2,3,1,0:T(4,128)}), f32[8,2,4,2,256]{4,2,3,1,0:T(4,128)S(1)}, u32[]{:S(2)}, u32[]{:S(2)}) async-start(f32[8,2,4,2,256]{4,2,3,1,0:T(4,128)} %fusion.2), calls=%async_computation.1 | async-start | bytes 262144 | tf_op jit(solution)/shard_map/all_to_all | solution.py:213

commit v9 on v6

--- a/solution.py
+++ b/solution.py
@@ -37,7 +37,7 @@
     )
 
 
-def attention_kernel(len_ref, q_ref, kv_ref, nkv_ref, o_ref, *, rows, kv_local, group_size):
+def score_kernel(len_ref, q_ref, kv_ref, s_ref, *, rows, kv_local, group_size):
     scale = float(HEAD) ** (-0.5)
     step = pl.program_id(0)
     cache_len = kv_ref.shape[1]
@@ -50,12 +50,24 @@
         for h in range(kv_local):
             cols = slice(h * HEAD, (h + 1) * HEAD)
             qrows = slice(h * group_size, (h + 1) * group_size)
+            scores = lax.dot_general(
+                q_ref[i, qrows, :], stacked[:, cols], (((1,), (1,)), ((), ())),
+                preferred_element_type=jnp.float32,
+            ) * scale
+            s_ref[i, qrows, :] = jnp.where(live, scores, -jnp.inf)
+
+
+def mix_kernel(q_ref, s_ref, kv_ref, nkv_ref, o_ref, *, rows, kv_local, group_size):
+    scale = float(HEAD) ** (-0.5)
+    cache_len = kv_ref.shape[1]
+    width = kv_ref.shape[3]
+    for i in range(rows):
+        stacked = kv_ref[i].reshape(2 * cache_len, width)
+        for h in range(kv_local):
+            cols = slice(h * HEAD, (h + 1) * HEAD)
+            qrows = slice(h * group_size, (h + 1) * group_size)
             q = q_ref[i, qrows, :]
-            block = stacked[:, cols]
-            scores = lax.dot_general(
-                q, block, (((1,), (1,)), ((), ())), preferred_element_type=jnp.float32
-            ) * scale
-            scores = jnp.where(live, scores, -jnp.inf)
+            scores = s_ref[i, qrows, :]
             new_key = nkv_ref[i, 0:1, cols].astype(jnp.float32)
             new_value = nkv_ref[i, 1:2, cols].astype(jnp.float32)
             own = jnp.sum(q.astype(jnp.float32) * new_key, axis=1, keepdims=True) * scale
@@ -65,7 +77,7 @@
             total = jnp.sum(weights, axis=1, keepdims=True) + own_weight
             probs = pltpu.roll(weights / total, 1, 1).astype(jnp.bfloat16)
             own_prob = (own_weight / total).astype(jnp.bfloat16).astype(jnp.float32)
-            context = jnp.dot(probs, block, preferred_element_type=jnp.float32)
+            context = jnp.dot(probs, stacked[:, cols], preferred_element_type=jnp.float32)
             context = context + own_prob * new_value
             o_ref[i, qrows, :] = context.astype(o_ref.dtype)
 
@@ -77,23 +89,32 @@
     heads = kv_local * group_size
     rows = 4
     query_heads = query.reshape(row_count, heads, HEAD)
-    kernel = functools.partial(
-        attention_kernel, rows=rows, kv_local=kv_local, group_size=group_size
-    )
-    out = pl.pallas_call(
-        kernel,
-        out_shape=jax.ShapeDtypeStruct((row_count, heads, HEAD), jnp.bfloat16),
+    opts = dict(rows=rows, kv_local=kv_local, group_size=group_size)
+    cache_spec = pl.BlockSpec((rows, cache_len, 2, width), lambda b, *_: (b, 0, 0, 0))
+    head_spec = pl.BlockSpec((rows, heads, HEAD), lambda b, *_: (b, 0, 0))
+    score_spec = pl.BlockSpec((rows, heads, 2 * cache_len), lambda b, *_: (b, 0, 0))
+    scores = pl.pallas_call(
+        functools.partial(score_kernel, **opts),
+        out_shape=jax.ShapeDtypeStruct((row_count, heads, 2 * cache_len), jnp.float32),
         grid_spec=pltpu.PrefetchScalarGridSpec(
             num_scalar_prefetch=1,
             grid=(row_count // rows,),
-            in_specs=[
-                pl.BlockSpec((rows, heads, HEAD), lambda b, lens: (b, 0, 0)),
-                pl.BlockSpec((rows, cache_len, 2, width), lambda b, lens: (b, 0, 0, 0)),
-                pl.BlockSpec((rows, 2, width), lambda b, lens: (b, 0, 0)),
-            ],
-            out_specs=pl.BlockSpec((rows, heads, HEAD), lambda b, lens: (b, 0, 0)),
+            in_specs=[head_spec, cache_spec],
+            out_specs=score_spec,
         ),
-    )(cached_length, query_heads, key_value_cache, new_kv)
+    )(cached_length, query_heads, key_value_cache)
+    out = pl.pallas_call(
+        functools.partial(mix_kernel, **opts),
+        out_shape=jax.ShapeDtypeStruct((row_count, heads, HEAD), jnp.bfloat16),
+        grid=(row_count // rows,),
+        in_specs=[
+            head_spec,
+            score_spec,
+            cache_spec,
+            pl.BlockSpec((rows, 2, width), lambda b: (b, 0, 0)),
+        ],
+        out_specs=head_spec,
+    )(query_heads, scores, key_value_cache, new_kv)
     return out.reshape(row_count, heads * HEAD)
 
 

time: 101 us -> 87.5 us (0.87)
  Pallas kernels: 33.4 us -> 25.9 us
  waiting for transfers between devices: 13.1 us -> 6.64 us
    pallas_call x1 -> x2, Pallas kernels: 33.4 us -> 25.9 us  [the longest x1 13.1 us: attend(): pl.pallas_call(functools.partial(mix_kernel, **opts), out_shape=jax.Shape...]
    all_to_all x1, waiting for transfers between devices: 6.5 us -> 0.01 us  [body(): lax.all_to_all(owner_delta, 'replica', split_axis=0, concat_axis=0, tiled...]
  transfers between devices with their start and end apart: 4 -> 4, of which waited for: 4 -> 3; matrix products, arithmetic and copies ran while one was open for 8% -> 9% of each run, Pallas kernels for 0% -> 15%
where the time goes in v9:
time: 87.5 us; the launch traced here: 86.8 us
  Pallas kernels  25.9 us (30%)
  local copies, waits for them, and re-layouts  17.9 us (20%)
  starting transfers between devices  10.7 us (12%)
  matrix products  10.5 us (12%)
  blocking collectives  8.65 us (10%)
  waiting for transfers between devices  6.64 us (8%)
  other arithmetic  5.66 us (6%)
  between operations  0.9 us (1%)
    pallas_call x1, Pallas kernels, attend(): pl.pallas_call(functools.partial(mix_kernel, **opts), out_shape=jax.Shape...  13.1 us
    pallas_call x1, Pallas kernels, attend(): pl.pallas_call(functools.partial(score_kernel, **opts), out_shape=jax.Sha...  12.8 us
    all_gather x1, blocking collectives, body(): gathered = lax.all_gather(hidden, 'tensor', axis=1, tiled=True)  8.65 us
    gather x1, local copies, waits for them, and re-layouts, body(): selected_down = adapter_down[got_ids]  8.15 us
    all_to_all x1, starting transfers between devices, body(): lax.all_to_all(payload, 'replica', split_axis=0, concat_axis=0, tiled=True)  5.81 us
    dot_general x1, matrix products, body(): jnp.einsum('jd,dcw->jcw', normed, key_value_weight, preferred_element_typ...  4.94 us
    dot_general x1, matrix products, body(): jnp.einsum('oksd,okdr->oksr', got_rows, selected_down, preferred_element_...  4.6 us
    all_to_all x1, starting transfers between devices, body(): lax.all_to_all(owner_delta, 'replica', split_axis=0, concat_axis=0, tiled...  3.64 us
  transfers between devices with their start and end apart: 4, of which 3 were waited for; matrix products, arithmetic and copies ran while one was open for 9% of the time, Pallas kernels for 15%

profile of v9, /device:TPU:0, one launch (start us, length us, event | category | flops | bytes accessed | tf_op | source)
XLA Modules:
  0.0 86.8 jit_solution(1233629708350165749)
XLA Ops:
  0.7 0.8 and_select_fusion.2
  1.4 0.7 fusion.16
  2.8 1.3 %gather_fusion = s32[16]{0:T(128)S(1)} fusion(s32[16]{0:T(128)} %bitcast.62, s32[1024]{0:T(1024)S(1)} %pad_clamp_fusion.4), kind=kCustom, calls=%fused_computation | custom fusion | bytes 192 | tf_op jit(solution)/shard_map/gather | solution.py:187
  4.4 0.7 copy.83
  7.0 8.6 %all_gather.3 = bf16[32,8192]{1,0:T(8,128)(2,1)S(1)} all-gather(bf16[32,2048]{1,0:T(8,128)(2,1)S(1)} %copy-done.1), channel_id=1, replica_groups=mesh['replica'=8,'tensor'=4] {'tensor'}, dimensions={1}, use_global_device_ids=true | all-gather | bytes 655360 | tf_op jit(solution)/shard_map/all_gather | solution.py:153
  16.1 0.7 gather_fusion.2
  17.3 0.8 pad_maximum_fusion
  18.2 5.8 %all-to-all-start = ((bf16[8,2,4,2176]{3,2,1,0:T(4,128)(2,1)}), bf16[8,2,4,2176]{3,2,1,0:T(4,128)(2,1)S(1)}, u32[]{:S(2)}, u32[]{:S(2)}) async-start(bf16[8,2,4,2176]{3,2,1,0:T(4,128)(2,1)} %pad_maximum_fusion), calls=%async_computation | async-start | bytes 557056 | tf_op jit(solution)/shard_map/all_to_all | solution.py:197
  24.1 0.7 gather_fusion.6
  24.8 0.7 gather_fusion.5
  25.5 4.9 %fusion = f32[32,2,256]{2,0,1:T(8,128)S(1)} fusion(bf16[8192,2,256]{2,1,0:T(2,128)(2,1)} %param.12, bf16[32,8192]{1,0:T(8,128)(2,1)S(1)} %fusion.5), kind=kOutput, calls=%fused_computation.8 | convolution fusion | flops 268435456 | bytes 8978432 | tf_op jit(solution)/shard_map/jd,dcw->jcw/dot_general | solution.py:214
  30.4 3.3 %all-to-all-done = bf16[8,2,4,2176]{3,2,1,0:T(4,128)(2,1)S(1)} async-done(((bf16[8,2,4,2176]{3,2,1,0:T(4,128)(2,1)}), bf16[8,2,4,2176]{3,2,1,0:T(4,128)(2,1)S(1)}, u32[]{:S(2)}, u32[]{:S(2)}) %all-to-all-start) | async-done | bytes 278560 | tf_op jit(solution)/shard_map/all_to_all | solution.py:197
  34.0 8.1 %gather_fusion.4 = bf16[16,2048,128]{2,1,0:T(8,128)(2,1)} fusion(bf16[16,2048,128]{2,1,0:T(8,128)(2,1)} %param.13, s32[1024]{0:T(1024)S(1)} %pad_clamp_fusion.2), kind=kCustom, calls=%fused_computation.4 | custom fusion | bytes 16777280 | tf_op jit(solution)/shard_map/gather | solution.py:200
  42.1 4.6 %fusion.7 = f32[8,2,4,128]{3,2,1,0:T(4,128)S(1)} fusion(bf16[8,2,2048,128]{3,2,1,0:T(8,128)(2,1)} %bitcast.64, bf16[8,2,4,2176]{3,2,1,0:T(4,128)(2,1)S(1)} %all-to-all-done), kind=kOutput, calls=%fused_computation.19 | convolution fusion | flops 33554432 | bytes 8683520 | tf_op jit(solution)/shard_map/oksd,okdr->oksr/dot_general | solution.py:202
  46.8 1.2 %collective-permute-done = f32[8,2,4,128]{3,2,1,0:T(4,128)S(1)} collective-permute-done((f32[8,2,4,128]{3,2,1,0:T(4,128)S(1)}, f32[8,2,4,128]{3,2,1,0:T(4,128)S(1)}, u32[]{:S(2)}, u32[]{:S(2)}) %collective-permute-start) | collective-permute-done | bytes 32800 | tf_op jit(solution)/shard_map/ppermute | solution.py:128
  48.0 1.2 %collective-permute-start.1 = (f32[8,2,4,128]{3,2,1,0:T(4,128)S(1)}, f32[8,2,4,128]{3,2,1,0:T(4,128)S(1)}, u32[]{:S(2)}, u32[]{:S(2)}) collective-permute-start(f32[8,2,4,128]{3,2,1,0:T(4,128)S(1)} %add.146), channel_id=1, source_target_pairs={{0,2},{1,3},{2,0},{3,1},{4,6},{5,7},{6,4},{7,5},{8,10},{9,11},{10,... | collective-permute-start | bytes 98312 | tf_op jit(solution)/shard_map/ppermute | solution.py:128
  49.8 2.2 %collective-permute-done.1 = f32[8,2,4,128]{3,2,1,0:T(4,128)S(1)} collective-permute-done((f32[8,2,4,128]{3,2,1,0:T(4,128)S(1)}, f32[8,2,4,128]{3,2,1,0:T(4,128)S(1)}, u32[]{:S(2)}, u32[]{:S(2)}) %collective-permute-start.1) | collective-permute-done | bytes 32800 | tf_op jit(solution)/shard_map/ppermute | solution.py:128
  52.1 0.9 %fusion.2 = f32[8,2,4,2,256]{4,2,3,1,0:T(4,128)} fusion(bf16[8,2,2,64,256]{4,3,2,1,0:T(8,128)(2,1)S(1)} %bitcast.65, bf16[8,2,4,2,64]{4,3,2,1,0:T(2,128)(2,1)S(1)} %reshape.340), kind=kOutput, calls=%fused_computation.13 | convolution fusion | flops 4227072 | bytes 1196032 | tf_op jit(solution)/shard_map/okscr,okcrw->okscw/dot_general | solution.py:208
  53.0 3.6 %all-to-all-start.1 = ((f32[8,2,4,2,256]{4,2,3,1,0:T(4,128)}), f32[8,2,4,2,256]{4,2,3,1,0:T(4,128)S(1)}, u32[]{:S(2)}, u32[]{:S(2)}) async-start(f32[8,2,4,2,256]{4,2,3,1,0:T(4,128)} %fusion.2), calls=%async_computation.1 | async-start | bytes 262144 | tf_op jit(solution)/shard_map/all_to_all | solution.py:211
  56.7 0.7 copy.92
  57.4 12.8 %shard_map.113.s_ref = f32[32,16,1024]{2,1,0:T(8,128)} custom-call(s32[32]{0:T(128)} %len_ref.1, bf16[32,16,128]{2,1,0:T(8,128)(2,1)} %bitcast.66, bf16[32,512,2,256]{3,2,1,0:T(2,128)(2,1)} %kv_ref.3), custom_call_target="tpu_custom_call" | custom-call | tf_op jit(solution)/shard_map/pallas_call | solution.py:96
  71.4 0.7 pad_maximum_fusion.1.nkv_ref
  72.1 13.1 %shard_map.114 = bf16[32,16,128]{2,1,0:T(8,128)(2,1)} custom-call(bf16[32,16,128]{2,1,0:T(8,128)(2,1)} %bitcast.67, f32[32,16,1024]{2,1,0:T(8,128)} %shard_map.113.s_ref, bf16[32,512,2,256]{3,2,1,0:T(2,128)(2,1)} %kv_ref.3, bf16[32,2,256]{2,1,0:T(2,128)(2,1)} %pad_maximum_fusion.1.nkv_ref), custom_call_target="tpu_custom_call" | custom-call | tf_op jit(solution)/shard_map/pallas_call | solution.py:106
  85.2 1.6 %copy.100 = bf16[4,8,16,128]{3,1,2,0:T(8,128)(2,1)} copy(bf16[4,8,16,128]{3,2,1,0:T(8,128)(2,1)} %bitcast.68) | data formatting | bytes 262144
  (70 shorter events, 6.1 us)
Async XLA Ops:
  0.6 48.6 %copy-start = (bf16[16,2,64,256]{3,2,1,0:T(8,128)(2,1)S(1)}, bf16[16,2,64,256]{3,2,1,0:T(8,128)(2,1)}, u32[]{:S(2)}) copy-start(bf16[16,2,64,256]{3,2,1,0:T(8,128)(2,1)} %param.14) | copy-start | bytes 3145732
  0.6 6.3 %copy-start.1 = (bf16[32,2048]{1,0:T(8,128)(2,1)S(1)}, bf16[32,2048]{1,0:T(8,128)(2,1)}, u32[]{:S(2)}) copy-start(bf16[32,2048]{1,0:T(8,128)(2,1)} %param.10) | copy-start | bytes 393220
  0.7 15.2 %copy-start.3 = (f32[8192]{0:T(1024)S(1)}, f32[8192]{0:T(1024)}, u32[]{:S(2)}) copy-start(f32[8192]{0:T(1024)} %param.11) | copy-start | bytes 98308
  18.2 15.5 %all-to-all-start = ((bf16[8,2,4,2176]{3,2,1,0:T(4,128)(2,1)}), bf16[8,2,4,2176]{3,2,1,0:T(4,128)(2,1)S(1)}, u32[]{:S(2)}, u32[]{:S(2)}) async-start(bf16[8,2,4,2176]{3,2,1,0:T(4,128)(2,1)} %pad_maximum_fusion), calls=%async_computation | async-start | bytes 557056 | tf_op jit(solution)/shard_map/all_to_all | solution.py:197
  42.1 14.5 %copy-start.4 = (s32[32]{0:T(128)S(1)}, s32[32]{0:T(128)}, u32[]{:S(2)}) copy-start(s32[32]{0:T(128)} %len_ref.1) | copy-start | bytes 388
  42.1 14.5 %copy-start.2 = (bf16[32,2048]{1,0:T(8,128)(2,1)S(1)}, bf16[32,2048]{1,0:T(8,128)(2,1)}, u32[]{:S(2)}) copy-start(bf16[32,2048]{1,0:T(8,128)(2,1)} %param.15) | copy-start | bytes 393220
  46.7 1.3 %collective-permute-start = (f32[8,2,4,128]{3,2,1,0:T(4,128)S(1)}, f32[8,2,4,128]{3,2,1,0:T(4,128)S(1)}, u32[]{:S(2)}, u32[]{:S(2)}) collective-permute-start(f32[8,2,4,128]{3,2,1,0:T(4,128)S(1)} %fusion.7), channel_id=1, source_target_pairs={{0,1},{1,0},{2,3},{3,2},{4,5},{5,4},{6,7},{7,6},{8,9},{9,8},{10,11... | collective-permute-start | bytes 98312 | tf_op jit(solution)/shard_map/ppermute | solution.py:128
  48.0 4.0 %collective-permute-start.1 = (f32[8,2,4,128]{3,2,1,0:T(4,128)S(1)}, f32[8,2,4,128]{3,2,1,0:T(4,128)S(1)}, u32[]{:S(2)}, u32[]{:S(2)}) collective-permute-start(f32[8,2,4,128]{3,2,1,0:T(4,128)S(1)} %add.146), channel_id=1, source_target_pairs={{0,2},{1,3},{2,0},{3,1},{4,6},{5,7},{6,4},{7,5},{8,10},{9,11},{10,... | collective-permute-start | bytes 98312 | tf_op jit(solution)/shard_map/ppermute | solution.py:128
  53.0 17.3 %all-to-all-start.1 = ((f32[8,2,4,2,256]{4,2,3,1,0:T(4,128)}), f32[8,2,4,2,256]{4,2,3,1,0:T(4,128)S(1)}, u32[]{:S(2)}, u32[]{:S(2)}) async-start(f32[8,2,4,2,256]{4,2,3,1,0:T(4,128)} %fusion.2), calls=%async_computation.1 | async-start | bytes 262144 | tf_op jit(solution)/shard_map/all_to_all | solution.py:211

commit v10 on v9

--- a/solution.py
+++ b/solution.py
@@ -197,10 +197,13 @@
     got = lax.all_to_all(payload, "replica", split_axis=0, concat_axis=0, tiled=True)
     got_rows = got[..., :part_width]
     got_ids = got[:, :, 0, part_width].astype(jnp.int32)
-    selected_down = adapter_down[got_ids]
     selected_up = adapter_up[got_ids]
-    partial_value = jnp.einsum(
-        "oksd,okdr->oksr", got_rows, selected_down, preferred_element_type=jnp.float32
+    every_adapter = jnp.einsum(
+        "oksd,adr->oksar", got_rows, adapter_down, preferred_element_type=jnp.float32
+    )
+    picked = got_ids[:, :, None] == jnp.arange(adapter_down.shape[0], dtype=jnp.int32)
+    partial_value = jnp.sum(
+        jnp.where(picked[:, :, None, :, None], every_adapter, 0.0), axis=3
     )
     summed = butterfly_sum(partial_value, "tensor").astype(jnp.bfloat16)
     summed = summed.reshape(summed.shape[:3] + (2, adapter_rank_size))

time: 87.5 us -> 79.7 us (0.911)
  local copies, waits for them, and re-layouts: 17.9 us -> 9.9 us
    gather x1 -> x0, local copies, waits for them, and re-layouts: 8.15 us -> none  [body(): selected_down = adapter_down[got_ids]]
  transfers between devices with their start and end apart: 4 -> 4, of which waited for: 3 -> 3; matrix products, arithmetic and copies ran while one was open for 9% -> 10% of each run, Pallas kernels for 15% -> 16%
where the time goes in v10:
time: 79.7 us; the launch traced here: 79 us
  Pallas kernels  25.9 us (32%)
  matrix products  10.8 us (14%)
  starting transfers between devices  10.6 us (13%)
  local copies, waits for them, and re-layouts  9.9 us (12%)
  blocking collectives  8.65 us (11%)
  waiting for transfers between devices  6.46 us (8%)
  other arithmetic  5.69 us (7%)
  between operations  0.92 us (1%)
    pallas_call x1, Pallas kernels, attend(): pl.pallas_call(functools.partial(mix_kernel, **opts), out_shape=jax.Shape...  13.1 us
    pallas_call x1, Pallas kernels, attend(): pl.pallas_call(functools.partial(score_kernel, **opts), out_shape=jax.Sha...  12.8 us
    all_gather x1, blocking collectives, body(): gathered = lax.all_gather(hidden, 'tensor', axis=1, tiled=True)  8.65 us
    all_to_all x1, starting transfers between devices, body(): lax.all_to_all(payload, 'replica', split_axis=0, concat_axis=0, tiled=True)  5.81 us
    dot_general x1, matrix products, body(): jnp.einsum('oksd,adr->oksar', got_rows, adapter_down, preferred_element_t...  5 us
    dot_general x1, matrix products, body(): jnp.einsum('jd,dcw->jcw', normed, key_value_weight, preferred_element_typ...  4.93 us
    all_to_all x1, starting transfers between devices, body(): lax.all_to_all(owner_delta, 'replica', split_axis=0, concat_axis=0, tiled...  3.63 us
    all_to_all x1, waiting for transfers between devices, body(): lax.all_to_all(payload, 'replica', split_axis=0, concat_axis=0, tiled=True)  3.26 us
  transfers between devices with their start and end apart: 4, of which 3 were waited for; matrix products, arithmetic and copies ran while one was open for 10% of the time, Pallas kernels for 16%

profile of v10, /device:TPU:0, one launch (start us, length us, event | category | flops | bytes accessed | tf_op | source)
XLA Modules:
  0.0 79.0 jit_solution(1663136973758714256)
XLA Ops:
  0.7 0.8 fusion.22
  1.4 0.7 and_select_fusion.2
  2.9 1.3 %gather_fusion = s32[16]{0:T(128)S(1)} fusion(s32[16]{0:T(128)} %bitcast.81, s32[1024]{0:T(1024)S(1)} %pad_clamp_fusion.4), kind=kCustom, calls=%fused_computation | custom fusion | bytes 192 | tf_op jit(solution)/shard_map/gather | solution.py:187
  4.5 0.7 copy.59
  5.4 0.7 bitcast_subtract_fusion.1
  7.1 8.6 %all_gather.3 = bf16[32,8192]{1,0:T(8,128)(2,1)S(1)} all-gather(bf16[32,2048]{1,0:T(8,128)(2,1)S(1)} %copy-done.1), channel_id=1, replica_groups=mesh['replica'=8,'tensor'=4] {'tensor'}, dimensions={1}, use_global_device_ids=true | all-gather | bytes 655360 | tf_op jit(solution)/shard_map/all_gather | solution.py:153
  16.2 0.7 gather_fusion.2
  17.3 0.8 %pad_maximum_fusion = bf16[8,2,4,2176]{3,2,1,0:T(4,128)(2,1)} fusion(bf16[8,2,4,128]{3,2,1,0:T(4,128)(2,1)S(1)} %broadcast_in_dim.54, bf16[8,2,4,2048]{3,2,1,0:T(4,128)(2,1)S(1)} %broadcast_select_fusion), kind=kLoop, calls=%fused_computation.21 | loop fusion | flops 557056 | bytes 557056 | tf_op jit(solution)/shard_map/concatenate | solution.py:196
  18.2 5.8 %all-to-all-start = ((bf16[8,2,4,2176]{3,2,1,0:T(4,128)(2,1)}), bf16[8,2,4,2176]{3,2,1,0:T(4,128)(2,1)S(1)}, u32[]{:S(2)}, u32[]{:S(2)}) async-start(bf16[8,2,4,2176]{3,2,1,0:T(4,128)(2,1)} %pad_maximum_fusion), calls=%async_computation | async-start | bytes 557056 | tf_op jit(solution)/shard_map/all_to_all | solution.py:197
  24.1 0.7 gather_fusion.5
  24.8 0.7 gather_fusion.4
  25.5 4.9 %fusion.2 = f32[32,2,256]{2,0,1:T(8,128)S(1)} fusion(bf16[8192,2,256]{2,1,0:T(2,128)(2,1)} %param.12, bf16[32,8192]{1,0:T(8,128)(2,1)S(1)} %fusion.13), kind=kOutput, calls=%fused_computation.9 | convolution fusion | flops 268435456 | bytes 8978432 | tf_op jit(solution)/shard_map/jd,dcw->jcw/dot_general | solution.py:217
  30.4 3.3 %all-to-all-done = bf16[8,2,4,2176]{3,2,1,0:T(4,128)(2,1)S(1)} async-done(((bf16[8,2,4,2176]{3,2,1,0:T(4,128)(2,1)}), bf16[8,2,4,2176]{3,2,1,0:T(4,128)(2,1)S(1)}, u32[]{:S(2)}, u32[]{:S(2)}) %all-to-all-start) | async-done | bytes 278560 | tf_op jit(solution)/shard_map/all_to_all | solution.py:197
  34.0 5.0 %fusion.7 = f32[8,2,4,128]{3,0,2,1:T(8,128)S(1)} fusion(bf16[16,2048,128]{2,1,0:T(8,128)(2,1)} %param.13, bf16[8,2,4,2048]{3,2,1,0:T(4,128)(2,1)S(1)} %slice.40, pred[8,2,16]{0,2,1:T(8,128)(4,1)S(1)} %iota_compare_fusion), kind=kOutput, calls=%fused_computation.14 | convolution fusion | flops 537124864 | bytes 8683776 | tf_op jit(solution)/shard_map/oksd,adr->oksar/dot_general | solution.py:201
  39.2 1.0 %collective-permute-done = f32[8,2,4,128]{3,0,2,1:T(8,128)S(1)} collective-permute-done((f32[8,2,4,128]{3,0,2,1:T(8,128)S(1)}, f32[8,2,4,128]{3,0,2,1:T(8,128)S(1)}, u32[]{:S(2)}, u32[]{:S(2)}) %collective-permute-start) | collective-permute-done | bytes 32800 | tf_op jit(solution)/shard_map/ppermute | solution.py:128
  40.3 1.1 %collective-permute-start.1 = (f32[8,2,4,128]{3,0,2,1:T(8,128)S(1)}, f32[8,2,4,128]{3,0,2,1:T(8,128)S(1)}, u32[]{:S(2)}, u32[]{:S(2)}) collective-permute-start(f32[8,2,4,128]{3,0,2,1:T(8,128)S(1)} %add.145), channel_id=1, source_target_pairs={{0,2},{1,3},{2,0},{3,1},{4,6},{5,7},{6,4},{7,5},{8,10},{9,11},{10,... | collective-permute-start | bytes 98312 | tf_op jit(solution)/shard_map/ppermute | solution.py:128
  42.0 2.2 %collective-permute-done.1 = f32[8,2,4,128]{3,0,2,1:T(8,128)S(1)} collective-permute-done((f32[8,2,4,128]{3,0,2,1:T(8,128)S(1)}, f32[8,2,4,128]{3,0,2,1:T(8,128)S(1)}, u32[]{:S(2)}, u32[]{:S(2)}) %collective-permute-start.1) | collective-permute-done | bytes 32800 | tf_op jit(solution)/shard_map/ppermute | solution.py:128
  44.3 0.9 %fusion.10 = f32[8,2,4,2,256]{4,2,3,1,0:T(4,128)} fusion(bf16[8,2,2,64,256]{4,3,2,1,0:T(8,128)(2,1)S(1)} %bitcast.83, bf16[8,2,4,2,64]{4,3,0,2,1:T(2,128)(2,1)S(1)} %reshape.348), kind=kOutput, calls=%fused_computation.16 | convolution fusion | flops 4227072 | bytes 1196032 | tf_op jit(solution)/shard_map/okscr,okcrw->okscw/dot_general | solution.py:211
  45.2 3.6 %all-to-all-start.1 = ((f32[8,2,4,2,256]{4,2,3,1,0:T(4,128)}), f32[8,2,4,2,256]{4,2,3,1,0:T(4,128)S(1)}, u32[]{:S(2)}, u32[]{:S(2)}) async-start(f32[8,2,4,2,256]{4,2,3,1,0:T(4,128)} %fusion.10), calls=%async_computation.1 | async-start | bytes 262144 | tf_op jit(solution)/shard_map/all_to_all | solution.py:214
  48.9 0.7 copy.72
  49.5 12.8 %shard_map.113.s_ref = f32[32,16,1024]{2,1,0:T(8,128)} custom-call(s32[32]{0:T(128)} %len_ref.1, bf16[32,16,128]{2,1,0:T(8,128)(2,1)} %bitcast.84, bf16[32,512,2,256]{3,2,1,0:T(2,128)(2,1)} %kv_ref.3), custom_call_target="tpu_custom_call" | custom-call | tf_op jit(solution)/shard_map/pallas_call | solution.py:96
  63.6 0.7 pad_maximum_fusion.1.nkv_ref
  64.3 13.1 %shard_map.114 = bf16[32,16,128]{2,1,0:T(8,128)(2,1)} custom-call(bf16[32,16,128]{2,1,0:T(8,128)(2,1)} %bitcast.85, f32[32,16,1024]{2,1,0:T(8,128)} %shard_map.113.s_ref, bf16[32,512,2,256]{3,2,1,0:T(2,128)(2,1)} %kv_ref.3, bf16[32,2,256]{2,1,0:T(2,128)(2,1)} %pad_maximum_fusion.1.nkv_ref), custom_call_target="tpu_custom_call" | custom-call | tf_op jit(solution)/shard_map/pallas_call | solution.py:106
  77.4 1.6 %copy.82 = bf16[4,8,16,128]{3,1,2,0:T(8,128)(2,1)} copy(bf16[4,8,16,128]{3,2,1,0:T(8,128)(2,1)} %bitcast.86) | data formatting | bytes 262144
  (72 shorter events, 5.6 us)
Async XLA Ops:
  0.6 40.7 %copy-start = (bf16[16,2,64,256]{3,2,1,0:T(8,128)(2,1)S(1)}, bf16[16,2,64,256]{3,2,1,0:T(8,128)(2,1)}, u32[]{:S(2)}) copy-start(bf16[16,2,64,256]{3,2,1,0:T(8,128)(2,1)} %param.14) | copy-start | bytes 3145732
  0.6 6.4 %copy-start.1 = (bf16[32,2048]{1,0:T(8,128)(2,1)S(1)}, bf16[32,2048]{1,0:T(8,128)(2,1)}, u32[]{:S(2)}) copy-start(bf16[32,2048]{1,0:T(8,128)(2,1)} %param.10) | copy-start | bytes 393220
  0.7 15.3 %copy-start.3 = (f32[8192]{0:T(1024)S(1)}, f32[8192]{0:T(1024)}, u32[]{:S(2)}) copy-start(f32[8192]{0:T(1024)} %param.11) | copy-start | bytes 98308
  18.2 15.5 %all-to-all-start = ((bf16[8,2,4,2176]{3,2,1,0:T(4,128)(2,1)}), bf16[8,2,4,2176]{3,2,1,0:T(4,128)(2,1)S(1)}, u32[]{:S(2)}, u32[]{:S(2)}) async-start(bf16[8,2,4,2176]{3,2,1,0:T(4,128)(2,1)} %pad_maximum_fusion), calls=%async_computation | async-start | bytes 557056 | tf_op jit(solution)/shard_map/all_to_all | solution.py:197
  33.9 14.9 %copy-start.4 = (s32[32]{0:T(128)S(1)}, s32[32]{0:T(128)}, u32[]{:S(2)}) copy-start(s32[32]{0:T(128)} %len_ref.1) | copy-start | bytes 388
  34.0 14.9 %copy-start.2 = (bf16[32,2048]{1,0:T(8,128)(2,1)S(1)}, bf16[32,2048]{1,0:T(8,128)(2,1)}, u32[]{:S(2)}) copy-start(bf16[32,2048]{1,0:T(8,128)(2,1)} %param.15) | copy-start | bytes 393220
  39.0 1.3 %collective-permute-start = (f32[8,2,4,128]{3,0,2,1:T(8,128)S(1)}, f32[8,2,4,128]{3,0,2,1:T(8,128)S(1)}, u32[]{:S(2)}, u32[]{:S(2)}) collective-permute-start(f32[8,2,4,128]{3,0,2,1:T(8,128)S(1)} %fusion.7), channel_id=1, source_target_pairs={{0,1},{1,0},{2,3},{3,2},{4,5},{5,4},{6,7},{7,6},{8,9},{9,8},{10,11... | collective-permute-start | bytes 98312 | tf_op jit(solution)/shard_map/ppermute | solution.py:128
  40.3 3.9 %collective-permute-start.1 = (f32[8,2,4,128]{3,0,2,1:T(8,128)S(1)}, f32[8,2,4,128]{3,0,2,1:T(8,128)S(1)}, u32[]{:S(2)}, u32[]{:S(2)}) collective-permute-start(f32[8,2,4,128]{3,0,2,1:T(8,128)S(1)} %add.145), channel_id=1, source_target_pairs={{0,2},{1,3},{2,0},{3,1},{4,6},{5,7},{6,4},{7,5},{8,10},{9,11},{10,... | collective-permute-start | bytes 98312 | tf_op jit(solution)/shard_map/ppermute | solution.py:128
  45.2 17.3 %all-to-all-start.1 = ((f32[8,2,4,2,256]{4,2,3,1,0:T(4,128)}), f32[8,2,4,2,256]{4,2,3,1,0:T(4,128)S(1)}, u32[]{:S(2)}, u32[]{:S(2)}) async-start(f32[8,2,4,2,256]{4,2,3,1,0:T(4,128)} %fusion.10), calls=%async_computation.1 | async-start | bytes 262144 | tf_op jit(solution)/shard_map/all_to_all | solution.py:214

commit v11 on v10

--- a/solution.py
+++ b/solution.py
@@ -79,7 +79,10 @@
             own_prob = (own_weight / total).astype(jnp.bfloat16).astype(jnp.float32)
             context = jnp.dot(probs, stacked[:, cols], preferred_element_type=jnp.float32)
             context = context + own_prob * new_value
-            o_ref[i, qrows, :] = context.astype(o_ref.dtype)
+            context = context.astype(o_ref.dtype)
+            for g in range(group_size):
+                lanes = slice((h * group_size + g) * HEAD, (h * group_size + g + 1) * HEAD)
+                o_ref[i:i + 1, lanes] = context[g:g + 1]
 
 
 def attend(query, key_value_cache, new_kv, cached_length, kv_local, group_size):
@@ -103,19 +106,20 @@
             out_specs=score_spec,
         ),
     )(cached_length, query_heads, key_value_cache)
+    mix_rows = 8 if row_count % 8 == 0 else row_count
     out = pl.pallas_call(
-        functools.partial(mix_kernel, **opts),
-        out_shape=jax.ShapeDtypeStruct((row_count, heads, HEAD), jnp.bfloat16),
-        grid=(row_count // rows,),
+        functools.partial(mix_kernel, rows=mix_rows, kv_local=kv_local, group_size=group_size),
+        out_shape=jax.ShapeDtypeStruct((row_count, heads * HEAD), jnp.bfloat16),
+        grid=(row_count // mix_rows,),
         in_specs=[
-            head_spec,
-            score_spec,
-            cache_spec,
-            pl.BlockSpec((rows, 2, width), lambda b: (b, 0, 0)),
+            pl.BlockSpec((mix_rows, heads, HEAD), lambda b: (b, 0, 0)),
+            pl.BlockSpec((mix_rows, heads, 2 * cache_len), lambda b: (b, 0, 0)),
+            pl.BlockSpec((mix_rows, cache_len, 2, width), lambda b: (b, 0, 0, 0)),
+            pl.BlockSpec((mix_rows, 2, width), lambda b: (b, 0, 0)),
         ],
-        out_specs=head_spec,
+        out_specs=pl.BlockSpec((mix_rows, heads * HEAD), lambda b: (b, 0)),
     )(query_heads, scores, key_value_cache, new_kv)
-    return out.reshape(row_count, heads * HEAD)
+    return out
 
 
 def butterfly_sum(value, axis):

time: 79.7 us -> 75.9 us (0.952)
  Pallas kernels: 25.9 us -> 23.9 us
  local copies, waits for them, and re-layouts: 9.9 us -> 8.3 us
    pallas_call x1, Pallas kernels: 13.1 us -> 11.1 us  [attend(): pl.pallas_call(functools.partial(mix_kernel, rows=mix_rows, kv_local=kv_l...]
    unnamed x13 -> x12, local copies, waits for them, and re-layouts: 2.4 us -> 0.8 us
  transfers between devices with their start and end apart: 4 -> 4, of which waited for: 3 -> 3; matrix products, arithmetic and copies ran while one was open for 10% -> 11% of each run, Pallas kernels for 16% -> 17%
where the time goes in v11:
time: 75.9 us; the launch traced here: 75.4 us
  Pallas kernels  23.9 us (31%)
  matrix products  10.8 us (14%)
  starting transfers between devices  10.6 us (14%)
  blocking collectives  8.65 us (11%)
  local copies, waits for them, and re-layouts  8.3 us (11%)
  waiting for transfers between devices  6.46 us (9%)
  other arithmetic  5.69 us (7%)
  between operations  0.92 us (1%)
    pallas_call x1, Pallas kernels, attend(): pl.pallas_call(functools.partial(score_kernel, **opts), out_shape=jax.Sha...  12.8 us
    pallas_call x1, Pallas kernels, attend(): pl.pallas_call(functools.partial(mix_kernel, rows=mix_rows, kv_local=kv_l...  11.1 us
    all_gather x1, blocking collectives, body(): gathered = lax.all_gather(hidden, 'tensor', axis=1, tiled=True)  8.65 us
    all_to_all x1, starting transfers between devices, body(): lax.all_to_all(payload, 'replica', split_axis=0, concat_axis=0, tiled=True)  5.81 us
    dot_general x1, matrix products, body(): jnp.einsum('oksd,adr->oksar', got_rows, adapter_down, preferred_element_t...  5 us
    dot_general x1, matrix products, body(): jnp.einsum('jd,dcw->jcw', normed, key_value_weight, preferred_element_typ...  4.93 us
    all_to_all x1, starting transfers between devices, body(): lax.all_to_all(owner_delta, 'replica', split_axis=0, concat_axis=0, tiled...  3.63 us
    all_to_all x1, waiting for transfers between devices, body(): lax.all_to_all(payload, 'replica', split_axis=0, concat_axis=0, tiled=True)  3.26 us
  transfers between devices with their start and end apart: 4, of which 3 were waited for; matrix products, arithmetic and copies ran while one was open for 11% of the time, Pallas kernels for 17%

profile of v11, /device:TPU:0, one launch (start us, length us, event | category | flops | bytes accessed | tf_op | source)
XLA Modules:
  0.0 75.4 jit_solution(13868367480376626134)
XLA Ops:
  0.7 0.8 %fusion.22 = s32[16]{0:T(128)S(1)} fusion(s32[1,16]{1,0:T(1,128)} %param.17), kind=kLoop, calls=%fused_computation.78 | loop fusion | flops 240 | bytes 128 | tf_op jit(solution)/shard_map/eq | solution.py:179
  1.4 0.7 and_select_fusion.2
  2.9 1.3 %gather_fusion = s32[16]{0:T(128)S(1)} fusion(s32[16]{0:T(128)} %bitcast.77, s32[1024]{0:T(1024)S(1)} %pad_clamp_fusion.4), kind=kCustom, calls=%fused_computation | custom fusion | bytes 192 | tf_op jit(solution)/shard_map/gather | solution.py:191
  4.5 0.7 copy.59
  5.4 0.7 bitcast_subtract_fusion.1
  6.1 0.7 gather_fusion.1
  7.1 8.6 %all_gather.3 = bf16[32,8192]{1,0:T(8,128)(2,1)S(1)} all-gather(bf16[32,2048]{1,0:T(8,128)(2,1)S(1)} %copy-done.1), channel_id=1, replica_groups=mesh['replica'=8,'tensor'=4] {'tensor'}, dimensions={1}, use_global_device_ids=true | all-gather | bytes 655360 | tf_op jit(solution)/shard_map/all_gather | solution.py:157
  16.2 0.7 gather_fusion.2
  17.3 0.8 %pad_maximum_fusion = bf16[8,2,4,2176]{3,2,1,0:T(4,128)(2,1)} fusion(bf16[8,2,4,128]{3,2,1,0:T(4,128)(2,1)S(1)} %broadcast_in_dim.54, bf16[8,2,4,2048]{3,2,1,0:T(4,128)(2,1)S(1)} %broadcast_select_fusion), kind=kLoop, calls=%fused_computation.21 | loop fusion | flops 557056 | bytes 557056 | tf_op jit(solution)/shard_map/concatenate | solution.py:200
  18.2 5.8 %all-to-all-start = ((bf16[8,2,4,2176]{3,2,1,0:T(4,128)(2,1)}), bf16[8,2,4,2176]{3,2,1,0:T(4,128)(2,1)S(1)}, u32[]{:S(2)}, u32[]{:S(2)}) async-start(bf16[8,2,4,2176]{3,2,1,0:T(4,128)(2,1)} %pad_maximum_fusion), calls=%async_computation | async-start | bytes 557056 | tf_op jit(solution)/shard_map/all_to_all | solution.py:201
  24.1 0.7 gather_fusion.5
  24.8 0.7 gather_fusion.4
  25.5 4.9 %fusion.2 = f32[32,2,256]{2,0,1:T(8,128)S(1)} fusion(bf16[8192,2,256]{2,1,0:T(2,128)(2,1)} %param.12, bf16[32,8192]{1,0:T(8,128)(2,1)S(1)} %fusion.13), kind=kOutput, calls=%fused_computation.9 | convolution fusion | flops 268435456 | bytes 8978432 | tf_op jit(solution)/shard_map/jd,dcw->jcw/dot_general | solution.py:221
  30.4 3.3 %all-to-all-done = bf16[8,2,4,2176]{3,2,1,0:T(4,128)(2,1)S(1)} async-done(((bf16[8,2,4,2176]{3,2,1,0:T(4,128)(2,1)}), bf16[8,2,4,2176]{3,2,1,0:T(4,128)(2,1)S(1)}, u32[]{:S(2)}, u32[]{:S(2)}) %all-to-all-start) | async-done | bytes 278560 | tf_op jit(solution)/shard_map/all_to_all | solution.py:201
  34.0 5.0 %fusion.7 = f32[8,2,4,128]{3,0,2,1:T(8,128)S(1)} fusion(bf16[16,2048,128]{2,1,0:T(8,128)(2,1)} %param.13, bf16[8,2,4,2048]{3,2,1,0:T(4,128)(2,1)S(1)} %slice.40, pred[8,2,16]{0,2,1:T(8,128)(4,1)S(1)} %iota_compare_fusion), kind=kOutput, calls=%fused_computation.14 | convolution fusion | flops 537124864 | bytes 8683776 | tf_op jit(solution)/shard_map/oksd,adr->oksar/dot_general | solution.py:205
  39.2 1.0 %collective-permute-done = f32[8,2,4,128]{3,0,2,1:T(8,128)S(1)} collective-permute-done((f32[8,2,4,128]{3,0,2,1:T(8,128)S(1)}, f32[8,2,4,128]{3,0,2,1:T(8,128)S(1)}, u32[]{:S(2)}, u32[]{:S(2)}) %collective-permute-start) | collective-permute-done | bytes 32800 | tf_op jit(solution)/shard_map/ppermute | solution.py:132
  40.3 1.1 %collective-permute-start.1 = (f32[8,2,4,128]{3,0,2,1:T(8,128)S(1)}, f32[8,2,4,128]{3,0,2,1:T(8,128)S(1)}, u32[]{:S(2)}, u32[]{:S(2)}) collective-permute-start(f32[8,2,4,128]{3,0,2,1:T(8,128)S(1)} %add.145), channel_id=1, source_target_pairs={{0,2},{1,3},{2,0},{3,1},{4,6},{5,7},{6,4},{7,5},{8,10},{9,11},{10,... | collective-permute-start | bytes 98312 | tf_op jit(solution)/shard_map/ppermute | solution.py:132
  42.0 2.2 %collective-permute-done.1 = f32[8,2,4,128]{3,0,2,1:T(8,128)S(1)} collective-permute-done((f32[8,2,4,128]{3,0,2,1:T(8,128)S(1)}, f32[8,2,4,128]{3,0,2,1:T(8,128)S(1)}, u32[]{:S(2)}, u32[]{:S(2)}) %collective-permute-start.1) | collective-permute-done | bytes 32800 | tf_op jit(solution)/shard_map/ppermute | solution.py:132
  44.3 0.9 %fusion.10 = f32[8,2,4,2,256]{4,2,3,1,0:T(4,128)} fusion(bf16[8,2,2,64,256]{4,3,2,1,0:T(8,128)(2,1)S(1)} %bitcast.79, bf16[8,2,4,2,64]{4,3,0,2,1:T(2,128)(2,1)S(1)} %reshape.345), kind=kOutput, calls=%fused_computation.16 | convolution fusion | flops 4227072 | bytes 1196032 | tf_op jit(solution)/shard_map/okscr,okcrw->okscw/dot_general | solution.py:215
  45.2 3.6 %all-to-all-start.1 = ((f32[8,2,4,2,256]{4,2,3,1,0:T(4,128)}), f32[8,2,4,2,256]{4,2,3,1,0:T(4,128)S(1)}, u32[]{:S(2)}, u32[]{:S(2)}) async-start(f32[8,2,4,2,256]{4,2,3,1,0:T(4,128)} %fusion.10), calls=%async_computation.1 | async-start | bytes 262144 | tf_op jit(solution)/shard_map/all_to_all | solution.py:218
  48.9 0.7 copy.72
  49.5 12.8 %shard_map.113.s_ref = f32[32,16,1024]{2,1,0:T(8,128)} custom-call(s32[32]{0:T(128)} %len_ref.1, bf16[32,16,128]{2,1,0:T(8,128)(2,1)} %bitcast.80, bf16[32,512,2,256]{3,2,1,0:T(2,128)(2,1)} %kv_ref.3), custom_call_target="tpu_custom_call" | custom-call | tf_op jit(solution)/shard_map/pallas_call | solution.py:99
  63.6 0.7 pad_maximum_fusion.1.nkv_ref
  64.3 11.1 %shard_map.114 = bf16[32,2048]{1,0:T(8,128)(2,1)} custom-call(bf16[32,16,128]{2,1,0:T(8,128)(2,1)} %bitcast.81, f32[32,16,1024]{2,1,0:T(8,128)} %shard_map.113.s_ref, bf16[32,512,2,256]{3,2,1,0:T(2,128)(2,1)} %kv_ref.3, bf16[32,2,256]{2,1,0:T(2,128)(2,1)} %pad_maximum_fusion.1.nkv_ref), custom_call_target="tpu_custom_call" | custom-call | tf_op jit(solution)/shard_map/pallas_call | solution.py:110
  (71 shorter events, 4.9 us)
Async XLA Ops:
  0.6 40.7 %copy-start = (bf16[16,2,64,256]{3,2,1,0:T(8,128)(2,1)S(1)}, bf16[16,2,64,256]{3,2,1,0:T(8,128)(2,1)}, u32[]{:S(2)}) copy-start(bf16[16,2,64,256]{3,2,1,0:T(8,128)(2,1)} %param.14) | copy-start | bytes 3145732
  0.6 6.4 %copy-start.1 = (bf16[32,2048]{1,0:T(8,128)(2,1)S(1)}, bf16[32,2048]{1,0:T(8,128)(2,1)}, u32[]{:S(2)}) copy-start(bf16[32,2048]{1,0:T(8,128)(2,1)} %param.10) | copy-start | bytes 393220
  0.7 15.3 %copy-start.3 = (f32[8192]{0:T(1024)S(1)}, f32[8192]{0:T(1024)}, u32[]{:S(2)}) copy-start(f32[8192]{0:T(1024)} %param.11) | copy-start | bytes 98308
  18.2 15.5 %all-to-all-start = ((bf16[8,2,4,2176]{3,2,1,0:T(4,128)(2,1)}), bf16[8,2,4,2176]{3,2,1,0:T(4,128)(2,1)S(1)}, u32[]{:S(2)}, u32[]{:S(2)}) async-start(bf16[8,2,4,2176]{3,2,1,0:T(4,128)(2,1)} %pad_maximum_fusion), calls=%async_computation | async-start | bytes 557056 | tf_op jit(solution)/shard_map/all_to_all | solution.py:201
  33.9 14.9 %copy-start.4 = (s32[32]{0:T(128)S(1)}, s32[32]{0:T(128)}, u32[]{:S(2)}) copy-start(s32[32]{0:T(128)} %len_ref.1) | copy-start | bytes 388
  34.0 14.9 %copy-start.2 = (bf16[32,2048]{1,0:T(8,128)(2,1)S(1)}, bf16[32,2048]{1,0:T(8,128)(2,1)}, u32[]{:S(2)}) copy-start(bf16[32,2048]{1,0:T(8,128)(2,1)} %param.15) | copy-start | bytes 393220
  39.0 1.3 %collective-permute-start = (f32[8,2,4,128]{3,0,2,1:T(8,128)S(1)}, f32[8,2,4,128]{3,0,2,1:T(8,128)S(1)}, u32[]{:S(2)}, u32[]{:S(2)}) collective-permute-start(f32[8,2,4,128]{3,0,2,1:T(8,128)S(1)} %fusion.7), channel_id=1, source_target_pairs={{0,1},{1,0},{2,3},{3,2},{4,5},{5,4},{6,7},{7,6},{8,9},{9,8},{10,11... | collective-permute-start | bytes 98312 | tf_op jit(solution)/shard_map/ppermute | solution.py:132
  40.3 3.9 %collective-permute-start.1 = (f32[8,2,4,128]{3,0,2,1:T(8,128)S(1)}, f32[8,2,4,128]{3,0,2,1:T(8,128)S(1)}, u32[]{:S(2)}, u32[]{:S(2)}) collective-permute-start(f32[8,2,4,128]{3,0,2,1:T(8,128)S(1)} %add.145), channel_id=1, source_target_pairs={{0,2},{1,3},{2,0},{3,1},{4,6},{5,7},{6,4},{7,5},{8,10},{9,11},{10,... | collective-permute-start | bytes 98312 | tf_op jit(solution)/shard_map/ppermute | solution.py:132
  45.2 17.3 %all-to-all-start.1 = ((f32[8,2,4,2,256]{4,2,3,1,0:T(4,128)}), f32[8,2,4,2,256]{4,2,3,1,0:T(4,128)S(1)}, u32[]{:S(2)}, u32[]{:S(2)}) async-start(f32[8,2,4,2,256]{4,2,3,1,0:T(4,128)} %fusion.10), calls=%async_computation.1 | async-start | bytes 262144 | tf_op jit(solution)/shard_map/all_to_all | solution.py:218

commit v12 on v11

--- a/solution.py
+++ b/solution.py
@@ -85,7 +85,7 @@
                 o_ref[i:i + 1, lanes] = context[g:g + 1]
 
 
-def attend(query, key_value_cache, new_kv, cached_length, kv_local, group_size):
+def attention_scores(query, key_value_cache, cached_length, kv_local, group_size):
     row_count = query.shape[0]
     cache_len = key_value_cache.shape[1]
     width = key_value_cache.shape[3]
@@ -106,6 +106,14 @@
             out_specs=score_spec,
         ),
     )(cached_length, query_heads, key_value_cache)
+    return query_heads, scores
+
+
+def attend(query_heads, scores, key_value_cache, new_kv, kv_local, group_size):
+    row_count = query_heads.shape[0]
+    cache_len = key_value_cache.shape[1]
+    width = key_value_cache.shape[3]
+    heads = kv_local * group_size
     mix_rows = 8 if row_count % 8 == 0 else row_count
     out = pl.pallas_call(
         functools.partial(mix_kernel, rows=mix_rows, kv_local=kv_local, group_size=group_size),
@@ -199,6 +207,11 @@
     )
     payload = jnp.concatenate([slot_rows, tags], axis=3)
     got = lax.all_to_all(payload, "replica", split_axis=0, concat_axis=0, tiled=True)
+    group_size = query.shape[1] // HEAD // kv_local
+    query_heads, scores = attention_scores(
+        query, key_value_cache, cached_length, kv_local, group_size
+    )
+    got, query_heads, scores = lax.optimization_barrier((got, query_heads, scores))
     got_rows = got[..., :part_width]
     got_ids = got[:, :, 0, part_width].astype(jnp.int32)
     selected_up = adapter_up[got_ids]
@@ -215,11 +228,12 @@
         jnp.einsum("okscr,okcrw->okscw", summed, selected_up, preferred_element_type=jnp.float32)
         * ADAPTER_SCALE
     )
+    owner_delta, late_normed = lax.optimization_barrier((owner_delta, normed))
     slot_delta = lax.all_to_all(owner_delta, "replica", split_axis=0, concat_axis=0, tiled=True)
     flat_delta = slot_delta.reshape((replicas * CAP * SLOT,) + slot_delta.shape[3:])
     adapter_delta = flat_delta[fetch_slot[segment_index] * SLOT + token_position]
     base_projection = jnp.einsum(
-        "jd,dcw->jcw", normed, key_value_weight, preferred_element_type=jnp.float32
+        "jd,dcw->jcw", late_normed, key_value_weight, preferred_element_type=jnp.float32
     )
     current_key_value = base_projection + adapter_delta
     rotated = rotate(
@@ -227,7 +241,7 @@
     ).reshape(row_count, kv_width)
     new_kv = jnp.stack([rotated, current_key_value[:, 1]], axis=1).astype(jnp.bfloat16)
     group_size = query.shape[1] // HEAD // kv_local
-    attended = attend(query, key_value_cache, new_kv, cached_length, kv_local, group_size)
+    attended = attend(query_heads, scores, key_value_cache, new_kv, kv_local, group_size)
     return (new_kv, attended)
 
 

time: 75.9 us -> 85.8 us (1.13)
  local copies, waits for them, and re-layouts: 8.3 us -> 16 us
  starting transfers between devices: 10.6 us -> 13 us
  waiting for transfers between devices: 6.46 us -> 4.89 us
  other arithmetic: 5.69 us -> 7.01 us
    optimization_barrier x0 -> x2, local copies, waits for them, and re-layouts: none -> 7.94 us  [body(): lax.optimization_barrier((got, query_heads, scores))]
    all_to_all x1, waiting for transfers between devices: 3.26 us -> 0.01 us  [body(): lax.all_to_all(payload, 'replica', split_axis=0, concat_axis=0, tiled=True)]
    all_to_all x1, waiting for transfers between devices: 0.01 us -> 2.41 us  [body(): lax.all_to_all(owner_delta, 'replica', split_axis=0, concat_axis=0, tiled...]
    all_to_all x1, starting transfers between devices: 3.63 us -> 5.99 us  [body(): lax.all_to_all(owner_delta, 'replica', split_axis=0, concat_axis=0, tiled...]
  transfers between devices with their start and end apart: 4 -> 4, of which waited for: 3 -> 3; matrix products, arithmetic and copies ran while one was open for 11% -> 10% of each run, Pallas kernels for 17% -> 15%
where the time goes in v12:
time: 85.8 us; the launch traced here: 85.2 us
  Pallas kernels  23.9 us (28%)
  local copies, waits for them, and re-layouts  16 us (19%)
  starting transfers between devices  13 us (15%)
  matrix products  10.8 us (13%)
  blocking collectives  8.65 us (10%)
  other arithmetic  7.01 us (8%)
  waiting for transfers between devices  4.89 us (6%)
  between operations  0.89 us (1%)
    pallas_call x1, Pallas kernels, attention_scores(): pl.pallas_call(functools.partial(score_kernel, **opts), out_shape=jax.Sha...  12.8 us
    pallas_call x1, Pallas kernels, attend(): pl.pallas_call(functools.partial(mix_kernel, rows=mix_rows, kv_local=kv_l...  11.1 us
    all_gather x1, blocking collectives, body(): gathered = lax.all_gather(hidden, 'tensor', axis=1, tiled=True)  8.65 us
    optimization_barrier x2, local copies, waits for them, and re-layouts, body(): lax.optimization_barrier((got, query_heads, scores))  7.94 us
    all_to_all x1, starting transfers between devices, body(): lax.all_to_all(owner_delta, 'replica', split_axis=0, concat_axis=0, tiled...  5.99 us
    all_to_all x1, starting transfers between devices, body(): lax.all_to_all(payload, 'replica', split_axis=0, concat_axis=0, tiled=True)  5.8 us
    dot_general x1, matrix products, body(): jnp.einsum('jd,dcw->jcw', late_normed, key_value_weight, preferred_elemen...  4.93 us
    dot_general x1, matrix products, body(): jnp.einsum('oksd,adr->oksar', got_rows, adapter_down, preferred_element_t...  4.91 us
  transfers between devices with their start and end apart: 4, of which 3 were waited for; matrix products, arithmetic and copies ran while one was open for 10% of the time, Pallas kernels for 15%

profile of v12, /device:TPU:0, one launch (start us, length us, event | category | flops | bytes accessed | tf_op | source)
XLA Modules:
  0.0 85.2 jit_solution(7192137303970395624)
XLA Ops:
  0.7 0.8 and_select_fusion.2
  1.4 0.7 fusion.22
  2.8 1.3 %gather_fusion = s32[16]{0:T(128)S(1)} fusion(s32[16]{0:T(128)} %bitcast.77, s32[1024]{0:T(1024)S(1)} %pad_clamp_fusion.4), kind=kCustom, calls=%fused_computation | custom fusion | bytes 192 | tf_op jit(solution)/shard_map/gather | solution.py:199
  4.4 0.7 copy.58
  7.0 8.6 %all_gather.3 = bf16[32,8192]{1,0:T(8,128)(2,1)S(1)} all-gather(bf16[32,2048]{1,0:T(8,128)(2,1)S(1)} %copy-done.1), channel_id=1, replica_groups=mesh['replica'=8,'tensor'=4] {'tensor'}, dimensions={1}, use_global_device_ids=true | all-gather | bytes 655360 | tf_op jit(solution)/shard_map/all_gather | solution.py:165
  16.1 0.7 gather_fusion.2
  17.4 0.8 pad_maximum_fusion
  18.2 5.8 %all-to-all-start = ((bf16[8,2,4,2176]{3,2,1,0:T(4,128)(2,1)}), bf16[8,2,4,2176]{3,2,1,0:T(4,128)(2,1)S(1)}, u32[]{:S(2)}, u32[]{:S(2)}) async-start(bf16[8,2,4,2176]{3,2,1,0:T(4,128)(2,1)} %pad_maximum_fusion), calls=%async_computation | async-start | bytes 557056 | tf_op jit(solution)/shard_map/all_to_all | solution.py:209
  24.1 0.7 gather_fusion.5
  24.8 0.7 gather_fusion.4
  25.5 0.7 copy.70
  26.2 12.8 %shard_map.113.s_ref = f32[32,16,1024]{2,1,0:T(8,128)} custom-call(s32[32]{0:T(128)} %len_ref.1, bf16[32,16,128]{2,1,0:T(8,128)(2,1)} %bitcast.80, bf16[32,512,2,256]{3,2,1,0:T(2,128)(2,1)} %kv_ref.3), custom_call_target="tpu_custom_call" | custom-call | tf_op jit(solution)/shard_map/pallas_call | solution.py:99
  39.2 7.9 %copy.60 = bf16[8,2,4,2176]{0,1,3,2:T(2,128)(2,1)} copy(bf16[8,2,4,2176]{3,2,1,0:T(4,128)(2,1)S(1)} %all-to-all-done) | data formatting | bytes 557056 | tf_op jit(solution)/shard_map/optimization_barrier | solution.py:214
  47.1 0.7 convert_bitcast_fusion
  47.8 4.9 %fusion.7 = f32[8,2,4,128]{3,0,2,1:T(8,128)S(1)} fusion(bf16[16,2048,128]{2,1,0:T(8,128)(2,1)} %param.13, bf16[8,2,4,2176]{3,0,2,1:T(8,128)(2,1)S(1)} %copy.62, pred[8,2,16]{0,2,1:T(8,128)(4,1)S(1)} %iota_compare_fusion), kind=kOutput, calls=%fused_computation.14 | convolution fusion | flops 537124864 | bytes 8687616 | tf_op jit(solution)/shard_map/oksd,adr->oksar/dot_general | solution.py:218
  52.9 0.7 compare_select_fusion.2
  54.0 1.1 %collective-permute-start.1 = (f32[8,2,4,128]{3,0,2,1:T(8,128)S(1)}, f32[8,2,4,128]{3,0,2,1:T(8,128)S(1)}, u32[]{:S(2)}, u32[]{:S(2)}) collective-permute-start(f32[8,2,4,128]{3,0,2,1:T(8,128)S(1)} %add.145), channel_id=1, source_target_pairs={{0,2},{1,3},{2,0},{3,1},{4,6},{5,7},{6,4},{7,5},{8,10},{9,11},{10,... | collective-permute-start | bytes 98312 | tf_op jit(solution)/shard_map/ppermute | solution.py:140
  55.7 2.2 %collective-permute-done.1 = f32[8,2,4,128]{3,0,2,1:T(8,128)S(1)} collective-permute-done((f32[8,2,4,128]{3,0,2,1:T(8,128)S(1)}, f32[8,2,4,128]{3,0,2,1:T(8,128)S(1)}, u32[]{:S(2)}, u32[]{:S(2)}) %collective-permute-start.1) | collective-permute-done | bytes 32800 | tf_op jit(solution)/shard_map/ppermute | solution.py:140
  58.0 0.9 %fusion.10 = f32[8,2,4,2,256]{4,2,3,1,0:T(4,128)} fusion(bf16[8,2,2,64,256]{4,3,2,1,0:T(8,128)(2,1)S(1)} %bitcast.79, bf16[8,2,4,2,64]{4,3,0,2,1:T(2,128)(2,1)S(1)} %reshape.346), kind=kOutput, calls=%fused_computation.16 | convolution fusion | flops 4227072 | bytes 1196032 | tf_op jit(solution)/shard_map/okscr,okcrw->okscw/dot_general | solution.py:228
  58.9 6.0 %all-to-all-start.1 = ((f32[8,2,4,2,256]{4,2,3,1,0:T(4,128)}), f32[8,2,4,2,256]{4,2,3,1,0:T(4,128)S(1)}, u32[]{:S(2)}, u32[]{:S(2)}) async-start(f32[8,2,4,2,256]{4,2,3,1,0:T(4,128)} %fusion.10), calls=%async_computation.1 | async-start | bytes 262144 | tf_op jit(solution)/shard_map/all_to_all | solution.py:232
  64.9 4.9 %fusion.2 = f32[32,2,256]{2,0,1:T(8,128)S(1)} fusion(bf16[8192,2,256]{2,1,0:T(2,128)(2,1)} %param.12, bf16[32,8192]{1,0:T(8,128)(2,1)S(1)} %fusion.13), kind=kOutput, calls=%fused_computation.9 | convolution fusion | flops 268435456 | bytes 8978432 | tf_op jit(solution)/shard_map/jd,dcw->jcw/dot_general | solution.py:235
  69.9 2.4 %all-to-all-done.1 = f32[8,2,4,2,256]{4,2,3,1,0:T(4,128)S(1)} async-done(((f32[8,2,4,2,256]{4,2,3,1,0:T(4,128)}), f32[8,2,4,2,256]{4,2,3,1,0:T(4,128)S(1)}, u32[]{:S(2)}, u32[]{:S(2)}) %all-to-all-start.1) | async-done | bytes 131104 | tf_op jit(solution)/shard_map/all_to_all | solution.py:232
  73.4 0.7 pad_maximum_fusion.1.nkv_ref
  74.1 11.1 %shard_map.114 = bf16[32,2048]{1,0:T(8,128)(2,1)} custom-call(bf16[32,16,128]{2,1,0:T(8,128)(2,1)} %bitcast.81, f32[32,16,1024]{2,1,0:T(8,128)} %shard_map.113.s_ref, bf16[32,512,2,256]{3,2,1,0:T(2,128)(2,1)} %kv_ref.3, bf16[32,2,256]{2,1,0:T(2,128)(2,1)} %pad_maximum_fusion.1.nkv_ref), custom_call_target="tpu_custom_call" | custom-call | tf_op jit(solution)/shard_map/pallas_call | solution.py:118
  (70 shorter events, 6.4 us)
Async XLA Ops:
  0.6 54.5 %copy-start = (bf16[16,2,64,256]{3,2,1,0:T(8,128)(2,1)S(1)}, bf16[16,2,64,256]{3,2,1,0:T(8,128)(2,1)}, u32[]{:S(2)}) copy-start(bf16[16,2,64,256]{3,2,1,0:T(8,128)(2,1)} %param.14) | copy-start | bytes 3145732
  0.6 6.3 %copy-start.1 = (bf16[32,2048]{1,0:T(8,128)(2,1)S(1)}, bf16[32,2048]{1,0:T(8,128)(2,1)}, u32[]{:S(2)}) copy-start(bf16[32,2048]{1,0:T(8,128)(2,1)} %param.10) | copy-start | bytes 393220
  0.7 15.2 %copy-start.3 = (f32[8192]{0:T(1024)S(1)}, f32[8192]{0:T(1024)}, u32[]{:S(2)}) copy-start(f32[8192]{0:T(1024)} %param.11) | copy-start | bytes 98308
  0.7 24.9 %copy-start.2 = (bf16[32,2048]{1,0:T(8,128)(2,1)S(1)}, bf16[32,2048]{1,0:T(8,128)(2,1)}, u32[]{:S(2)}) copy-start(bf16[32,2048]{1,0:T(8,128)(2,1)} %param.15) | copy-start | bytes 393220
  2.8 23.4 %copy-start.4 = (s32[32]{0:T(128)S(1)}, s32[32]{0:T(128)}, u32[]{:S(2)}) copy-start(s32[32]{0:T(128)} %len_ref.1) | copy-start | bytes 388
  18.2 21.0 %all-to-all-start = ((bf16[8,2,4,2176]{3,2,1,0:T(4,128)(2,1)}), bf16[8,2,4,2176]{3,2,1,0:T(4,128)(2,1)S(1)}, u32[]{:S(2)}, u32[]{:S(2)}) async-start(bf16[8,2,4,2176]{3,2,1,0:T(4,128)(2,1)} %pad_maximum_fusion), calls=%async_computation | async-start | bytes 557056 | tf_op jit(solution)/shard_map/all_to_all | solution.py:209
  52.7 1.3 %collective-permute-start = (f32[8,2,4,128]{3,0,2,1:T(8,128)S(1)}, f32[8,2,4,128]{3,0,2,1:T(8,128)S(1)}, u32[]{:S(2)}, u32[]{:S(2)}) collective-permute-start(f32[8,2,4,128]{3,0,2,1:T(8,128)S(1)} %fusion.7), channel_id=1, source_target_pairs={{0,1},{1,0},{2,3},{3,2},{4,5},{5,4},{6,7},{7,6},{8,9},{9,8},{10,11... | collective-permute-start | bytes 98312 | tf_op jit(solution)/shard_map/ppermute | solution.py:140
  54.0 3.9 %collective-permute-start.1 = (f32[8,2,4,128]{3,0,2,1:T(8,128)S(1)}, f32[8,2,4,128]{3,0,2,1:T(8,128)S(1)}, u32[]{:S(2)}, u32[]{:S(2)}) collective-permute-start(f32[8,2,4,128]{3,0,2,1:T(8,128)S(1)} %add.145), channel_id=1, source_target_pairs={{0,2},{1,3},{2,0},{3,1},{4,6},{5,7},{6,4},{7,5},{8,10},{9,11},{10,... | collective-permute-start | bytes 98312 | tf_op jit(solution)/shard_map/ppermute | solution.py:140
  58.9 13.3 %all-to-all-start.1 = ((f32[8,2,4,2,256]{4,2,3,1,0:T(4,128)}), f32[8,2,4,2,256]{4,2,3,1,0:T(4,128)S(1)}, u32[]{:S(2)}, u32[]{:S(2)}) async-start(f32[8,2,4,2,256]{4,2,3,1,0:T(4,128)} %fusion.10), calls=%async_computation.1 | async-start | bytes 262144 | tf_op jit(solution)/shard_map/all_to_all | solution.py:232

commit v13 on v11

--- a/solution.py
+++ b/solution.py
@@ -90,7 +90,7 @@
     cache_len = key_value_cache.shape[1]
     width = key_value_cache.shape[3]
     heads = kv_local * group_size
-    rows = 4
+    rows = 8 if row_count % 8 == 0 else row_count
     query_heads = query.reshape(row_count, heads, HEAD)
     opts = dict(rows=rows, kv_local=kv_local, group_size=group_size)
     cache_spec = pl.BlockSpec((rows, cache_len, 2, width), lambda b, *_: (b, 0, 0, 0))

time: 75.9 us -> 74 us (0.975)
  Pallas kernels: 23.9 us -> 22.1 us
    pallas_call x1, Pallas kernels: 12.8 us -> 11 us  [attend(): pl.pallas_call(functools.partial(score_kernel, **opts), out_shape=jax.Sha...]
  transfers between devices with their start and end apart: 4 -> 4, of which waited for: 3 -> 3; matrix products, arithmetic and copies ran while one was open for 11% -> 11% of each run, Pallas kernels for 17% -> 15%
where the time goes in v13:
time: 74 us; the launch traced here: 73.5 us
  Pallas kernels  22.1 us (30%)
  matrix products  10.8 us (15%)
  starting transfers between devices  10.6 us (14%)
  blocking collectives  8.65 us (12%)
  local copies, waits for them, and re-layouts  8.3 us (11%)
  waiting for transfers between devices  6.46 us (9%)
  other arithmetic  5.69 us (8%)
  between operations  0.92 us (1%)
    pallas_call x1, Pallas kernels, attend(): pl.pallas_call(functools.partial(mix_kernel, rows=mix_rows, kv_local=kv_l...  11.1 us
    pallas_call x1, Pallas kernels, attend(): pl.pallas_call(functools.partial(score_kernel, **opts), out_shape=jax.Sha...  11 us
    all_gather x1, blocking collectives, body(): gathered = lax.all_gather(hidden, 'tensor', axis=1, tiled=True)  8.65 us
    all_to_all x1, starting transfers between devices, body(): lax.all_to_all(payload, 'replica', split_axis=0, concat_axis=0, tiled=True)  5.81 us
    dot_general x1, matrix products, body(): jnp.einsum('oksd,adr->oksar', got_rows, adapter_down, preferred_element_t...  5 us
    dot_general x1, matrix products, body(): jnp.einsum('jd,dcw->jcw', normed, key_value_weight, preferred_element_typ...  4.93 us
    all_to_all x1, starting transfers between devices, body(): lax.all_to_all(owner_delta, 'replica', split_axis=0, concat_axis=0, tiled...  3.63 us
    all_to_all x1, waiting for transfers between devices, body(): lax.all_to_all(payload, 'replica', split_axis=0, concat_axis=0, tiled=True)  3.26 us
  transfers between devices with their start and end apart: 4, of which 3 were waited for; matrix products, arithmetic and copies ran while one was open for 11% of the time, Pallas kernels for 15%

profile of v13, /device:TPU:0, one launch (start us, length us, event | category | flops | bytes accessed | tf_op | source)
XLA Modules:
  0.0 73.5 jit_solution(16544585217257780413)
XLA Ops:
  0.7 0.8 %fusion.22 = s32[16]{0:T(128)S(1)} fusion(s32[1,16]{1,0:T(1,128)} %param.17), kind=kLoop, calls=%fused_computation.78 | loop fusion | flops 240 | bytes 128 | tf_op jit(solution)/shard_map/eq | solution.py:179
  1.4 0.7 and_select_fusion.2
  2.9 1.3 %gather_fusion = s32[16]{0:T(128)S(1)} fusion(s32[16]{0:T(128)} %bitcast.77, s32[1024]{0:T(1024)S(1)} %pad_clamp_fusion.4), kind=kCustom, calls=%fused_computation | custom fusion | bytes 192 | tf_op jit(solution)/shard_map/gather | solution.py:191
  4.5 0.7 %copy.59 = s32[16,1]{1,0:T(8,128)S(1)} copy(s32[16,1]{0,1:T(1,128)} %bitcast.78) | data formatting | bytes 128 | tf_op jit(solution)/shard_map/reshape.321
  5.4 0.7 bitcast_subtract_fusion.1
  6.1 0.7 gather_fusion.1
  7.1 8.6 %all_gather.3 = bf16[32,8192]{1,0:T(8,128)(2,1)S(1)} all-gather(bf16[32,2048]{1,0:T(8,128)(2,1)S(1)} %copy-done.1), channel_id=1, replica_groups=mesh['replica'=8,'tensor'=4] {'tensor'}, dimensions={1}, use_global_device_ids=true | all-gather | bytes 655360 | tf_op jit(solution)/shard_map/all_gather | solution.py:157
  16.2 0.7 %gather_fusion.2 = bf16[64,2048]{1,0:T(8,128)(2,1)S(1)} fusion(bf16[32,2048]{1,0:T(8,128)(2,1)S(1)} %constant_dynamic-slice_fusion, s32[1024]{0:T(1024)S(1)} %pad_clamp_fusion.3), kind=kCustom, calls=%fused_computation.2 | custom fusion | bytes 524544 | tf_op jit(solution)/shard_map/gather | solution.py:195
  17.3 0.8 %pad_maximum_fusion = bf16[8,2,4,2176]{3,2,1,0:T(4,128)(2,1)} fusion(bf16[8,2,4,128]{3,2,1,0:T(4,128)(2,1)S(1)} %broadcast_in_dim.54, bf16[8,2,4,2048]{3,2,1,0:T(4,128)(2,1)S(1)} %broadcast_select_fusion), kind=kLoop, calls=%fused_computation.21 | loop fusion | flops 557056 | bytes 557056 | tf_op jit(solution)/shard_map/concatenate | solution.py:200
  18.2 5.8 %all-to-all-start = ((bf16[8,2,4,2176]{3,2,1,0:T(4,128)(2,1)}), bf16[8,2,4,2176]{3,2,1,0:T(4,128)(2,1)S(1)}, u32[]{:S(2)}, u32[]{:S(2)}) async-start(bf16[8,2,4,2176]{3,2,1,0:T(4,128)(2,1)} %pad_maximum_fusion), calls=%async_computation | async-start | bytes 557056 | tf_op jit(solution)/shard_map/all_to_all | solution.py:201
  24.1 0.7 gather_fusion.5
  24.8 0.7 gather_fusion.4
  25.5 4.9 %fusion.2 = f32[32,2,256]{2,0,1:T(8,128)S(1)} fusion(bf16[8192,2,256]{2,1,0:T(2,128)(2,1)} %param.12, bf16[32,8192]{1,0:T(8,128)(2,1)S(1)} %fusion.13), kind=kOutput, calls=%fused_computation.9 | convolution fusion | flops 268435456 | bytes 8978432 | tf_op jit(solution)/shard_map/jd,dcw->jcw/dot_general | solution.py:221
  30.4 3.3 %all-to-all-done = bf16[8,2,4,2176]{3,2,1,0:T(4,128)(2,1)S(1)} async-done(((bf16[8,2,4,2176]{3,2,1,0:T(4,128)(2,1)}), bf16[8,2,4,2176]{3,2,1,0:T(4,128)(2,1)S(1)}, u32[]{:S(2)}, u32[]{:S(2)}) %all-to-all-start) | async-done | bytes 278560 | tf_op jit(solution)/shard_map/all_to_all | solution.py:201
  34.0 5.0 %fusion.7 = f32[8,2,4,128]{3,0,2,1:T(8,128)S(1)} fusion(bf16[16,2048,128]{2,1,0:T(8,128)(2,1)} %param.13, bf16[8,2,4,2048]{3,2,1,0:T(4,128)(2,1)S(1)} %slice.40, pred[8,2,16]{0,2,1:T(8,128)(4,1)S(1)} %iota_compare_fusion), kind=kOutput, calls=%fused_computation.14 | convolution fusion | flops 537124864 | bytes 8683776 | tf_op jit(solution)/shard_map/oksd,adr->oksar/dot_general | solution.py:205
  39.2 1.0 %collective-permute-done = f32[8,2,4,128]{3,0,2,1:T(8,128)S(1)} collective-permute-done((f32[8,2,4,128]{3,0,2,1:T(8,128)S(1)}, f32[8,2,4,128]{3,0,2,1:T(8,128)S(1)}, u32[]{:S(2)}, u32[]{:S(2)}) %collective-permute-start) | collective-permute-done | bytes 32800 | tf_op jit(solution)/shard_map/ppermute | solution.py:132
  40.3 1.1 %collective-permute-start.1 = (f32[8,2,4,128]{3,0,2,1:T(8,128)S(1)}, f32[8,2,4,128]{3,0,2,1:T(8,128)S(1)}, u32[]{:S(2)}, u32[]{:S(2)}) collective-permute-start(f32[8,2,4,128]{3,0,2,1:T(8,128)S(1)} %add.145), channel_id=1, source_target_pairs={{0,2},{1,3},{2,0},{3,1},{4,6},{5,7},{6,4},{7,5},{8,10},{9,11},{10,... | collective-permute-start | bytes 98312 | tf_op jit(solution)/shard_map/ppermute | solution.py:132
  42.0 2.2 %collective-permute-done.1 = f32[8,2,4,128]{3,0,2,1:T(8,128)S(1)} collective-permute-done((f32[8,2,4,128]{3,0,2,1:T(8,128)S(1)}, f32[8,2,4,128]{3,0,2,1:T(8,128)S(1)}, u32[]{:S(2)}, u32[]{:S(2)}) %collective-permute-start.1) | collective-permute-done | bytes 32800 | tf_op jit(solution)/shard_map/ppermute | solution.py:132
  44.3 0.9 %fusion.10 = f32[8,2,4,2,256]{4,2,3,1,0:T(4,128)} fusion(bf16[8,2,2,64,256]{4,3,2,1,0:T(8,128)(2,1)S(1)} %bitcast.79, bf16[8,2,4,2,64]{4,3,0,2,1:T(2,128)(2,1)S(1)} %reshape.345), kind=kOutput, calls=%fused_computation.16 | convolution fusion | flops 4227072 | bytes 1196032 | tf_op jit(solution)/shard_map/okscr,okcrw->okscw/dot_general | solution.py:215
  45.2 3.6 %all-to-all-start.1 = ((f32[8,2,4,2,256]{4,2,3,1,0:T(4,128)}), f32[8,2,4,2,256]{4,2,3,1,0:T(4,128)S(1)}, u32[]{:S(2)}, u32[]{:S(2)}) async-start(f32[8,2,4,2,256]{4,2,3,1,0:T(4,128)} %fusion.10), calls=%async_computation.1 | async-start | bytes 262144 | tf_op jit(solution)/shard_map/all_to_all | solution.py:218
  48.9 0.7 copy.72
  49.5 11.0 %shard_map.113.s_ref = f32[32,16,1024]{2,1,0:T(8,128)} custom-call(s32[32]{0:T(128)} %len_ref.1, bf16[32,16,128]{2,1,0:T(8,128)(2,1)} %bitcast.80, bf16[32,512,2,256]{3,2,1,0:T(2,128)(2,1)} %kv_ref.3), custom_call_target="tpu_custom_call" | custom-call | tf_op jit(solution)/shard_map/pallas_call | solution.py:99
  61.7 0.7 pad_maximum_fusion.1.nkv_ref
  62.4 11.1 %shard_map.114 = bf16[32,2048]{1,0:T(8,128)(2,1)} custom-call(bf16[32,16,128]{2,1,0:T(8,128)(2,1)} %bitcast.81, f32[32,16,1024]{2,1,0:T(8,128)} %shard_map.113.s_ref, bf16[32,512,2,256]{3,2,1,0:T(2,128)(2,1)} %kv_ref.3, bf16[32,2,256]{2,1,0:T(2,128)(2,1)} %pad_maximum_fusion.1.nkv_ref), custom_call_target="tpu_custom_call" | custom-call | tf_op jit(solution)/shard_map/pallas_call | solution.py:110
  (71 shorter events, 4.9 us)
Async XLA Ops:
  0.6 40.7 %copy-start = (bf16[16,2,64,256]{3,2,1,0:T(8,128)(2,1)S(1)}, bf16[16,2,64,256]{3,2,1,0:T(8,128)(2,1)}, u32[]{:S(2)}) copy-start(bf16[16,2,64,256]{3,2,1,0:T(8,128)(2,1)} %param.14) | copy-start | bytes 3145732
  0.6 6.4 %copy-start.1 = (bf16[32,2048]{1,0:T(8,128)(2,1)S(1)}, bf16[32,2048]{1,0:T(8,128)(2,1)}, u32[]{:S(2)}) copy-start(bf16[32,2048]{1,0:T(8,128)(2,1)} %param.10) | copy-start | bytes 393220
  0.7 15.3 %copy-start.3 = (f32[8192]{0:T(1024)S(1)}, f32[8192]{0:T(1024)}, u32[]{:S(2)}) copy-start(f32[8192]{0:T(1024)} %param.11) | copy-start | bytes 98308
  18.2 15.5 %all-to-all-start = ((bf16[8,2,4,2176]{3,2,1,0:T(4,128)(2,1)}), bf16[8,2,4,2176]{3,2,1,0:T(4,128)(2,1)S(1)}, u32[]{:S(2)}, u32[]{:S(2)}) async-start(bf16[8,2,4,2176]{3,2,1,0:T(4,128)(2,1)} %pad_maximum_fusion), calls=%async_computation | async-start | bytes 557056 | tf_op jit(solution)/shard_map/all_to_all | solution.py:201
  33.9 14.9 %copy-start.4 = (s32[32]{0:T(128)S(1)}, s32[32]{0:T(128)}, u32[]{:S(2)}) copy-start(s32[32]{0:T(128)} %len_ref.1) | copy-start | bytes 388
  34.0 14.9 %copy-start.2 = (bf16[32,2048]{1,0:T(8,128)(2,1)S(1)}, bf16[32,2048]{1,0:T(8,128)(2,1)}, u32[]{:S(2)}) copy-start(bf16[32,2048]{1,0:T(8,128)(2,1)} %param.15) | copy-start | bytes 393220
  39.0 1.3 %collective-permute-start = (f32[8,2,4,128]{3,0,2,1:T(8,128)S(1)}, f32[8,2,4,128]{3,0,2,1:T(8,128)S(1)}, u32[]{:S(2)}, u32[]{:S(2)}) collective-permute-start(f32[8,2,4,128]{3,0,2,1:T(8,128)S(1)} %fusion.7), channel_id=1, source_target_pairs={{0,1},{1,0},{2,3},{3,2},{4,5},{5,4},{6,7},{7,6},{8,9},{9,8},{10,11... | collective-permute-start | bytes 98312 | tf_op jit(solution)/shard_map/ppermute | solution.py:132
  40.3 3.9 %collective-permute-start.1 = (f32[8,2,4,128]{3,0,2,1:T(8,128)S(1)}, f32[8,2,4,128]{3,0,2,1:T(8,128)S(1)}, u32[]{:S(2)}, u32[]{:S(2)}) collective-permute-start(f32[8,2,4,128]{3,0,2,1:T(8,128)S(1)} %add.145), channel_id=1, source_target_pairs={{0,2},{1,3},{2,0},{3,1},{4,6},{5,7},{6,4},{7,5},{8,10},{9,11},{10,... | collective-permute-start | bytes 98312 | tf_op jit(solution)/shard_map/ppermute | solution.py:132
  45.2 15.4 %all-to-all-start.1 = ((f32[8,2,4,2,256]{4,2,3,1,0:T(4,128)}), f32[8,2,4,2,256]{4,2,3,1,0:T(4,128)S(1)}, u32[]{:S(2)}, u32[]{:S(2)}) async-start(f32[8,2,4,2,256]{4,2,3,1,0:T(4,128)} %fusion.10), calls=%async_computation.1 | async-start | bytes 262144 | tf_op jit(solution)/shard_map/all_to_all | solution.py:218

commit v14 on v13

--- a/solution.py
+++ b/solution.py
@@ -90,7 +90,7 @@
     cache_len = key_value_cache.shape[1]
     width = key_value_cache.shape[3]
     heads = kv_local * group_size
-    rows = 8 if row_count % 8 == 0 else row_count
+    rows = 16 if row_count % 16 == 0 else row_count
     query_heads = query.reshape(row_count, heads, HEAD)
     opts = dict(rows=rows, kv_local=kv_local, group_size=group_size)
     cache_spec = pl.BlockSpec((rows, cache_len, 2, width), lambda b, *_: (b, 0, 0, 0))
@@ -106,7 +106,7 @@
             out_specs=score_spec,
         ),
     )(cached_length, query_heads, key_value_cache)
-    mix_rows = 8 if row_count % 8 == 0 else row_count
+    mix_rows = 16 if row_count % 16 == 0 else row_count
     out = pl.pallas_call(
         functools.partial(mix_kernel, rows=mix_rows, kv_local=kv_local, group_size=group_size),
         out_shape=jax.ShapeDtypeStruct((row_count, heads * HEAD), jnp.bfloat16),

time: 74 us -> 74.2 us (level)
  no operation moved by 1% of the time
where the time goes in v14:
time: 74.2 us; the launch traced here: 73.7 us
  Pallas kernels  22.3 us (30%)
  matrix products  10.8 us (15%)
  starting transfers between devices  10.6 us (14%)
  blocking collectives  8.65 us (12%)
  local copies, waits for them, and re-layouts  8.3 us (11%)
  waiting for transfers between devices  6.46 us (9%)
  other arithmetic  5.69 us (8%)
  between operations  0.92 us (1%)
    pallas_call x1, Pallas kernels, attend(): pl.pallas_call(functools.partial(mix_kernel, rows=mix_rows, kv_local=kv_l...  11.2 us
    pallas_call x1, Pallas kernels, attend(): pl.pallas_call(functools.partial(score_kernel, **opts), out_shape=jax.Sha...  11.1 us
    all_gather x1, blocking collectives, body(): gathered = lax.all_gather(hidden, 'tensor', axis=1, tiled=True)  8.65 us
    all_to_all x1, starting transfers between devices, body(): lax.all_to_all(payload, 'replica', split_axis=0, concat_axis=0, tiled=True)  5.81 us
    dot_general x1, matrix products, body(): jnp.einsum('oksd,adr->oksar', got_rows, adapter_down, preferred_element_t...  5 us
    dot_general x1, matrix products, body(): jnp.einsum('jd,dcw->jcw', normed, key_value_weight, preferred_element_typ...  4.94 us
    all_to_all x1, starting transfers between devices, body(): lax.all_to_all(owner_delta, 'replica', split_axis=0, concat_axis=0, tiled...  3.64 us
    all_to_all x1, waiting for transfers between devices, body(): lax.all_to_all(payload, 'replica', split_axis=0, concat_axis=0, tiled=True)  3.26 us
  transfers between devices with their start and end apart: 4, of which 3 were waited for; matrix products, arithmetic and copies ran while one was open for 11% of the time, Pallas kernels for 15%

profile of v14, /device:TPU:0, one launch (start us, length us, event | category | flops | bytes accessed | tf_op | source)
XLA Modules:
  0.0 73.7 jit_solution(4597684902350459865)
XLA Ops:
  0.7 0.8 %fusion.22 = s32[16]{0:T(128)S(1)} fusion(s32[1,16]{1,0:T(1,128)} %param.17), kind=kLoop, calls=%fused_computation.78 | loop fusion | flops 240 | bytes 128 | tf_op jit(solution)/shard_map/eq | solution.py:179
  1.4 0.7 and_select_fusion.2
  2.9 1.3 %gather_fusion = s32[16]{0:T(128)S(1)} fusion(s32[16]{0:T(128)} %bitcast.77, s32[1024]{0:T(1024)S(1)} %pad_clamp_fusion.4), kind=kCustom, calls=%fused_computation | custom fusion | bytes 192 | tf_op jit(solution)/shard_map/gather | solution.py:191
  4.5 0.7 copy.59
  5.4 0.7 bitcast_subtract_fusion.1
  6.1 0.7 gather_fusion.1
  7.1 8.6 %all_gather.3 = bf16[32,8192]{1,0:T(8,128)(2,1)S(1)} all-gather(bf16[32,2048]{1,0:T(8,128)(2,1)S(1)} %copy-done.1), channel_id=1, replica_groups=mesh['replica'=8,'tensor'=4] {'tensor'}, dimensions={1}, use_global_device_ids=true | all-gather | bytes 655360 | tf_op jit(solution)/shard_map/all_gather | solution.py:157
  16.2 0.7 %gather_fusion.2 = bf16[64,2048]{1,0:T(8,128)(2,1)S(1)} fusion(bf16[32,2048]{1,0:T(8,128)(2,1)S(1)} %constant_dynamic-slice_fusion, s32[1024]{0:T(1024)S(1)} %pad_clamp_fusion.3), kind=kCustom, calls=%fused_computation.2 | custom fusion | bytes 524544 | tf_op jit(solution)/shard_map/gather | solution.py:195
  17.3 0.8 %pad_maximum_fusion = bf16[8,2,4,2176]{3,2,1,0:T(4,128)(2,1)} fusion(bf16[8,2,4,128]{3,2,1,0:T(4,128)(2,1)S(1)} %broadcast_in_dim.54, bf16[8,2,4,2048]{3,2,1,0:T(4,128)(2,1)S(1)} %broadcast_select_fusion), kind=kLoop, calls=%fused_computation.21 | loop fusion | flops 557056 | bytes 557056 | tf_op jit(solution)/shard_map/concatenate | solution.py:200
  18.2 5.8 %all-to-all-start = ((bf16[8,2,4,2176]{3,2,1,0:T(4,128)(2,1)}), bf16[8,2,4,2176]{3,2,1,0:T(4,128)(2,1)S(1)}, u32[]{:S(2)}, u32[]{:S(2)}) async-start(bf16[8,2,4,2176]{3,2,1,0:T(4,128)(2,1)} %pad_maximum_fusion), calls=%async_computation | async-start | bytes 557056 | tf_op jit(solution)/shard_map/all_to_all | solution.py:201
  24.1 0.7 gather_fusion.5
  24.8 0.7 gather_fusion.4
  25.5 4.9 %fusion.2 = f32[32,2,256]{2,0,1:T(8,128)S(1)} fusion(bf16[8192,2,256]{2,1,0:T(2,128)(2,1)} %param.12, bf16[32,8192]{1,0:T(8,128)(2,1)S(1)} %fusion.13), kind=kOutput, calls=%fused_computation.9 | convolution fusion | flops 268435456 | bytes 8978432 | tf_op jit(solution)/shard_map/jd,dcw->jcw/dot_general | solution.py:221
  30.4 3.3 %all-to-all-done = bf16[8,2,4,2176]{3,2,1,0:T(4,128)(2,1)S(1)} async-done(((bf16[8,2,4,2176]{3,2,1,0:T(4,128)(2,1)}), bf16[8,2,4,2176]{3,2,1,0:T(4,128)(2,1)S(1)}, u32[]{:S(2)}, u32[]{:S(2)}) %all-to-all-start) | async-done | bytes 278560 | tf_op jit(solution)/shard_map/all_to_all | solution.py:201
  34.0 5.0 %fusion.7 = f32[8,2,4,128]{3,0,2,1:T(8,128)S(1)} fusion(bf16[16,2048,128]{2,1,0:T(8,128)(2,1)} %param.13, bf16[8,2,4,2048]{3,2,1,0:T(4,128)(2,1)S(1)} %slice.40, pred[8,2,16]{0,2,1:T(8,128)(4,1)S(1)} %iota_compare_fusion), kind=kOutput, calls=%fused_computation.14 | convolution fusion | flops 537124864 | bytes 8683776 | tf_op jit(solution)/shard_map/oksd,adr->oksar/dot_general | solution.py:205
  39.2 1.0 %collective-permute-done = f32[8,2,4,128]{3,0,2,1:T(8,128)S(1)} collective-permute-done((f32[8,2,4,128]{3,0,2,1:T(8,128)S(1)}, f32[8,2,4,128]{3,0,2,1:T(8,128)S(1)}, u32[]{:S(2)}, u32[]{:S(2)}) %collective-permute-start) | collective-permute-done | bytes 32800 | tf_op jit(solution)/shard_map/ppermute | solution.py:132
  40.3 1.1 %collective-permute-start.1 = (f32[8,2,4,128]{3,0,2,1:T(8,128)S(1)}, f32[8,2,4,128]{3,0,2,1:T(8,128)S(1)}, u32[]{:S(2)}, u32[]{:S(2)}) collective-permute-start(f32[8,2,4,128]{3,0,2,1:T(8,128)S(1)} %add.145), channel_id=1, source_target_pairs={{0,2},{1,3},{2,0},{3,1},{4,6},{5,7},{6,4},{7,5},{8,10},{9,11},{10,... | collective-permute-start | bytes 98312 | tf_op jit(solution)/shard_map/ppermute | solution.py:132
  42.0 2.2 %collective-permute-done.1 = f32[8,2,4,128]{3,0,2,1:T(8,128)S(1)} collective-permute-done((f32[8,2,4,128]{3,0,2,1:T(8,128)S(1)}, f32[8,2,4,128]{3,0,2,1:T(8,128)S(1)}, u32[]{:S(2)}, u32[]{:S(2)}) %collective-permute-start.1) | collective-permute-done | bytes 32800 | tf_op jit(solution)/shard_map/ppermute | solution.py:132
  44.3 0.9 %fusion.10 = f32[8,2,4,2,256]{4,2,3,1,0:T(4,128)} fusion(bf16[8,2,2,64,256]{4,3,2,1,0:T(8,128)(2,1)S(1)} %bitcast.79, bf16[8,2,4,2,64]{4,3,0,2,1:T(2,128)(2,1)S(1)} %reshape.345), kind=kOutput, calls=%fused_computation.16 | convolution fusion | flops 4227072 | bytes 1196032 | tf_op jit(solution)/shard_map/okscr,okcrw->okscw/dot_general | solution.py:215
  45.2 3.6 %all-to-all-start.1 = ((f32[8,2,4,2,256]{4,2,3,1,0:T(4,128)}), f32[8,2,4,2,256]{4,2,3,1,0:T(4,128)S(1)}, u32[]{:S(2)}, u32[]{:S(2)}) async-start(f32[8,2,4,2,256]{4,2,3,1,0:T(4,128)} %fusion.10), calls=%async_computation.1 | async-start | bytes 262144 | tf_op jit(solution)/shard_map/all_to_all | solution.py:218
  48.9 0.7 copy.72
  49.5 11.1 %shard_map.113.s_ref = f32[32,16,1024]{2,1,0:T(8,128)} custom-call(s32[32]{0:T(128)} %len_ref.1, bf16[32,16,128]{2,1,0:T(8,128)(2,1)} %bitcast.80, bf16[32,512,2,256]{3,2,1,0:T(2,128)(2,1)} %kv_ref.3), custom_call_target="tpu_custom_call" | custom-call | tf_op jit(solution)/shard_map/pallas_call | solution.py:99
  61.8 0.7 pad_maximum_fusion.1.nkv_ref
  62.5 11.2 %shard_map.114 = bf16[32,2048]{1,0:T(8,128)(2,1)} custom-call(bf16[32,16,128]{2,1,0:T(8,128)(2,1)} %bitcast.81, f32[32,16,1024]{2,1,0:T(8,128)} %shard_map.113.s_ref, bf16[32,512,2,256]{3,2,1,0:T(2,128)(2,1)} %kv_ref.3, bf16[32,2,256]{2,1,0:T(2,128)(2,1)} %pad_maximum_fusion.1.nkv_ref), custom_call_target="tpu_custom_call" | custom-call | tf_op jit(solution)/shard_map/pallas_call | solution.py:110
  (71 shorter events, 4.9 us)
Async XLA Ops:
  0.6 40.7 %copy-start = (bf16[16,2,64,256]{3,2,1,0:T(8,128)(2,1)S(1)}, bf16[16,2,64,256]{3,2,1,0:T(8,128)(2,1)}, u32[]{:S(2)}) copy-start(bf16[16,2,64,256]{3,2,1,0:T(8,128)(2,1)} %param.14) | copy-start | bytes 3145732
  0.6 6.4 %copy-start.1 = (bf16[32,2048]{1,0:T(8,128)(2,1)S(1)}, bf16[32,2048]{1,0:T(8,128)(2,1)}, u32[]{:S(2)}) copy-start(bf16[32,2048]{1,0:T(8,128)(2,1)} %param.10) | copy-start | bytes 393220
  0.7 15.3 %copy-start.3 = (f32[8192]{0:T(1024)S(1)}, f32[8192]{0:T(1024)}, u32[]{:S(2)}) copy-start(f32[8192]{0:T(1024)} %param.11) | copy-start | bytes 98308
  18.2 15.5 %all-to-all-start = ((bf16[8,2,4,2176]{3,2,1,0:T(4,128)(2,1)}), bf16[8,2,4,2176]{3,2,1,0:T(4,128)(2,1)S(1)}, u32[]{:S(2)}, u32[]{:S(2)}) async-start(bf16[8,2,4,2176]{3,2,1,0:T(4,128)(2,1)} %pad_maximum_fusion), calls=%async_computation | async-start | bytes 557056 | tf_op jit(solution)/shard_map/all_to_all | solution.py:201
  33.9 14.9 %copy-start.4 = (s32[32]{0:T(128)S(1)}, s32[32]{0:T(128)}, u32[]{:S(2)}) copy-start(s32[32]{0:T(128)} %len_ref.1) | copy-start | bytes 388
  34.0 14.9 %copy-start.2 = (bf16[32,2048]{1,0:T(8,128)(2,1)S(1)}, bf16[32,2048]{1,0:T(8,128)(2,1)}, u32[]{:S(2)}) copy-start(bf16[32,2048]{1,0:T(8,128)(2,1)} %param.15) | copy-start | bytes 393220
  39.0 1.3 %collective-permute-start = (f32[8,2,4,128]{3,0,2,1:T(8,128)S(1)}, f32[8,2,4,128]{3,0,2,1:T(8,128)S(1)}, u32[]{:S(2)}, u32[]{:S(2)}) collective-permute-start(f32[8,2,4,128]{3,0,2,1:T(8,128)S(1)} %fusion.7), channel_id=1, source_target_pairs={{0,1},{1,0},{2,3},{3,2},{4,5},{5,4},{6,7},{7,6},{8,9},{9,8},{10,11... | collective-permute-start | bytes 98312 | tf_op jit(solution)/shard_map/ppermute | solution.py:132
  40.3 3.9 %collective-permute-start.1 = (f32[8,2,4,128]{3,0,2,1:T(8,128)S(1)}, f32[8,2,4,128]{3,0,2,1:T(8,128)S(1)}, u32[]{:S(2)}, u32[]{:S(2)}) collective-permute-start(f32[8,2,4,128]{3,0,2,1:T(8,128)S(1)} %add.145), channel_id=1, source_target_pairs={{0,2},{1,3},{2,0},{3,1},{4,6},{5,7},{6,4},{7,5},{8,10},{9,11},{10,... | collective-permute-start | bytes 98312 | tf_op jit(solution)/shard_map/ppermute | solution.py:132
  45.2 15.6 %all-to-all-start.1 = ((f32[8,2,4,2,256]{4,2,3,1,0:T(4,128)}), f32[8,2,4,2,256]{4,2,3,1,0:T(4,128)S(1)}, u32[]{:S(2)}, u32[]{:S(2)}) async-start(f32[8,2,4,2,256]{4,2,3,1,0:T(4,128)} %fusion.10), calls=%async_computation.1 | async-start | bytes 262144 | tf_op jit(solution)/shard_map/all_to_all | solution.py:218

commit v15 on v13

--- a/solution.py
+++ b/solution.py
@@ -134,6 +134,24 @@
     return value
 
 
+def butterfly_gather(value, axis):
+    size = lax.axis_size(axis)
+    if size & (size - 1):
+        return lax.all_gather(value, axis, axis=1, tiled=True)
+    index = lax.axis_index(axis)
+    stride = 1
+    while stride < size:
+        pairs = [(i, i ^ stride) for i in range(size)]
+        other = lax.ppermute(value, axis, pairs)
+        value = jnp.where(
+            (index & stride) == 0,
+            jnp.concatenate([value, other], axis=1),
+            jnp.concatenate([other, value], axis=1),
+        )
+        stride *= 2
+    return value
+
+
 def body(
     hidden,
     input_norm_gain,
@@ -154,16 +172,15 @@
     adapter_rank_size = adapter_up.shape[2]
     replicas = lax.axis_size("replica")
     segments = segment_sizes.shape[1]
-    gathered = lax.all_gather(hidden, "tensor", axis=1, tiled=True)
-    widened = gathered.astype(jnp.float32)
-    normed = (
-        widened
-        * lax.rsqrt(jnp.mean(widened * widened, axis=1, keepdims=True) + EPSILON)
-        * input_norm_gain
-    ).astype(jnp.bfloat16)
-    own_cols = lax.dynamic_slice_in_dim(
-        normed, lax.axis_index("tensor") * part_width, part_width, 1
-    )
+    local = hidden.astype(jnp.float32)
+    squares = butterfly_sum(jnp.sum(local * local, axis=1, keepdims=True), "tensor")
+    row_scale = lax.rsqrt(squares / (part_width * lax.axis_size("tensor")) + EPSILON)
+    own_gain = lax.dynamic_slice_in_dim(
+        input_norm_gain, lax.axis_index("tensor") * part_width, part_width, 0
+    )
+    own_cols = (local * row_scale * own_gain).astype(jnp.bfloat16)
+    gathered = butterfly_gather(hidden, "tensor")
+    normed = (gathered.astype(jnp.float32) * row_scale * input_norm_gain).astype(jnp.bfloat16)
     seg_counts = segment_sizes[0]
     adapters = segment_adapter[0]
     seg_ends = jnp.cumsum(seg_counts, dtype=jnp.int32)

time: 74 us -> 75.5 us (1.020)
  blocking collectives: 8.65 us -> 0 us
  starting transfers between devices: 10.6 us -> 18.1 us
  other arithmetic: 5.69 us -> 7.06 us
  waiting for transfers between devices: 6.46 us -> 7.64 us
    all_gather x1 -> x0, blocking collectives: 8.65 us -> none  [body(): gathered = lax.all_gather(hidden, 'tensor', axis=1, tiled=True)]
    all_to_all x1, waiting for transfers between devices: 3.26 us -> 0.01 us  [body(): lax.all_to_all(payload, 'replica', split_axis=0, concat_axis=0, tiled=True)]
    ppermute x2 -> x4, starting transfers between devices: 1.17 us -> 3.71 us  [butterfly_sum(): value = value + lax.ppermute(value, axis, pairs)]
    all_to_all x1, starting transfers between devices: 3.63 us -> 6 us  [body(): lax.all_to_all(owner_delta, 'replica', split_axis=0, concat_axis=0, tiled...]
    all_to_all x1, waiting for transfers between devices: 0.01 us -> 2.32 us  [body(): lax.all_to_all(owner_delta, 'replica', split_axis=0, concat_axis=0, tiled...]
    ppermute x2 -> x4, waiting for transfers between devices: 3.2 us -> 5.31 us  [butterfly_sum(): value = value + lax.ppermute(value, axis, pairs)]
    ppermute x0 -> x2, starting transfers between devices: none -> 2.1 us  [butterfly_gather(): other = lax.ppermute(value, axis, pairs)]
    reduce_sum x1, other arithmetic: 0.24 us -> 1.04 us  [body(): jnp.sum(local * local, axis=1, keepdims=True)]
  transfers between devices with their start and end apart: 4 -> 8, of which waited for: 3 -> 4; matrix products, arithmetic and copies ran while one was open for 11% -> 33% of each run, Pallas kernels for 15% -> 15%
where the time goes in v15:
time: 75.5 us; the launch traced here: 75 us
  Pallas kernels  22.1 us (29%)
  starting transfers between devices  18.1 us (24%)
  matrix products  10.9 us (14%)
  local copies, waits for them, and re-layouts  8.28 us (11%)
  waiting for transfers between devices  7.64 us (10%)
  other arithmetic  7.06 us (9%)
  between operations  0.91 us (1%)
    pallas_call x1, Pallas kernels, attend(): pl.pallas_call(functools.partial(mix_kernel, rows=mix_rows, kv_local=kv_l...  11.1 us
    pallas_call x1, Pallas kernels, attend(): pl.pallas_call(functools.partial(score_kernel, **opts), out_shape=jax.Sha...  11 us
    all_to_all x1, starting transfers between devices, body(): lax.all_to_all(payload, 'replica', split_axis=0, concat_axis=0, tiled=True)  6.31 us
    all_to_all x1, starting transfers between devices, body(): lax.all_to_all(owner_delta, 'replica', split_axis=0, concat_axis=0, tiled...  6 us
    ppermute x4, waiting for transfers between devices, butterfly_sum(): value = value + lax.ppermute(value, axis, pairs)  5.31 us
    dot_general x1, matrix products, body(): jnp.einsum('jd,dcw->jcw', normed, key_value_weight, preferred_element_typ...  5.02 us
    dot_general x1, matrix products, body(): jnp.einsum('oksd,adr->oksar', got_rows, adapter_down, preferred_element_t...  4.98 us
    ppermute x4, starting transfers between devices, butterfly_sum(): value = value + lax.ppermute(value, axis, pairs)  3.71 us
  transfers between devices with their start and end apart: 8, of which 4 were waited for; matrix products, arithmetic and copies ran while one was open for 33% of the time, Pallas kernels for 15%

profile of v15, /device:TPU:0, one launch (start us, length us, event | category | flops | bytes accessed | tf_op | source)
XLA Modules:
  0.0 75.0 jit_solution(3047724974931093788)
XLA Ops:
  1.2 1.0 %fusion.21 = f32[32]{0:T(128)S(1)} fusion(bf16[32,2048]{1,0:T(8,128)(2,1)} %param.10), kind=kLoop, calls=%fused_computation.29 | loop fusion | flops 196576 | bytes 131200 | tf_op jit(solution)/shard_map/reduce_sum | solution.py:176
  2.4 0.7 fusion.31
  3.1 0.7 and_select_fusion.2
  4.0 0.7 copy.59
  6.8 1.3 %gather_fusion = s32[16]{0:T(128)S(1)} fusion(s32[16]{0:T(128)} %bitcast.82, s32[1024]{0:T(1024)S(1)} %pad_clamp_fusion.4), kind=kCustom, calls=%fused_computation | custom fusion | bytes 192 | tf_op jit(solution)/shard_map/gather | solution.py:208
  9.1 0.7 gather_fusion.5
  9.8 0.7 gather_fusion.4
  11.1 2.9 %collective-permute-start.3 = (f32[32,1]{0,1:T(1,128)S(1)}, f32[32,1]{0,1:T(1,128)S(1)}, u32[]{:S(2)}, u32[]{:S(2)}) collective-permute-start(f32[32,1]{0,1:T(1,128)S(1)} %bitcast_add_fusion), channel_id=1, source_target_pairs={{0,2},{1,3},{2,0},{3,1},{4,6},{5,7},{6,4},{7,5},{8,10},{9,11},{10,... | collective-permute-start | bytes 392 | tf_op jit(solution)/shard_map/ppermute | solution.py:132
  14.0 1.5 %collective-permute-done.3 = f32[32,1]{0,1:T(1,128)S(1)} collective-permute-done((f32[32,1]{0,1:T(1,128)S(1)}, f32[32,1]{0,1:T(1,128)S(1)}, u32[]{:S(2)}, u32[]{:S(2)}) %collective-permute-start.3) | collective-permute-done | bytes 160 | tf_op jit(solution)/shard_map/ppermute | solution.py:132
  15.6 0.7 gather_fusion.2
  16.8 0.9 %pad_maximum_fusion = bf16[8,2,4,2176]{3,2,1,0:T(4,128)(2,1)} fusion(bf16[8,2,4,128]{3,2,1,0:T(4,128)(2,1)S(1)} %broadcast_in_dim.61, bf16[8,2,4,2048]{3,2,1,0:T(4,128)(2,1)S(1)} %broadcast_select_fusion), kind=kLoop, calls=%fused_computation.28 | loop fusion | flops 557056 | bytes 557056 | tf_op jit(solution)/shard_map/concatenate | solution.py:217
  17.7 6.3 %all-to-all-start = ((bf16[8,2,4,2176]{3,2,1,0:T(4,128)(2,1)}), bf16[8,2,4,2176]{3,2,1,0:T(4,128)(2,1)S(1)}, u32[]{:S(2)}, u32[]{:S(2)}) async-start(bf16[8,2,4,2176]{3,2,1,0:T(4,128)(2,1)} %pad_maximum_fusion), calls=%async_computation | async-start | bytes 557056 | tf_op jit(solution)/shard_map/all_to_all | solution.py:218
  24.0 0.7 copy.72
  24.7 11.0 %shard_map.113.s_ref = f32[32,16,1024]{2,1,0:T(8,128)} custom-call(s32[32]{0:T(128)} %len_ref.1, bf16[32,16,128]{2,1,0:T(8,128)(2,1)} %bitcast.84, bf16[32,512,2,256]{3,2,1,0:T(2,128)(2,1)} %kv_ref.3), custom_call_target="tpu_custom_call" | custom-call | tf_op jit(solution)/shard_map/pallas_call | solution.py:99
  35.7 1.6 %collective-permute-start.1 = (bf16[32,4096]{1,0:T(8,128)(2,1)S(1)}, bf16[32,4096]{1,0:T(8,128)(2,1)S(1)}, u32[]{:S(2)}, u32[]{:S(2)}) collective-permute-start(bf16[32,4096]{1,0:T(8,128)(2,1)S(1)} %maximum_select_fusion.2), channel_id=1, source_target_pairs={{0,2},{1,3},{2,0},{3,1},{4,6},{5,7},{6,4},{7,5},{8,10},{9,11},{10,... | collective-permute-start | bytes 786440 | tf_op jit(solution)/shard_map/ppermute | solution.py:145
  37.5 5.0 %fusion.7 = f32[8,2,4,128]{3,0,2,1:T(8,128)S(1)} fusion(bf16[16,2048,128]{2,1,0:T(8,128)(2,1)} %param.13, bf16[8,2,4,2048]{3,2,1,0:T(4,128)(2,1)S(1)} %slice.40, pred[8,2,16]{0,2,1:T(8,128)(4,1)S(1)} %iota_compare_fusion), kind=kOutput, calls=%fused_computation.12 | convolution fusion | flops 537124864 | bytes 8683776 | tf_op jit(solution)/shard_map/oksd,adr->oksar/dot_general | solution.py:222
  42.8 1.0 %collective-permute-done.4 = f32[8,2,4,128]{3,0,2,1:T(8,128)S(1)} collective-permute-done((f32[8,2,4,128]{3,0,2,1:T(8,128)S(1)}, f32[8,2,4,128]{3,0,2,1:T(8,128)S(1)}, u32[]{:S(2)}, u32[]{:S(2)}) %collective-permute-start.4) | collective-permute-done | bytes 32800 | tf_op jit(solution)/shard_map/ppermute | solution.py:132
  44.9 2.8 %collective-permute-done.5 = f32[8,2,4,128]{3,0,2,1:T(8,128)S(1)} collective-permute-done((f32[8,2,4,128]{3,0,2,1:T(8,128)S(1)}, f32[8,2,4,128]{3,0,2,1:T(8,128)S(1)}, u32[]{:S(2)}, u32[]{:S(2)}) %collective-permute-start.5) | collective-permute-done | bytes 32800 | tf_op jit(solution)/shard_map/ppermute | solution.py:132
  47.8 0.9 %fusion.10 = f32[8,2,4,2,256]{4,2,3,1,0:T(4,128)} fusion(bf16[8,2,2,64,256]{4,3,2,1,0:T(8,128)(2,1)S(1)} %bitcast.83, bf16[8,2,4,2,64]{4,3,0,2,1:T(2,128)(2,1)S(1)} %reshape.338), kind=kOutput, calls=%fused_computation.14 | convolution fusion | flops 4227072 | bytes 1196032 | tf_op jit(solution)/shard_map/okscr,okcrw->okscw/dot_general | solution.py:232
  48.7 6.0 %all-to-all-start.1 = ((f32[8,2,4,2,256]{4,2,3,1,0:T(4,128)}), f32[8,2,4,2,256]{4,2,3,1,0:T(4,128)S(1)}, u32[]{:S(2)}, u32[]{:S(2)}) async-start(f32[8,2,4,2,256]{4,2,3,1,0:T(4,128)} %fusion.10), calls=%async_computation.1 | async-start | bytes 262144 | tf_op jit(solution)/shard_map/all_to_all | solution.py:235
  54.7 5.0 %fusion.2 = f32[32,2,256]{2,0,1:T(8,128)S(1)} fusion(bf16[8192,2,256]{2,1,0:T(2,128)(2,1)} %param.12, bf16[32,4096]{1,0:T(8,128)(2,1)S(1)} %collective-permute-done.1, bf16[32,4096]{1,0:T(8,128)(2,1)S(1)} %maximum_select_fusion.2, f32[8192]{0:T(1024)S(1)} %copy-done.3, f32[32]{0:T(128)S(1)} %rsqrt_bitcast_fusion, pred[]{:T(512)S(6)} %eq.74), kind=kOutput, calls=%fused_computation.9 | convolution fusion | flops 271843328 | bytes 9011329 | tf_op jit(solution)/shard_map/jd,dcw->jcw/dot_general | solution.py:238
  59.7 2.3 %all-to-all-done.1 = f32[8,2,4,2,256]{4,2,3,1,0:T(4,128)S(1)} async-done(((f32[8,2,4,2,256]{4,2,3,1,0:T(4,128)}), f32[8,2,4,2,256]{4,2,3,1,0:T(4,128)S(1)}, u32[]{:S(2)}, u32[]{:S(2)}) %all-to-all-start.1) | async-done | bytes 131104 | tf_op jit(solution)/shard_map/all_to_all | solution.py:235
  63.2 0.7 pad_maximum_fusion.1.nkv_ref
  63.9 11.1 %shard_map.114 = bf16[32,2048]{1,0:T(8,128)(2,1)} custom-call(bf16[32,16,128]{2,1,0:T(8,128)(2,1)} %bitcast.85, f32[32,16,1024]{2,1,0:T(8,128)} %shard_map.113.s_ref, bf16[32,512,2,256]{3,2,1,0:T(2,128)(2,1)} %kv_ref.3, bf16[32,2,256]{2,1,0:T(2,128)(2,1)} %pad_maximum_fusion.1.nkv_ref), custom_call_target="tpu_custom_call" | custom-call | tf_op jit(solution)/shard_map/pallas_call | solution.py:110
  (78 shorter events, 7.8 us)
Async XLA Ops:
  0.6 43.7 %copy-start = (bf16[16,2,64,256]{3,2,1,0:T(8,128)(2,1)S(1)}, bf16[16,2,64,256]{3,2,1,0:T(8,128)(2,1)}, u32[]{:S(2)}) copy-start(bf16[16,2,64,256]{3,2,1,0:T(8,128)(2,1)} %param.14) | copy-start | bytes 3145732
  0.6 14.9 %copy-start.1 = (bf16[32,2048]{1,0:T(8,128)(2,1)S(1)}, bf16[32,2048]{1,0:T(8,128)(2,1)}, u32[]{:S(2)}) copy-start(bf16[32,2048]{1,0:T(8,128)(2,1)} %param.10) | copy-start | bytes 393220
  0.7 13.4 %copy-start.3 = (f32[8192]{0:T(1024)S(1)}, f32[8192]{0:T(1024)}, u32[]{:S(2)}) copy-start(f32[8192]{0:T(1024)} %param.11) | copy-start | bytes 98308
  0.7 23.3 %copy-start.2 = (bf16[32,2048]{1,0:T(8,128)(2,1)S(1)}, bf16[32,2048]{1,0:T(8,128)(2,1)}, u32[]{:S(2)}) copy-start(bf16[32,2048]{1,0:T(8,128)(2,1)} %param.15) | copy-start | bytes 393220
  0.7 34.9 %collective-permute-start = (bf16[32,2048]{1,0:T(8,128)(2,1)}, bf16[32,2048]{1,0:T(8,128)(2,1)S(1)}, u32[]{:S(2)}, u32[]{:S(2)}) collective-permute-start(bf16[32,2048]{1,0:T(8,128)(2,1)} %param.10), channel_id=1, source_target_pairs={{0,1},{1,0},{2,3},{3,2},{4,5},{5,4},{6,7},{7,6},{8,9},{9,8},{10,11... | collective-permute-start | bytes 393224 | tf_op jit(solution)/shard_map/ppermute | solution.py:145
  2.2 8.8 %collective-permute-start.2 = (f32[32,1]{0,1:T(1,128)S(1)}, f32[32,1]{0,1:T(1,128)S(1)}, u32[]{:S(2)}, u32[]{:S(2)}) collective-permute-start(f32[32,1]{0,1:T(1,128)S(1)} %bitcast.89), channel_id=1, source_target_pairs={{0,1},{1,0},{2,3},{3,2},{4,5},{5,4},{6,7},{7,6},{8,9},{9,8},{10,11... | collective-permute-start | bytes 392 | tf_op jit(solution)/shard_map/ppermute | solution.py:132
  11.1 4.4 %collective-permute-start.3 = (f32[32,1]{0,1:T(1,128)S(1)}, f32[32,1]{0,1:T(1,128)S(1)}, u32[]{:S(2)}, u32[]{:S(2)}) collective-permute-start(f32[32,1]{0,1:T(1,128)S(1)} %bitcast_add_fusion), channel_id=1, source_target_pairs={{0,2},{1,3},{2,0},{3,1},{4,6},{5,7},{6,4},{7,5},{8,10},{9,11},{10,... | collective-permute-start | bytes 392 | tf_op jit(solution)/shard_map/ppermute | solution.py:132
  17.7 19.6 %all-to-all-start = ((bf16[8,2,4,2176]{3,2,1,0:T(4,128)(2,1)}), bf16[8,2,4,2176]{3,2,1,0:T(4,128)(2,1)S(1)}, u32[]{:S(2)}, u32[]{:S(2)}) async-start(bf16[8,2,4,2176]{3,2,1,0:T(4,128)(2,1)} %pad_maximum_fusion), calls=%async_computation | async-start | bytes 557056 | tf_op jit(solution)/shard_map/all_to_all | solution.py:218
  35.7 19.0 %collective-permute-start.1 = (bf16[32,4096]{1,0:T(8,128)(2,1)S(1)}, bf16[32,4096]{1,0:T(8,128)(2,1)S(1)}, u32[]{:S(2)}, u32[]{:S(2)}) collective-permute-start(bf16[32,4096]{1,0:T(8,128)(2,1)S(1)} %maximum_select_fusion.2), channel_id=1, source_target_pairs={{0,2},{1,3},{2,0},{3,1},{4,6},{5,7},{6,4},{7,5},{8,10},{9,11},{10,... | collective-permute-start | bytes 786440 | tf_op jit(solution)/shard_map/ppermute | solution.py:145
  42.5 1.3 %collective-permute-start.4 = (f32[8,2,4,128]{3,0,2,1:T(8,128)S(1)}, f32[8,2,4,128]{3,0,2,1:T(8,128)S(1)}, u32[]{:S(2)}, u32[]{:S(2)}) collective-permute-start(f32[8,2,4,128]{3,0,2,1:T(8,128)S(1)} %fusion.7), channel_id=1, source_target_pairs={{0,1},{1,0},{2,3},{3,2},{4,5},{5,4},{6,7},{7,6},{8,9},{9,8},{10,11... | collective-permute-start | bytes 98312 | tf_op jit(solution)/shard_map/ppermute | solution.py:132
  43.8 3.9 %collective-permute-start.5 = (f32[8,2,4,128]{3,0,2,1:T(8,128)S(1)}, f32[8,2,4,128]{3,0,2,1:T(8,128)S(1)}, u32[]{:S(2)}, u32[]{:S(2)}) collective-permute-start(f32[8,2,4,128]{3,0,2,1:T(8,128)S(1)} %add.148), channel_id=1, source_target_pairs={{0,2},{1,3},{2,0},{3,1},{4,6},{5,7},{6,4},{7,5},{8,10},{9,11},{10,... | collective-permute-start | bytes 98312 | tf_op jit(solution)/shard_map/ppermute | solution.py:132
  48.7 13.3 %all-to-all-start.1 = ((f32[8,2,4,2,256]{4,2,3,1,0:T(4,128)}), f32[8,2,4,2,256]{4,2,3,1,0:T(4,128)S(1)}, u32[]{:S(2)}, u32[]{:S(2)}) async-start(f32[8,2,4,2,256]{4,2,3,1,0:T(4,128)} %fusion.10), calls=%async_computation.1 | async-start | bytes 262144 | tf_op jit(solution)/shard_map/all_to_all | solution.py:235

commit v16 on v15

--- a/solution.py
+++ b/solution.py
@@ -179,7 +179,7 @@
         input_norm_gain, lax.axis_index("tensor") * part_width, part_width, 0
     )
     own_cols = (local * row_scale * own_gain).astype(jnp.bfloat16)
-    gathered = butterfly_gather(hidden, "tensor")
+    gathered = lax.all_gather(hidden, "tensor", axis=1, tiled=True)
     normed = (gathered.astype(jnp.float32) * row_scale * input_norm_gain).astype(jnp.bfloat16)
     seg_counts = segment_sizes[0]
     adapters = segment_adapter[0]

time: 75.5 us -> 78.5 us (1.040)
  blocking collectives: 0 us -> 6.87 us
  starting transfers between devices: 18.1 us -> 13.1 us
  waiting for transfers between devices: 7.64 us -> 8.72 us
    all_gather x0 -> x1, blocking collectives: none -> 6.87 us  [body(): gathered = lax.all_gather(hidden, 'tensor', axis=1, tiled=True)]
    all_to_all x1, waiting for transfers between devices: 0.01 us -> 2.57 us  [body(): lax.all_to_all(payload, 'replica', split_axis=0, concat_axis=0, tiled=True)]
    all_to_all x1, starting transfers between devices: 6 us -> 3.64 us  [body(): lax.all_to_all(owner_delta, 'replica', split_axis=0, concat_axis=0, tiled...]
    ppermute x2 -> x0, starting transfers between devices: 2.1 us -> none  [butterfly_gather(): other = lax.ppermute(value, axis, pairs)]
    ppermute x4, waiting for transfers between devices: 5.31 us -> 3.8 us  [butterfly_sum(): value = value + lax.ppermute(value, axis, pairs)]
  transfers between devices with their start and end apart: 8 -> 6, of which waited for: 4 -> 4; matrix products, arithmetic and copies ran while one was open for 33% -> 19% of each run, Pallas kernels for 15% -> 14%
where the time goes in v16:
time: 78.5 us; the launch traced here: 78 us
  Pallas kernels  22.2 us (28%)
  starting transfers between devices  13.1 us (17%)
  matrix products  10.9 us (14%)
  waiting for transfers between devices  8.72 us (11%)
  local copies, waits for them, and re-layouts  8.28 us (11%)
  other arithmetic  7.1 us (9%)
  blocking collectives  6.87 us (9%)
  between operations  0.89 us (1%)
    pallas_call x1, Pallas kernels, attend(): pl.pallas_call(functools.partial(mix_kernel, rows=mix_rows, kv_local=kv_l...  11.1 us
    pallas_call x1, Pallas kernels, attend(): pl.pallas_call(functools.partial(score_kernel, **opts), out_shape=jax.Sha...  11.1 us
    all_gather x1, blocking collectives, body(): gathered = lax.all_gather(hidden, 'tensor', axis=1, tiled=True)  6.87 us
    all_to_all x1, starting transfers between devices, body(): lax.all_to_all(payload, 'replica', split_axis=0, concat_axis=0, tiled=True)  5.81 us
    dot_general x1, matrix products, body(): jnp.einsum('jd,dcw->jcw', normed, key_value_weight, preferred_element_typ...  4.98 us
    dot_general x1, matrix products, body(): jnp.einsum('oksd,adr->oksar', got_rows, adapter_down, preferred_element_t...  4.96 us
    ppermute x4, waiting for transfers between devices, butterfly_sum(): value = value + lax.ppermute(value, axis, pairs)  3.8 us
    all_to_all x1, starting transfers between devices, body(): lax.all_to_all(owner_delta, 'replica', split_axis=0, concat_axis=0, tiled...  3.64 us
  transfers between devices with their start and end apart: 6, of which 4 were waited for; matrix products, arithmetic and copies ran while one was open for 19% of the time, Pallas kernels for 14%

profile of v16, /device:TPU:0, one launch (start us, length us, event | category | flops | bytes accessed | tf_op | source)
XLA Modules:
  0.0 78.0 jit_solution(11127313706236841759)
XLA Ops:
  0.7 1.1 %fusion.15 = f32[32]{0:T(128)S(1)} fusion(bf16[32,2048]{1,0:T(8,128)(2,1)} %param.10), kind=kLoop, calls=%fused_computation.22 | loop fusion | flops 196576 | bytes 131200 | tf_op jit(solution)/shard_map/reduce_sum | solution.py:176
  2.3 0.7 fusion.25
  3.0 0.7 and_select_fusion.2
  3.9 0.7 copy.59
  6.7 1.3 %gather_fusion = s32[16]{0:T(128)S(1)} fusion(s32[16]{0:T(128)} %bitcast.82, s32[1024]{0:T(1024)S(1)} %pad_clamp_fusion.4), kind=kCustom, calls=%fused_computation | custom fusion | bytes 192 | tf_op jit(solution)/shard_map/gather | solution.py:208
  9.1 0.7 gather_fusion.5
  9.8 0.7 gather_fusion.4
  10.8 0.7 copy.72
  11.5 2.5 %collective-permute-start.1 = (f32[32,1]{0,1:T(1,128)S(1)}, f32[32,1]{0,1:T(1,128)S(1)}, u32[]{:S(2)}, u32[]{:S(2)}) collective-permute-start(f32[32,1]{0,1:T(1,128)S(1)} %bitcast_add_fusion), channel_id=1, source_target_pairs={{0,2},{1,3},{2,0},{3,1},{4,6},{5,7},{6,4},{7,5},{8,10},{9,11},{10,... | collective-permute-start | bytes 392 | tf_op jit(solution)/shard_map/ppermute | solution.py:132
  14.0 11.1 %shard_map.113.s_ref = f32[32,16,1024]{2,1,0:T(8,128)} custom-call(s32[32]{0:T(128)} %len_ref.1, bf16[32,16,128]{2,1,0:T(8,128)(2,1)} %bitcast.84, bf16[32,512,2,256]{3,2,1,0:T(2,128)(2,1)} %kv_ref.3), custom_call_target="tpu_custom_call" | custom-call | tf_op jit(solution)/shard_map/pallas_call | solution.py:99
  25.3 0.7 gather_fusion.2
  26.4 0.9 %pad_maximum_fusion = bf16[8,2,4,2176]{3,2,1,0:T(4,128)(2,1)} fusion(bf16[8,2,4,128]{3,2,1,0:T(4,128)(2,1)S(1)} %broadcast_in_dim.61, bf16[8,2,4,2048]{3,2,1,0:T(4,128)(2,1)S(1)} %broadcast_select_fusion), kind=kLoop, calls=%fused_computation.21 | loop fusion | flops 557056 | bytes 557056 | tf_op jit(solution)/shard_map/concatenate | solution.py:217
  27.3 5.8 %all-to-all-start = ((bf16[8,2,4,2176]{3,2,1,0:T(4,128)(2,1)}), bf16[8,2,4,2176]{3,2,1,0:T(4,128)(2,1)S(1)}, u32[]{:S(2)}, u32[]{:S(2)}) async-start(bf16[8,2,4,2176]{3,2,1,0:T(4,128)(2,1)} %pad_maximum_fusion), calls=%async_computation | async-start | bytes 557056 | tf_op jit(solution)/shard_map/all_to_all | solution.py:218
  33.1 6.9 %all_gather.3 = bf16[32,8192]{1,0:T(8,128)(2,1)S(1)} all-gather(bf16[32,2048]{1,0:T(8,128)(2,1)S(1)} %copy-done.1), channel_id=1, replica_groups=mesh['replica'=8,'tensor'=4] {'tensor'}, dimensions={1}, use_global_device_ids=true | all-gather | bytes 655360 | tf_op jit(solution)/shard_map/all_gather | solution.py:182
  40.1 2.6 %all-to-all-done = bf16[8,2,4,2176]{3,2,1,0:T(4,128)(2,1)S(1)} async-done(((bf16[8,2,4,2176]{3,2,1,0:T(4,128)(2,1)}), bf16[8,2,4,2176]{3,2,1,0:T(4,128)(2,1)S(1)}, u32[]{:S(2)}, u32[]{:S(2)}) %all-to-all-start) | async-done | bytes 278560 | tf_op jit(solution)/shard_map/all_to_all | solution.py:218
  42.9 5.0 %fusion.7 = f32[8,2,4,128]{3,0,2,1:T(8,128)S(1)} fusion(bf16[16,2048,128]{2,1,0:T(8,128)(2,1)} %param.13, bf16[8,2,4,2048]{3,2,1,0:T(4,128)(2,1)S(1)} %slice.40, pred[8,2,16]{0,2,1:T(8,128)(4,1)S(1)} %iota_compare_fusion), kind=kOutput, calls=%fused_computation.12 | convolution fusion | flops 537124864 | bytes 8683776 | tf_op jit(solution)/shard_map/oksd,adr->oksar/dot_general | solution.py:222
  48.2 1.0 %collective-permute-done.2 = f32[8,2,4,128]{3,0,2,1:T(8,128)S(1)} collective-permute-done((f32[8,2,4,128]{3,0,2,1:T(8,128)S(1)}, f32[8,2,4,128]{3,0,2,1:T(8,128)S(1)}, u32[]{:S(2)}, u32[]{:S(2)}) %collective-permute-start.2) | collective-permute-done | bytes 32800 | tf_op jit(solution)/shard_map/ppermute | solution.py:132
  50.3 2.8 %collective-permute-done.3 = f32[8,2,4,128]{3,0,2,1:T(8,128)S(1)} collective-permute-done((f32[8,2,4,128]{3,0,2,1:T(8,128)S(1)}, f32[8,2,4,128]{3,0,2,1:T(8,128)S(1)}, u32[]{:S(2)}, u32[]{:S(2)}) %collective-permute-start.3) | collective-permute-done | bytes 32800 | tf_op jit(solution)/shard_map/ppermute | solution.py:132
  53.2 0.9 %fusion.10 = f32[8,2,4,2,256]{4,2,3,1,0:T(4,128)} fusion(bf16[8,2,2,64,256]{4,3,2,1,0:T(8,128)(2,1)S(1)} %bitcast.83, bf16[8,2,4,2,64]{4,3,0,2,1:T(2,128)(2,1)S(1)} %reshape.338), kind=kOutput, calls=%fused_computation.14 | convolution fusion | flops 4227072 | bytes 1196032 | tf_op jit(solution)/shard_map/okscr,okcrw->okscw/dot_general | solution.py:232
  54.1 3.6 %all-to-all-start.1 = ((f32[8,2,4,2,256]{4,2,3,1,0:T(4,128)}), f32[8,2,4,2,256]{4,2,3,1,0:T(4,128)S(1)}, u32[]{:S(2)}, u32[]{:S(2)}) async-start(f32[8,2,4,2,256]{4,2,3,1,0:T(4,128)} %fusion.10), calls=%async_computation.1 | async-start | bytes 262144 | tf_op jit(solution)/shard_map/all_to_all | solution.py:235
  57.7 5.0 %fusion.2 = f32[32,2,256]{2,0,1:T(8,128)S(1)} fusion(bf16[8192,2,256]{2,1,0:T(2,128)(2,1)} %param.12, bf16[32,8192]{1,0:T(8,128)(2,1)S(1)} %all_gather.3, f32[8192]{0:T(1024)S(1)} %copy-done.3, f32[32]{0:T(128)S(1)} %rsqrt_bitcast_fusion), kind=kOutput, calls=%fused_computation.9 | convolution fusion | flops 269484032 | bytes 9011328 | tf_op jit(solution)/shard_map/jd,dcw->jcw/dot_general | solution.py:238
  62.7 2.4 %all-to-all-done.1 = f32[8,2,4,2,256]{4,2,3,1,0:T(4,128)S(1)} async-done(((f32[8,2,4,2,256]{4,2,3,1,0:T(4,128)}), f32[8,2,4,2,256]{4,2,3,1,0:T(4,128)S(1)}, u32[]{:S(2)}, u32[]{:S(2)}) %all-to-all-start.1) | async-done | bytes 131104 | tf_op jit(solution)/shard_map/all_to_all | solution.py:235
  66.2 0.7 pad_maximum_fusion.1.nkv_ref
  66.9 11.1 %shard_map.114 = bf16[32,2048]{1,0:T(8,128)(2,1)} custom-call(bf16[32,16,128]{2,1,0:T(8,128)(2,1)} %bitcast.85, f32[32,16,1024]{2,1,0:T(8,128)} %shard_map.113.s_ref, bf16[32,512,2,256]{3,2,1,0:T(2,128)(2,1)} %kv_ref.3, bf16[32,2,256]{2,1,0:T(2,128)(2,1)} %pad_maximum_fusion.1.nkv_ref), custom_call_target="tpu_custom_call" | custom-call | tf_op jit(solution)/shard_map/pallas_call | solution.py:110
  (75 shorter events, 7.6 us)
Async XLA Ops:
  0.6 49.1 %copy-start = (bf16[16,2,64,256]{3,2,1,0:T(8,128)(2,1)S(1)}, bf16[16,2,64,256]{3,2,1,0:T(8,128)(2,1)}, u32[]{:S(2)}) copy-start(bf16[16,2,64,256]{3,2,1,0:T(8,128)(2,1)} %param.14) | copy-start | bytes 3145732
  0.6 10.2 %copy-start.2 = (bf16[32,2048]{1,0:T(8,128)(2,1)S(1)}, bf16[32,2048]{1,0:T(8,128)(2,1)}, u32[]{:S(2)}) copy-start(bf16[32,2048]{1,0:T(8,128)(2,1)} %param.15) | copy-start | bytes 393220
  1.8 9.7 %collective-permute-start = (f32[32,1]{0,1:T(1,128)S(1)}, f32[32,1]{0,1:T(1,128)S(1)}, u32[]{:S(2)}, u32[]{:S(2)}) collective-permute-start(f32[32,1]{0,1:T(1,128)S(1)} %bitcast.89), channel_id=1, source_target_pairs={{0,1},{1,0},{2,3},{3,2},{4,5},{5,4},{6,7},{7,6},{8,9},{9,8},{10,11... | collective-permute-start | bytes 392 | tf_op jit(solution)/shard_map/ppermute | solution.py:132
  11.5 13.6 %collective-permute-start.1 = (f32[32,1]{0,1:T(1,128)S(1)}, f32[32,1]{0,1:T(1,128)S(1)}, u32[]{:S(2)}, u32[]{:S(2)}) collective-permute-start(f32[32,1]{0,1:T(1,128)S(1)} %bitcast_add_fusion), channel_id=1, source_target_pairs={{0,2},{1,3},{2,0},{3,1},{4,6},{5,7},{6,4},{7,5},{8,10},{9,11},{10,... | collective-permute-start | bytes 392 | tf_op jit(solution)/shard_map/ppermute | solution.py:132
  14.0 11.1 %copy-start.1 = (bf16[32,2048]{1,0:T(8,128)(2,1)S(1)}, bf16[32,2048]{1,0:T(8,128)(2,1)}, u32[]{:S(2)}) copy-start(bf16[32,2048]{1,0:T(8,128)(2,1)} %param.10) | copy-start | bytes 393220
  14.0 11.1 %dynamic-slice-start = ((f32[8192]{0:T(1024)}, s32[]{:T(128)}), f32[2048]{0:T(1024)S(1)}, s32[]{:S(2)}) async-start(f32[8192]{0:T(1024)} %param.11, s32[]{:T(128)} %select_n.121), calls=%async_computation.2 | async-start | bytes 16896 | tf_op jit(solution)/shard_map/dynamic_slice | solution.py:178
  27.3 15.4 %all-to-all-start = ((bf16[8,2,4,2176]{3,2,1,0:T(4,128)(2,1)}), bf16[8,2,4,2176]{3,2,1,0:T(4,128)(2,1)S(1)}, u32[]{:S(2)}, u32[]{:S(2)}) async-start(bf16[8,2,4,2176]{3,2,1,0:T(4,128)(2,1)} %pad_maximum_fusion), calls=%async_computation | async-start | bytes 557056 | tf_op jit(solution)/shard_map/all_to_all | solution.py:218
  42.9 14.8 %copy-start.3 = (f32[8192]{0:T(1024)S(1)}, f32[8192]{0:T(1024)}, u32[]{:S(2)}) copy-start(f32[8192]{0:T(1024)} %param.11) | copy-start | bytes 98308
  47.9 1.3 %collective-permute-start.2 = (f32[8,2,4,128]{3,0,2,1:T(8,128)S(1)}, f32[8,2,4,128]{3,0,2,1:T(8,128)S(1)}, u32[]{:S(2)}, u32[]{:S(2)}) collective-permute-start(f32[8,2,4,128]{3,0,2,1:T(8,128)S(1)} %fusion.7), channel_id=1, source_target_pairs={{0,1},{1,0},{2,3},{3,2},{4,5},{5,4},{6,7},{7,6},{8,9},{9,8},{10,11... | collective-permute-start | bytes 98312 | tf_op jit(solution)/shard_map/ppermute | solution.py:132
  49.2 3.9 %collective-permute-start.3 = (f32[8,2,4,128]{3,0,2,1:T(8,128)S(1)}, f32[8,2,4,128]{3,0,2,1:T(8,128)S(1)}, u32[]{:S(2)}, u32[]{:S(2)}) collective-permute-start(f32[8,2,4,128]{3,0,2,1:T(8,128)S(1)} %add.148), channel_id=1, source_target_pairs={{0,2},{1,3},{2,0},{3,1},{4,6},{5,7},{6,4},{7,5},{8,10},{9,11},{10,... | collective-permute-start | bytes 98312 | tf_op jit(solution)/shard_map/ppermute | solution.py:132
  54.1 11.0 %all-to-all-start.1 = ((f32[8,2,4,2,256]{4,2,3,1,0:T(4,128)}), f32[8,2,4,2,256]{4,2,3,1,0:T(4,128)S(1)}, u32[]{:S(2)}, u32[]{:S(2)}) async-start(f32[8,2,4,2,256]{4,2,3,1,0:T(4,128)} %fusion.10), calls=%async_computation.1 | async-start | bytes 262144 | tf_op jit(solution)/shard_map/all_to_all | solution.py:235

commit v17 on v13

--- a/solution.py
+++ b/solution.py
@@ -34,6 +34,16 @@
             second_half * cosine_term + first_half * sine_term,
         ],
         axis=-1,
+    )
+
+
+def head_rows(q_ref, i, h, group_size):
+    return jnp.concatenate(
+        [
+            q_ref[i:i + 1, (h * group_size + g) * HEAD:(h * group_size + g + 1) * HEAD]
+            for g in range(group_size)
+        ],
+        axis=0,
     )
 
 
@@ -51,7 +61,7 @@
             cols = slice(h * HEAD, (h + 1) * HEAD)
             qrows = slice(h * group_size, (h + 1) * group_size)
             scores = lax.dot_general(
-                q_ref[i, qrows, :], stacked[:, cols], (((1,), (1,)), ((), ())),
+                head_rows(q_ref, i, h, group_size), stacked[:, cols], (((1,), (1,)), ((), ())),
                 preferred_element_type=jnp.float32,
             ) * scale
             s_ref[i, qrows, :] = jnp.where(live, scores, -jnp.inf)
@@ -66,7 +76,7 @@
         for h in range(kv_local):
             cols = slice(h * HEAD, (h + 1) * HEAD)
             qrows = slice(h * group_size, (h + 1) * group_size)
-            q = q_ref[i, qrows, :]
+            q = head_rows(q_ref, i, h, group_size)
             scores = s_ref[i, qrows, :]
             new_key = nkv_ref[i, 0:1, cols].astype(jnp.float32)
             new_value = nkv_ref[i, 1:2, cols].astype(jnp.float32)
@@ -91,10 +101,10 @@
     width = key_value_cache.shape[3]
     heads = kv_local * group_size
     rows = 8 if row_count % 8 == 0 else row_count
-    query_heads = query.reshape(row_count, heads, HEAD)
+    query_heads = query
     opts = dict(rows=rows, kv_local=kv_local, group_size=group_size)
     cache_spec = pl.BlockSpec((rows, cache_len, 2, width), lambda b, *_: (b, 0, 0, 0))
-    head_spec = pl.BlockSpec((rows, heads, HEAD), lambda b, *_: (b, 0, 0))
+    head_spec = pl.BlockSpec((rows, heads * HEAD), lambda b, *_: (b, 0))
     score_spec = pl.BlockSpec((rows, heads, 2 * cache_len), lambda b, *_: (b, 0, 0))
     scores = pl.pallas_call(
         functools.partial(score_kernel, **opts),
@@ -112,7 +122,7 @@
         out_shape=jax.ShapeDtypeStruct((row_count, heads * HEAD), jnp.bfloat16),
         grid=(row_count // mix_rows,),
         in_specs=[
-            pl.BlockSpec((mix_rows, heads, HEAD), lambda b: (b, 0, 0)),
+            pl.BlockSpec((mix_rows, heads * HEAD), lambda b: (b, 0)),
             pl.BlockSpec((mix_rows, heads, 2 * cache_len), lambda b: (b, 0, 0)),
             pl.BlockSpec((mix_rows, cache_len, 2, width), lambda b: (b, 0, 0, 0)),
             pl.BlockSpec((mix_rows, 2, width), lambda b: (b, 0, 0)),

time: 74 us -> 73.4 us (level)
  transfers between devices with their start and end apart: 4 -> 4, of which waited for: 3 -> 3; matrix products, arithmetic and copies ran while one was open for 11% -> 10% of each run, Pallas kernels for 15% -> 15%
where the time goes in v17:
time: 73.4 us; the launch traced here: 73 us
  Pallas kernels  22.2 us (30%)
  matrix products  10.8 us (15%)
  starting transfers between devices  10.6 us (14%)
  blocking collectives  8.65 us (12%)
  local copies, waits for them, and re-layouts  7.63 us (10%)
  waiting for transfers between devices  6.46 us (9%)
  other arithmetic  5.69 us (8%)
  between operations  0.9 us (1%)
    pallas_call x1, Pallas kernels, attend(): pl.pallas_call(functools.partial(mix_kernel, rows=mix_rows, kv_local=kv_l...  11.2 us
    pallas_call x1, Pallas kernels, attend(): pl.pallas_call(functools.partial(score_kernel, **opts), out_shape=jax.Sha...  11 us
    all_gather x1, blocking collectives, body(): gathered = lax.all_gather(hidden, 'tensor', axis=1, tiled=True)  8.65 us
    all_to_all x1, starting transfers between devices, body(): lax.all_to_all(payload, 'replica', split_axis=0, concat_axis=0, tiled=True)  5.81 us
    dot_general x1, matrix products, body(): jnp.einsum('oksd,adr->oksar', got_rows, adapter_down, preferred_element_t...  4.96 us
    dot_general x1, matrix products, body(): jnp.einsum('jd,dcw->jcw', normed, key_value_weight, preferred_element_typ...  4.93 us
    all_to_all x1, starting transfers between devices, body(): lax.all_to_all(owner_delta, 'replica', split_axis=0, concat_axis=0, tiled...  3.64 us
    all_to_all x1, waiting for transfers between devices, body(): lax.all_to_all(payload, 'replica', split_axis=0, concat_axis=0, tiled=True)  3.26 us
  transfers between devices with their start and end apart: 4, of which 3 were waited for; matrix products, arithmetic and copies ran while one was open for 10% of the time, Pallas kernels for 15%

profile of v17, /device:TPU:0, one launch (start us, length us, event | category | flops | bytes accessed | tf_op | source)
XLA Modules:
  0.0 73.0 jit_solution(4545534186823094594)
XLA Ops:
  0.7 0.8 %fusion.22 = s32[16]{0:T(128)S(1)} fusion(s32[1,16]{1,0:T(1,128)} %param.17), kind=kLoop, calls=%fused_computation.78 | loop fusion | flops 240 | bytes 128 | tf_op jit(solution)/shard_map/eq | solution.py:189
  1.4 0.7 and_select_fusion.2
  2.9 1.3 %gather_fusion = s32[16]{0:T(128)S(1)} fusion(s32[16]{0:T(128)} %bitcast.75, s32[1024]{0:T(1024)S(1)} %pad_clamp_fusion.4), kind=kCustom, calls=%fused_computation | custom fusion | bytes 192 | tf_op jit(solution)/shard_map/gather | solution.py:201
  4.5 0.7 %copy.59 = s32[16,1]{1,0:T(8,128)S(1)} copy(s32[16,1]{0,1:T(1,128)} %bitcast.76) | data formatting | bytes 128 | tf_op jit(solution)/shard_map/reshape.320
  5.4 0.7 bitcast_subtract_fusion.1
  6.1 0.7 gather_fusion.1
  7.1 8.6 %all_gather.3 = bf16[32,8192]{1,0:T(8,128)(2,1)S(1)} all-gather(bf16[32,2048]{1,0:T(8,128)(2,1)S(1)} %copy-done.1), channel_id=1, replica_groups=mesh['replica'=8,'tensor'=4] {'tensor'}, dimensions={1}, use_global_device_ids=true | all-gather | bytes 655360 | tf_op jit(solution)/shard_map/all_gather | solution.py:167
  16.2 0.7 %gather_fusion.2 = bf16[64,2048]{1,0:T(8,128)(2,1)S(1)} fusion(bf16[32,2048]{1,0:T(8,128)(2,1)S(1)} %constant_dynamic-slice_fusion, s32[1024]{0:T(1024)S(1)} %pad_clamp_fusion.3), kind=kCustom, calls=%fused_computation.2 | custom fusion | bytes 524544 | tf_op jit(solution)/shard_map/gather | solution.py:205
  17.3 0.8 %pad_maximum_fusion = bf16[8,2,4,2176]{3,2,1,0:T(4,128)(2,1)} fusion(bf16[8,2,4,128]{3,2,1,0:T(4,128)(2,1)S(1)} %broadcast_in_dim.54, bf16[8,2,4,2048]{3,2,1,0:T(4,128)(2,1)S(1)} %broadcast_select_fusion), kind=kLoop, calls=%fused_computation.21 | loop fusion | flops 557056 | bytes 557056 | tf_op jit(solution)/shard_map/concatenate | solution.py:210
  18.2 5.8 %all-to-all-start = ((bf16[8,2,4,2176]{3,2,1,0:T(4,128)(2,1)}), bf16[8,2,4,2176]{3,2,1,0:T(4,128)(2,1)S(1)}, u32[]{:S(2)}, u32[]{:S(2)}) async-start(bf16[8,2,4,2176]{3,2,1,0:T(4,128)(2,1)} %pad_maximum_fusion), calls=%async_computation | async-start | bytes 557056 | tf_op jit(solution)/shard_map/all_to_all | solution.py:211
  24.1 0.7 gather_fusion.5
  24.8 0.7 gather_fusion.4
  25.5 4.9 %fusion.2 = f32[32,2,256]{2,0,1:T(8,128)S(1)} fusion(bf16[8192,2,256]{2,1,0:T(2,128)(2,1)} %param.12, bf16[32,8192]{1,0:T(8,128)(2,1)S(1)} %fusion.13), kind=kOutput, calls=%fused_computation.9 | convolution fusion | flops 268435456 | bytes 8978432 | tf_op jit(solution)/shard_map/jd,dcw->jcw/dot_general | solution.py:231
  30.4 3.3 %all-to-all-done = bf16[8,2,4,2176]{3,2,1,0:T(4,128)(2,1)S(1)} async-done(((bf16[8,2,4,2176]{3,2,1,0:T(4,128)(2,1)}), bf16[8,2,4,2176]{3,2,1,0:T(4,128)(2,1)S(1)}, u32[]{:S(2)}, u32[]{:S(2)}) %all-to-all-start) | async-done | bytes 278560 | tf_op jit(solution)/shard_map/all_to_all | solution.py:211
  34.0 5.0 %fusion.7 = f32[8,2,4,128]{3,0,2,1:T(8,128)S(1)} fusion(bf16[16,2048,128]{2,1,0:T(8,128)(2,1)} %param.13, bf16[8,2,4,2048]{3,2,1,0:T(4,128)(2,1)S(1)} %slice.40, pred[8,2,16]{0,2,1:T(8,128)(4,1)S(1)} %iota_compare_fusion), kind=kOutput, calls=%fused_computation.14 | convolution fusion | flops 537124864 | bytes 8683776 | tf_op jit(solution)/shard_map/oksd,adr->oksar/dot_general | solution.py:215
  39.2 1.0 %collective-permute-done = f32[8,2,4,128]{3,0,2,1:T(8,128)S(1)} collective-permute-done((f32[8,2,4,128]{3,0,2,1:T(8,128)S(1)}, f32[8,2,4,128]{3,0,2,1:T(8,128)S(1)}, u32[]{:S(2)}, u32[]{:S(2)}) %collective-permute-start) | collective-permute-done | bytes 32800 | tf_op jit(solution)/shard_map/ppermute | solution.py:142
  40.2 1.1 %collective-permute-start.1 = (f32[8,2,4,128]{3,0,2,1:T(8,128)S(1)}, f32[8,2,4,128]{3,0,2,1:T(8,128)S(1)}, u32[]{:S(2)}, u32[]{:S(2)}) collective-permute-start(f32[8,2,4,128]{3,0,2,1:T(8,128)S(1)} %add.145), channel_id=1, source_target_pairs={{0,2},{1,3},{2,0},{3,1},{4,6},{5,7},{6,4},{7,5},{8,10},{9,11},{10,... | collective-permute-start | bytes 98312 | tf_op jit(solution)/shard_map/ppermute | solution.py:142
  41.9 2.2 %collective-permute-done.1 = f32[8,2,4,128]{3,0,2,1:T(8,128)S(1)} collective-permute-done((f32[8,2,4,128]{3,0,2,1:T(8,128)S(1)}, f32[8,2,4,128]{3,0,2,1:T(8,128)S(1)}, u32[]{:S(2)}, u32[]{:S(2)}) %collective-permute-start.1) | collective-permute-done | bytes 32800 | tf_op jit(solution)/shard_map/ppermute | solution.py:142
  44.2 0.9 %fusion.10 = f32[8,2,4,2,256]{4,2,3,1,0:T(4,128)} fusion(bf16[8,2,2,64,256]{4,3,2,1,0:T(8,128)(2,1)S(1)} %bitcast.77, bf16[8,2,4,2,64]{4,3,0,2,1:T(2,128)(2,1)S(1)} %reshape.342), kind=kOutput, calls=%fused_computation.16 | convolution fusion | flops 4227072 | bytes 1196032 | tf_op jit(solution)/shard_map/okscr,okcrw->okscw/dot_general | solution.py:225
  45.1 3.6 %all-to-all-start.1 = ((f32[8,2,4,2,256]{4,2,3,1,0:T(4,128)}), f32[8,2,4,2,256]{4,2,3,1,0:T(4,128)S(1)}, u32[]{:S(2)}, u32[]{:S(2)}) async-start(f32[8,2,4,2,256]{4,2,3,1,0:T(4,128)} %fusion.10), calls=%async_computation.1 | async-start | bytes 262144 | tf_op jit(solution)/shard_map/all_to_all | solution.py:228
  48.8 11.0 %shard_map.113.s_ref = f32[32,16,1024]{2,1,0:T(8,128)} custom-call(s32[32]{0:T(128)} %len_ref.1, bf16[32,2048]{1,0:T(8,128)(2,1)} %q_ref.3, bf16[32,512,2,256]{3,2,1,0:T(2,128)(2,1)} %kv_ref.3), custom_call_target="tpu_custom_call" | custom-call | tf_op jit(solution)/shard_map/pallas_call | solution.py:109
  60.1 0.6 gather_fusion.6
  61.1 0.7 pad_maximum_fusion.1.nkv_ref
  61.8 11.2 %shard_map.114 = bf16[32,2048]{1,0:T(8,128)(2,1)} custom-call(bf16[32,2048]{1,0:T(8,128)(2,1)} %q_ref.3, f32[32,16,1024]{2,1,0:T(8,128)} %shard_map.113.s_ref, bf16[32,512,2,256]{3,2,1,0:T(2,128)(2,1)} %kv_ref.3, bf16[32,2,256]{2,1,0:T(2,128)(2,1)} %pad_maximum_fusion.1.nkv_ref), custom_call_target="tpu_custom_call" | custom-call | tf_op jit(solution)/shard_map/pallas_call | solution.py:120
  (68 shorter events, 4.3 us)
Async XLA Ops:
  0.6 40.7 %copy-start = (bf16[16,2,64,256]{3,2,1,0:T(8,128)(2,1)S(1)}, bf16[16,2,64,256]{3,2,1,0:T(8,128)(2,1)}, u32[]{:S(2)}) copy-start(bf16[16,2,64,256]{3,2,1,0:T(8,128)(2,1)} %param.14) | copy-start | bytes 3145732
  0.6 6.4 %copy-start.1 = (bf16[32,2048]{1,0:T(8,128)(2,1)S(1)}, bf16[32,2048]{1,0:T(8,128)(2,1)}, u32[]{:S(2)}) copy-start(bf16[32,2048]{1,0:T(8,128)(2,1)} %param.10) | copy-start | bytes 393220
  0.7 15.3 %copy-start.2 = (f32[8192]{0:T(1024)S(1)}, f32[8192]{0:T(1024)}, u32[]{:S(2)}) copy-start(f32[8192]{0:T(1024)} %param.11) | copy-start | bytes 98308
  18.2 15.5 %all-to-all-start = ((bf16[8,2,4,2176]{3,2,1,0:T(4,128)(2,1)}), bf16[8,2,4,2176]{3,2,1,0:T(4,128)(2,1)S(1)}, u32[]{:S(2)}, u32[]{:S(2)}) async-start(bf16[8,2,4,2176]{3,2,1,0:T(4,128)(2,1)} %pad_maximum_fusion), calls=%async_computation | async-start | bytes 557056 | tf_op jit(solution)/shard_map/all_to_all | solution.py:211
  33.9 14.8 %copy-start.3 = (s32[32]{0:T(128)S(1)}, s32[32]{0:T(128)}, u32[]{:S(2)}) copy-start(s32[32]{0:T(128)} %len_ref.1) | copy-start | bytes 388
  38.9 1.3 %collective-permute-start = (f32[8,2,4,128]{3,0,2,1:T(8,128)S(1)}, f32[8,2,4,128]{3,0,2,1:T(8,128)S(1)}, u32[]{:S(2)}, u32[]{:S(2)}) collective-permute-start(f32[8,2,4,128]{3,0,2,1:T(8,128)S(1)} %fusion.7), channel_id=1, source_target_pairs={{0,1},{1,0},{2,3},{3,2},{4,5},{5,4},{6,7},{7,6},{8,9},{9,8},{10,11... | collective-permute-start | bytes 98312 | tf_op jit(solution)/shard_map/ppermute | solution.py:142
  40.2 3.9 %collective-permute-start.1 = (f32[8,2,4,128]{3,0,2,1:T(8,128)S(1)}, f32[8,2,4,128]{3,0,2,1:T(8,128)S(1)}, u32[]{:S(2)}, u32[]{:S(2)}) collective-permute-start(f32[8,2,4,128]{3,0,2,1:T(8,128)S(1)} %add.145), channel_id=1, source_target_pairs={{0,2},{1,3},{2,0},{3,1},{4,6},{5,7},{6,4},{7,5},{8,10},{9,11},{10,... | collective-permute-start | bytes 98312 | tf_op jit(solution)/shard_map/ppermute | solution.py:142
  45.1 14.9 %all-to-all-start.1 = ((f32[8,2,4,2,256]{4,2,3,1,0:T(4,128)}), f32[8,2,4,2,256]{4,2,3,1,0:T(4,128)S(1)}, u32[]{:S(2)}, u32[]{:S(2)}) async-start(f32[8,2,4,2,256]{4,2,3,1,0:T(4,128)} %fusion.10), calls=%async_computation.1 | async-start | bytes 262144 | tf_op jit(solution)/shard_map/all_to_all | solution.py:228

commit v18 on v17

--- a/solution.py
+++ b/solution.py
@@ -100,7 +100,7 @@
     cache_len = key_value_cache.shape[1]
     width = key_value_cache.shape[3]
     heads = kv_local * group_size
-    rows = 8 if row_count % 8 == 0 else row_count
+    rows = 16 if row_count % 16 == 0 else row_count
     query_heads = query
     opts = dict(rows=rows, kv_local=kv_local, group_size=group_size)
     cache_spec = pl.BlockSpec((rows, cache_len, 2, width), lambda b, *_: (b, 0, 0, 0))

time: 73.4 us -> 73.5 us (level)
  no operation moved by 1% of the time
where the time goes in v18:
time: 73.5 us; the launch traced here: 73.1 us
  Pallas kernels  22.4 us (30%)
  matrix products  10.8 us (15%)
  starting transfers between devices  10.6 us (14%)
  blocking collectives  8.65 us (12%)
  local copies, waits for them, and re-layouts  7.63 us (10%)
  waiting for transfers between devices  6.46 us (9%)
  other arithmetic  5.69 us (8%)
  between operations  0.9 us (1%)
    pallas_call x1, Pallas kernels, attend(): pl.pallas_call(functools.partial(score_kernel, **opts), out_shape=jax.Sha...  11.2 us
    pallas_call x1, Pallas kernels, attend(): pl.pallas_call(functools.partial(mix_kernel, rows=mix_rows, kv_local=kv_l...  11.2 us
    all_gather x1, blocking collectives, body(): gathered = lax.all_gather(hidden, 'tensor', axis=1, tiled=True)  8.65 us
    all_to_all x1, starting transfers between devices, body(): lax.all_to_all(payload, 'replica', split_axis=0, concat_axis=0, tiled=True)  5.81 us
    dot_general x1, matrix products, body(): jnp.einsum('oksd,adr->oksar', got_rows, adapter_down, preferred_element_t...  4.96 us
    dot_general x1, matrix products, body(): jnp.einsum('jd,dcw->jcw', normed, key_value_weight, preferred_element_typ...  4.93 us
    all_to_all x1, starting transfers between devices, body(): lax.all_to_all(owner_delta, 'replica', split_axis=0, concat_axis=0, tiled...  3.64 us
    all_to_all x1, waiting for transfers between devices, body(): lax.all_to_all(payload, 'replica', split_axis=0, concat_axis=0, tiled=True)  3.26 us
  transfers between devices with their start and end apart: 4, of which 3 were waited for; matrix products, arithmetic and copies ran while one was open for 10% of the time, Pallas kernels for 15%

profile of v18, /device:TPU:0, one launch (start us, length us, event | category | flops | bytes accessed | tf_op | source)
XLA Modules:
  0.0 73.1 jit_solution(15400743718111049105)
XLA Ops:
  0.7 0.8 %fusion.22 = s32[16]{0:T(128)S(1)} fusion(s32[1,16]{1,0:T(1,128)} %param.17), kind=kLoop, calls=%fused_computation.78 | loop fusion | flops 240 | bytes 128 | tf_op jit(solution)/shard_map/eq | solution.py:189
  1.4 0.7 and_select_fusion.2
  2.9 1.3 %gather_fusion = s32[16]{0:T(128)S(1)} fusion(s32[16]{0:T(128)} %bitcast.75, s32[1024]{0:T(1024)S(1)} %pad_clamp_fusion.4), kind=kCustom, calls=%fused_computation | custom fusion | bytes 192 | tf_op jit(solution)/shard_map/gather | solution.py:201
  4.5 0.7 %copy.59 = s32[16,1]{1,0:T(8,128)S(1)} copy(s32[16,1]{0,1:T(1,128)} %bitcast.76) | data formatting | bytes 128 | tf_op jit(solution)/shard_map/reshape.320
  5.4 0.7 bitcast_subtract_fusion.1
  6.1 0.7 gather_fusion.1
  7.1 8.6 %all_gather.3 = bf16[32,8192]{1,0:T(8,128)(2,1)S(1)} all-gather(bf16[32,2048]{1,0:T(8,128)(2,1)S(1)} %copy-done.1), channel_id=1, replica_groups=mesh['replica'=8,'tensor'=4] {'tensor'}, dimensions={1}, use_global_device_ids=true | all-gather | bytes 655360 | tf_op jit(solution)/shard_map/all_gather | solution.py:167
  16.2 0.7 %gather_fusion.2 = bf16[64,2048]{1,0:T(8,128)(2,1)S(1)} fusion(bf16[32,2048]{1,0:T(8,128)(2,1)S(1)} %constant_dynamic-slice_fusion, s32[1024]{0:T(1024)S(1)} %pad_clamp_fusion.3), kind=kCustom, calls=%fused_computation.2 | custom fusion | bytes 524544 | tf_op jit(solution)/shard_map/gather | solution.py:205
  17.3 0.8 %pad_maximum_fusion = bf16[8,2,4,2176]{3,2,1,0:T(4,128)(2,1)} fusion(bf16[8,2,4,128]{3,2,1,0:T(4,128)(2,1)S(1)} %broadcast_in_dim.54, bf16[8,2,4,2048]{3,2,1,0:T(4,128)(2,1)S(1)} %broadcast_select_fusion), kind=kLoop, calls=%fused_computation.21 | loop fusion | flops 557056 | bytes 557056 | tf_op jit(solution)/shard_map/concatenate | solution.py:210
  18.2 5.8 %all-to-all-start = ((bf16[8,2,4,2176]{3,2,1,0:T(4,128)(2,1)}), bf16[8,2,4,2176]{3,2,1,0:T(4,128)(2,1)S(1)}, u32[]{:S(2)}, u32[]{:S(2)}) async-start(bf16[8,2,4,2176]{3,2,1,0:T(4,128)(2,1)} %pad_maximum_fusion), calls=%async_computation | async-start | bytes 557056 | tf_op jit(solution)/shard_map/all_to_all | solution.py:211
  24.1 0.7 gather_fusion.5
  24.8 0.7 gather_fusion.4
  25.5 4.9 %fusion.2 = f32[32,2,256]{2,0,1:T(8,128)S(1)} fusion(bf16[8192,2,256]{2,1,0:T(2,128)(2,1)} %param.12, bf16[32,8192]{1,0:T(8,128)(2,1)S(1)} %fusion.13), kind=kOutput, calls=%fused_computation.9 | convolution fusion | flops 268435456 | bytes 8978432 | tf_op jit(solution)/shard_map/jd,dcw->jcw/dot_general | solution.py:231
  30.4 3.3 %all-to-all-done = bf16[8,2,4,2176]{3,2,1,0:T(4,128)(2,1)S(1)} async-done(((bf16[8,2,4,2176]{3,2,1,0:T(4,128)(2,1)}), bf16[8,2,4,2176]{3,2,1,0:T(4,128)(2,1)S(1)}, u32[]{:S(2)}, u32[]{:S(2)}) %all-to-all-start) | async-done | bytes 278560 | tf_op jit(solution)/shard_map/all_to_all | solution.py:211
  34.0 5.0 %fusion.7 = f32[8,2,4,128]{3,0,2,1:T(8,128)S(1)} fusion(bf16[16,2048,128]{2,1,0:T(8,128)(2,1)} %param.13, bf16[8,2,4,2048]{3,2,1,0:T(4,128)(2,1)S(1)} %slice.40, pred[8,2,16]{0,2,1:T(8,128)(4,1)S(1)} %iota_compare_fusion), kind=kOutput, calls=%fused_computation.14 | convolution fusion | flops 537124864 | bytes 8683776 | tf_op jit(solution)/shard_map/oksd,adr->oksar/dot_general | solution.py:215
  39.2 1.0 %collective-permute-done = f32[8,2,4,128]{3,0,2,1:T(8,128)S(1)} collective-permute-done((f32[8,2,4,128]{3,0,2,1:T(8,128)S(1)}, f32[8,2,4,128]{3,0,2,1:T(8,128)S(1)}, u32[]{:S(2)}, u32[]{:S(2)}) %collective-permute-start) | collective-permute-done | bytes 32800 | tf_op jit(solution)/shard_map/ppermute | solution.py:142
  40.2 1.1 %collective-permute-start.1 = (f32[8,2,4,128]{3,0,2,1:T(8,128)S(1)}, f32[8,2,4,128]{3,0,2,1:T(8,128)S(1)}, u32[]{:S(2)}, u32[]{:S(2)}) collective-permute-start(f32[8,2,4,128]{3,0,2,1:T(8,128)S(1)} %add.145), channel_id=1, source_target_pairs={{0,2},{1,3},{2,0},{3,1},{4,6},{5,7},{6,4},{7,5},{8,10},{9,11},{10,... | collective-permute-start | bytes 98312 | tf_op jit(solution)/shard_map/ppermute | solution.py:142
  41.9 2.2 %collective-permute-done.1 = f32[8,2,4,128]{3,0,2,1:T(8,128)S(1)} collective-permute-done((f32[8,2,4,128]{3,0,2,1:T(8,128)S(1)}, f32[8,2,4,128]{3,0,2,1:T(8,128)S(1)}, u32[]{:S(2)}, u32[]{:S(2)}) %collective-permute-start.1) | collective-permute-done | bytes 32800 | tf_op jit(solution)/shard_map/ppermute | solution.py:142
  44.2 0.9 %fusion.10 = f32[8,2,4,2,256]{4,2,3,1,0:T(4,128)} fusion(bf16[8,2,2,64,256]{4,3,2,1,0:T(8,128)(2,1)S(1)} %bitcast.77, bf16[8,2,4,2,64]{4,3,0,2,1:T(2,128)(2,1)S(1)} %reshape.342), kind=kOutput, calls=%fused_computation.16 | convolution fusion | flops 4227072 | bytes 1196032 | tf_op jit(solution)/shard_map/okscr,okcrw->okscw/dot_general | solution.py:225
  45.1 3.6 %all-to-all-start.1 = ((f32[8,2,4,2,256]{4,2,3,1,0:T(4,128)}), f32[8,2,4,2,256]{4,2,3,1,0:T(4,128)S(1)}, u32[]{:S(2)}, u32[]{:S(2)}) async-start(f32[8,2,4,2,256]{4,2,3,1,0:T(4,128)} %fusion.10), calls=%async_computation.1 | async-start | bytes 262144 | tf_op jit(solution)/shard_map/all_to_all | solution.py:228
  48.8 11.2 %shard_map.113.s_ref = f32[32,16,1024]{2,1,0:T(8,128)} custom-call(s32[32]{0:T(128)} %len_ref.1, bf16[32,2048]{1,0:T(8,128)(2,1)} %q_ref.3, bf16[32,512,2,256]{3,2,1,0:T(2,128)(2,1)} %kv_ref.3), custom_call_target="tpu_custom_call" | custom-call | tf_op jit(solution)/shard_map/pallas_call | solution.py:109
  60.2 0.6 gather_fusion.6
  61.2 0.7 pad_maximum_fusion.1.nkv_ref
  61.9 11.2 %shard_map.114 = bf16[32,2048]{1,0:T(8,128)(2,1)} custom-call(bf16[32,2048]{1,0:T(8,128)(2,1)} %q_ref.3, f32[32,16,1024]{2,1,0:T(8,128)} %shard_map.113.s_ref, bf16[32,512,2,256]{3,2,1,0:T(2,128)(2,1)} %kv_ref.3, bf16[32,2,256]{2,1,0:T(2,128)(2,1)} %pad_maximum_fusion.1.nkv_ref), custom_call_target="tpu_custom_call" | custom-call | tf_op jit(solution)/shard_map/pallas_call | solution.py:120
  (68 shorter events, 4.3 us)
Async XLA Ops:
  0.6 40.7 %copy-start = (bf16[16,2,64,256]{3,2,1,0:T(8,128)(2,1)S(1)}, bf16[16,2,64,256]{3,2,1,0:T(8,128)(2,1)}, u32[]{:S(2)}) copy-start(bf16[16,2,64,256]{3,2,1,0:T(8,128)(2,1)} %param.14) | copy-start | bytes 3145732
  0.6 6.4 %copy-start.1 = (bf16[32,2048]{1,0:T(8,128)(2,1)S(1)}, bf16[32,2048]{1,0:T(8,128)(2,1)}, u32[]{:S(2)}) copy-start(bf16[32,2048]{1,0:T(8,128)(2,1)} %param.10) | copy-start | bytes 393220
  0.7 15.3 %copy-start.2 = (f32[8192]{0:T(1024)S(1)}, f32[8192]{0:T(1024)}, u32[]{:S(2)}) copy-start(f32[8192]{0:T(1024)} %param.11) | copy-start | bytes 98308
  18.2 15.5 %all-to-all-start = ((bf16[8,2,4,2176]{3,2,1,0:T(4,128)(2,1)}), bf16[8,2,4,2176]{3,2,1,0:T(4,128)(2,1)S(1)}, u32[]{:S(2)}, u32[]{:S(2)}) async-start(bf16[8,2,4,2176]{3,2,1,0:T(4,128)(2,1)} %pad_maximum_fusion), calls=%async_computation | async-start | bytes 557056 | tf_op jit(solution)/shard_map/all_to_all | solution.py:211
  33.9 14.8 %copy-start.3 = (s32[32]{0:T(128)S(1)}, s32[32]{0:T(128)}, u32[]{:S(2)}) copy-start(s32[32]{0:T(128)} %len_ref.1) | copy-start | bytes 388
  38.9 1.3 %collective-permute-start = (f32[8,2,4,128]{3,0,2,1:T(8,128)S(1)}, f32[8,2,4,128]{3,0,2,1:T(8,128)S(1)}, u32[]{:S(2)}, u32[]{:S(2)}) collective-permute-start(f32[8,2,4,128]{3,0,2,1:T(8,128)S(1)} %fusion.7), channel_id=1, source_target_pairs={{0,1},{1,0},{2,3},{3,2},{4,5},{5,4},{6,7},{7,6},{8,9},{9,8},{10,11... | collective-permute-start | bytes 98312 | tf_op jit(solution)/shard_map/ppermute | solution.py:142
  40.2 3.9 %collective-permute-start.1 = (f32[8,2,4,128]{3,0,2,1:T(8,128)S(1)}, f32[8,2,4,128]{3,0,2,1:T(8,128)S(1)}, u32[]{:S(2)}, u32[]{:S(2)}) collective-permute-start(f32[8,2,4,128]{3,0,2,1:T(8,128)S(1)} %add.145), channel_id=1, source_target_pairs={{0,2},{1,3},{2,0},{3,1},{4,6},{5,7},{6,4},{7,5},{8,10},{9,11},{10,... | collective-permute-start | bytes 98312 | tf_op jit(solution)/shard_map/ppermute | solution.py:142
  45.1 15.0 %all-to-all-start.1 = ((f32[8,2,4,2,256]{4,2,3,1,0:T(4,128)}), f32[8,2,4,2,256]{4,2,3,1,0:T(4,128)S(1)}, u32[]{:S(2)}, u32[]{:S(2)}) async-start(f32[8,2,4,2,256]{4,2,3,1,0:T(4,128)} %fusion.10), calls=%async_computation.1 | async-start | bytes 262144 | tf_op jit(solution)/shard_map/all_to_all | solution.py:228

commit v19 on v17

--- a/solution.py
+++ b/solution.py
@@ -116,7 +116,7 @@
             out_specs=score_spec,
         ),
     )(cached_length, query_heads, key_value_cache)
-    mix_rows = 8 if row_count % 8 == 0 else row_count
+    mix_rows = 16 if row_count % 16 == 0 else row_count
     out = pl.pallas_call(
         functools.partial(mix_kernel, rows=mix_rows, kv_local=kv_local, group_size=group_size),
         out_shape=jax.ShapeDtypeStruct((row_count, heads * HEAD), jnp.bfloat16),

time: 73.4 us -> 73.6 us (level)
  no operation moved by 1% of the time
where the time goes in v19:
time: 73.6 us; the launch traced here: 73.1 us
  Pallas kernels  22.4 us (30%)
  matrix products  10.8 us (15%)
  starting transfers between devices  10.6 us (14%)
  blocking collectives  8.65 us (12%)
  local copies, waits for them, and re-layouts  7.63 us (10%)
  waiting for transfers between devices  6.46 us (9%)
  other arithmetic  5.69 us (8%)
  between operations  0.9 us (1%)
    pallas_call x1, Pallas kernels, attend(): pl.pallas_call(functools.partial(mix_kernel, rows=mix_rows, kv_local=kv_l...  11.3 us
    pallas_call x1, Pallas kernels, attend(): pl.pallas_call(functools.partial(score_kernel, **opts), out_shape=jax.Sha...  11 us
    all_gather x1, blocking collectives, body(): gathered = lax.all_gather(hidden, 'tensor', axis=1, tiled=True)  8.65 us
    all_to_all x1, starting transfers between devices, body(): lax.all_to_all(payload, 'replica', split_axis=0, concat_axis=0, tiled=True)  5.81 us
    dot_general x1, matrix products, body(): jnp.einsum('oksd,adr->oksar', got_rows, adapter_down, preferred_element_t...  4.96 us
    dot_general x1, matrix products, body(): jnp.einsum('jd,dcw->jcw', normed, key_value_weight, preferred_element_typ...  4.93 us
    all_to_all x1, starting transfers between devices, body(): lax.all_to_all(owner_delta, 'replica', split_axis=0, concat_axis=0, tiled...  3.64 us
    all_to_all x1, waiting for transfers between devices, body(): lax.all_to_all(payload, 'replica', split_axis=0, concat_axis=0, tiled=True)  3.26 us
  transfers between devices with their start and end apart: 4, of which 3 were waited for; matrix products, arithmetic and copies ran while one was open for 10% of the time, Pallas kernels for 15%

profile of v19, /device:TPU:0, one launch (start us, length us, event | category | flops | bytes accessed | tf_op | source)
XLA Modules:
  0.0 73.1 jit_solution(2150104361220029128)
XLA Ops:
  0.7 0.8 %fusion.22 = s32[16]{0:T(128)S(1)} fusion(s32[1,16]{1,0:T(1,128)} %param.17), kind=kLoop, calls=%fused_computation.78 | loop fusion | flops 240 | bytes 128 | tf_op jit(solution)/shard_map/eq | solution.py:189
  1.4 0.7 and_select_fusion.2
  2.9 1.3 %gather_fusion = s32[16]{0:T(128)S(1)} fusion(s32[16]{0:T(128)} %bitcast.75, s32[1024]{0:T(1024)S(1)} %pad_clamp_fusion.4), kind=kCustom, calls=%fused_computation | custom fusion | bytes 192 | tf_op jit(solution)/shard_map/gather | solution.py:201
  4.5 0.7 %copy.59 = s32[16,1]{1,0:T(8,128)S(1)} copy(s32[16,1]{0,1:T(1,128)} %bitcast.76) | data formatting | bytes 128 | tf_op jit(solution)/shard_map/reshape.320
  5.4 0.7 bitcast_subtract_fusion.1
  6.1 0.7 gather_fusion.1
  7.1 8.6 %all_gather.3 = bf16[32,8192]{1,0:T(8,128)(2,1)S(1)} all-gather(bf16[32,2048]{1,0:T(8,128)(2,1)S(1)} %copy-done.1), channel_id=1, replica_groups=mesh['replica'=8,'tensor'=4] {'tensor'}, dimensions={1}, use_global_device_ids=true | all-gather | bytes 655360 | tf_op jit(solution)/shard_map/all_gather | solution.py:167
  16.2 0.7 %gather_fusion.2 = bf16[64,2048]{1,0:T(8,128)(2,1)S(1)} fusion(bf16[32,2048]{1,0:T(8,128)(2,1)S(1)} %constant_dynamic-slice_fusion, s32[1024]{0:T(1024)S(1)} %pad_clamp_fusion.3), kind=kCustom, calls=%fused_computation.2 | custom fusion | bytes 524544 | tf_op jit(solution)/shard_map/gather | solution.py:205
  17.3 0.8 %pad_maximum_fusion = bf16[8,2,4,2176]{3,2,1,0:T(4,128)(2,1)} fusion(bf16[8,2,4,128]{3,2,1,0:T(4,128)(2,1)S(1)} %broadcast_in_dim.54, bf16[8,2,4,2048]{3,2,1,0:T(4,128)(2,1)S(1)} %broadcast_select_fusion), kind=kLoop, calls=%fused_computation.21 | loop fusion | flops 557056 | bytes 557056 | tf_op jit(solution)/shard_map/concatenate | solution.py:210
  18.2 5.8 %all-to-all-start = ((bf16[8,2,4,2176]{3,2,1,0:T(4,128)(2,1)}), bf16[8,2,4,2176]{3,2,1,0:T(4,128)(2,1)S(1)}, u32[]{:S(2)}, u32[]{:S(2)}) async-start(bf16[8,2,4,2176]{3,2,1,0:T(4,128)(2,1)} %pad_maximum_fusion), calls=%async_computation | async-start | bytes 557056 | tf_op jit(solution)/shard_map/all_to_all | solution.py:211
  24.1 0.7 gather_fusion.5
  24.8 0.7 gather_fusion.4
  25.5 4.9 %fusion.2 = f32[32,2,256]{2,0,1:T(8,128)S(1)} fusion(bf16[8192,2,256]{2,1,0:T(2,128)(2,1)} %param.12, bf16[32,8192]{1,0:T(8,128)(2,1)S(1)} %fusion.13), kind=kOutput, calls=%fused_computation.9 | convolution fusion | flops 268435456 | bytes 8978432 | tf_op jit(solution)/shard_map/jd,dcw->jcw/dot_general | solution.py:231
  30.4 3.3 %all-to-all-done = bf16[8,2,4,2176]{3,2,1,0:T(4,128)(2,1)S(1)} async-done(((bf16[8,2,4,2176]{3,2,1,0:T(4,128)(2,1)}), bf16[8,2,4,2176]{3,2,1,0:T(4,128)(2,1)S(1)}, u32[]{:S(2)}, u32[]{:S(2)}) %all-to-all-start) | async-done | bytes 278560 | tf_op jit(solution)/shard_map/all_to_all | solution.py:211
  34.0 5.0 %fusion.7 = f32[8,2,4,128]{3,0,2,1:T(8,128)S(1)} fusion(bf16[16,2048,128]{2,1,0:T(8,128)(2,1)} %param.13, bf16[8,2,4,2048]{3,2,1,0:T(4,128)(2,1)S(1)} %slice.40, pred[8,2,16]{0,2,1:T(8,128)(4,1)S(1)} %iota_compare_fusion), kind=kOutput, calls=%fused_computation.14 | convolution fusion | flops 537124864 | bytes 8683776 | tf_op jit(solution)/shard_map/oksd,adr->oksar/dot_general | solution.py:215
  39.2 1.0 %collective-permute-done = f32[8,2,4,128]{3,0,2,1:T(8,128)S(1)} collective-permute-done((f32[8,2,4,128]{3,0,2,1:T(8,128)S(1)}, f32[8,2,4,128]{3,0,2,1:T(8,128)S(1)}, u32[]{:S(2)}, u32[]{:S(2)}) %collective-permute-start) | collective-permute-done | bytes 32800 | tf_op jit(solution)/shard_map/ppermute | solution.py:142
  40.2 1.1 %collective-permute-start.1 = (f32[8,2,4,128]{3,0,2,1:T(8,128)S(1)}, f32[8,2,4,128]{3,0,2,1:T(8,128)S(1)}, u32[]{:S(2)}, u32[]{:S(2)}) collective-permute-start(f32[8,2,4,128]{3,0,2,1:T(8,128)S(1)} %add.145), channel_id=1, source_target_pairs={{0,2},{1,3},{2,0},{3,1},{4,6},{5,7},{6,4},{7,5},{8,10},{9,11},{10,... | collective-permute-start | bytes 98312 | tf_op jit(solution)/shard_map/ppermute | solution.py:142
  41.9 2.2 %collective-permute-done.1 = f32[8,2,4,128]{3,0,2,1:T(8,128)S(1)} collective-permute-done((f32[8,2,4,128]{3,0,2,1:T(8,128)S(1)}, f32[8,2,4,128]{3,0,2,1:T(8,128)S(1)}, u32[]{:S(2)}, u32[]{:S(2)}) %collective-permute-start.1) | collective-permute-done | bytes 32800 | tf_op jit(solution)/shard_map/ppermute | solution.py:142
  44.2 0.9 %fusion.10 = f32[8,2,4,2,256]{4,2,3,1,0:T(4,128)} fusion(bf16[8,2,2,64,256]{4,3,2,1,0:T(8,128)(2,1)S(1)} %bitcast.77, bf16[8,2,4,2,64]{4,3,0,2,1:T(2,128)(2,1)S(1)} %reshape.342), kind=kOutput, calls=%fused_computation.16 | convolution fusion | flops 4227072 | bytes 1196032 | tf_op jit(solution)/shard_map/okscr,okcrw->okscw/dot_general | solution.py:225
  45.1 3.6 %all-to-all-start.1 = ((f32[8,2,4,2,256]{4,2,3,1,0:T(4,128)}), f32[8,2,4,2,256]{4,2,3,1,0:T(4,128)S(1)}, u32[]{:S(2)}, u32[]{:S(2)}) async-start(f32[8,2,4,2,256]{4,2,3,1,0:T(4,128)} %fusion.10), calls=%async_computation.1 | async-start | bytes 262144 | tf_op jit(solution)/shard_map/all_to_all | solution.py:228
  48.8 11.0 %shard_map.113.s_ref = f32[32,16,1024]{2,1,0:T(8,128)} custom-call(s32[32]{0:T(128)} %len_ref.1, bf16[32,2048]{1,0:T(8,128)(2,1)} %q_ref.3, bf16[32,512,2,256]{3,2,1,0:T(2,128)(2,1)} %kv_ref.3), custom_call_target="tpu_custom_call" | custom-call | tf_op jit(solution)/shard_map/pallas_call | solution.py:109
  60.1 0.6 gather_fusion.6
  61.1 0.7 pad_maximum_fusion.1.nkv_ref
  61.8 11.3 %shard_map.114 = bf16[32,2048]{1,0:T(8,128)(2,1)} custom-call(bf16[32,2048]{1,0:T(8,128)(2,1)} %q_ref.3, f32[32,16,1024]{2,1,0:T(8,128)} %shard_map.113.s_ref, bf16[32,512,2,256]{3,2,1,0:T(2,128)(2,1)} %kv_ref.3, bf16[32,2,256]{2,1,0:T(2,128)(2,1)} %pad_maximum_fusion.1.nkv_ref), custom_call_target="tpu_custom_call" | custom-call | tf_op jit(solution)/shard_map/pallas_call | solution.py:120
  (68 shorter events, 4.3 us)
Async XLA Ops:
  0.6 40.7 %copy-start = (bf16[16,2,64,256]{3,2,1,0:T(8,128)(2,1)S(1)}, bf16[16,2,64,256]{3,2,1,0:T(8,128)(2,1)}, u32[]{:S(2)}) copy-start(bf16[16,2,64,256]{3,2,1,0:T(8,128)(2,1)} %param.14) | copy-start | bytes 3145732
  0.6 6.4 %copy-start.1 = (bf16[32,2048]{1,0:T(8,128)(2,1)S(1)}, bf16[32,2048]{1,0:T(8,128)(2,1)}, u32[]{:S(2)}) copy-start(bf16[32,2048]{1,0:T(8,128)(2,1)} %param.10) | copy-start | bytes 393220
  0.7 15.3 %copy-start.2 = (f32[8192]{0:T(1024)S(1)}, f32[8192]{0:T(1024)}, u32[]{:S(2)}) copy-start(f32[8192]{0:T(1024)} %param.11) | copy-start | bytes 98308
  18.2 15.5 %all-to-all-start = ((bf16[8,2,4,2176]{3,2,1,0:T(4,128)(2,1)}), bf16[8,2,4,2176]{3,2,1,0:T(4,128)(2,1)S(1)}, u32[]{:S(2)}, u32[]{:S(2)}) async-start(bf16[8,2,4,2176]{3,2,1,0:T(4,128)(2,1)} %pad_maximum_fusion), calls=%async_computation | async-start | bytes 557056 | tf_op jit(solution)/shard_map/all_to_all | solution.py:211
  33.9 14.8 %copy-start.3 = (s32[32]{0:T(128)S(1)}, s32[32]{0:T(128)}, u32[]{:S(2)}) copy-start(s32[32]{0:T(128)} %len_ref.1) | copy-start | bytes 388
  38.9 1.3 %collective-permute-start = (f32[8,2,4,128]{3,0,2,1:T(8,128)S(1)}, f32[8,2,4,128]{3,0,2,1:T(8,128)S(1)}, u32[]{:S(2)}, u32[]{:S(2)}) collective-permute-start(f32[8,2,4,128]{3,0,2,1:T(8,128)S(1)} %fusion.7), channel_id=1, source_target_pairs={{0,1},{1,0},{2,3},{3,2},{4,5},{5,4},{6,7},{7,6},{8,9},{9,8},{10,11... | collective-permute-start | bytes 98312 | tf_op jit(solution)/shard_map/ppermute | solution.py:142
  40.2 3.9 %collective-permute-start.1 = (f32[8,2,4,128]{3,0,2,1:T(8,128)S(1)}, f32[8,2,4,128]{3,0,2,1:T(8,128)S(1)}, u32[]{:S(2)}, u32[]{:S(2)}) collective-permute-start(f32[8,2,4,128]{3,0,2,1:T(8,128)S(1)} %add.145), channel_id=1, source_target_pairs={{0,2},{1,3},{2,0},{3,1},{4,6},{5,7},{6,4},{7,5},{8,10},{9,11},{10,... | collective-permute-start | bytes 98312 | tf_op jit(solution)/shard_map/ppermute | solution.py:142
  45.1 14.9 %all-to-all-start.1 = ((f32[8,2,4,2,256]{4,2,3,1,0:T(4,128)}), f32[8,2,4,2,256]{4,2,3,1,0:T(4,128)S(1)}, u32[]{:S(2)}, u32[]{:S(2)}) async-start(f32[8,2,4,2,256]{4,2,3,1,0:T(4,128)} %fusion.10), calls=%async_computation.1 | async-start | bytes 262144 | tf_op jit(solution)/shard_map/all_to_all | solution.py:228
